TPU v7x, 256 devices: a whole 4x4x8 slice. The times are simulated.
256 devices in a mesh: outer: 4 (over x_lo, core), inner: 64 (over y, z, x_hi).
Axes of the slice: x: 4 (x_hi: 2, x_lo: 2; x = x_hi * 2 + x_lo), y: 4, z: 8, core: 2. Of those that a mesh axis runs over, the one named last changes fastest.
Arguments:
- queue: bfloat16 [1048576, 512], P(('outer', 'inner')), may hold values from -100 to 100
- pred: bfloat16 [32768, 512], P(('outer', 'inner')), may hold values from -1 to 1
- owner: int32 [32768, 1], P(('outer', 'inner')), may hold values from 0 to 255, as said below
- slot: int32 [32768], P(('outer', 'inner')), may hold values from 0 to 4095
Outputs:
- grad_pred: float32 [32768, 512], P(('outer', 'inner'))
Inputs may be any that keep to these rules, and one draw needn't show every extreme that they name: Queue shard o lies on the device of outer index o // 64 and inner index o % 64. Among the rows of one device (aligned blocks of 128 rows), at most 4 name owners of one inner index; among the rows of one outer group (aligned blocks of 8192 rows), at most 64 name the same owner.
All inputs are finite; a program needn't handle non-finite values.
Results may differ from a plain program's by a relative error of at most 0.012.
Values may be sent and summed in bfloat16 or wider, within the bound.
No kernel may reach another device: no remote copies, remote signals or barrier semaphores. Data moves between devices by JAX's collectives and lax.ppermute only.
A program may use at most 128 MiB of HBM per device.

v0:
```python
import jax
import jax.numpy as jnp
from jax import lax
from jax.sharding import PartitionSpec as P

EPS = 1e-06
INV_TAU = 10.0


def block_exp(row_block, column_block):
    return jnp.exp(
        jnp.einsum("rd,cd->rc", row_block, column_block, preferred_element_type=jnp.float32)
        * INV_TAU
    )


def mixed_weights(exponent, row_total, column_total, row_first, column_first, rows_dev):
    row_offset = jnp.arange(exponent.shape[0], dtype=jnp.int32)[:, None] - row_first
    column_offset = jnp.arange(exponent.shape[1], dtype=jnp.int32)[None, :] - column_first
    diagonal = ((row_offset == column_offset) & (row_offset >= 0) & (row_offset < rows_dev)).astype(
        jnp.float32
    )
    return (
        0.5 * (exponent / row_total[:, None] + exponent / column_total[None, :]) - diagonal
    ).astype(jnp.bfloat16)


def column_terms(weights, row_block):
    return lax.dot_general(
        weights, row_block, (((0,), (0,)), ((), ())), preferred_element_type=jnp.float32
    )


def shards(queue, pred, owner, slot):
    outer_count = lax.axis_size("outer")
    inner_count = lax.axis_size("inner")
    rows_dev = pred.shape[0]
    feature_width = queue.shape[1]
    cap_member = max(2, 2 * rows_dev // inner_count)
    cap_group = inner_count * cap_member // outer_count
    owners_of = owner[:, 0]
    owner_member = owners_of % inner_count
    owner_group = owners_of // inner_count
    position = jnp.arange(rows_dev, dtype=jnp.int32)
    earlier = (owner_member[:, None] == owner_member[None, :]) & (
        position[None, :] < position[:, None]
    )
    member_place = owner_member * cap_member + jnp.sum(earlier.astype(jnp.int32), 1)
    request_slot = jnp.full((inner_count * cap_member,), -1, jnp.int32).at[member_place].set(slot)
    request_group = (
        jnp.full((inner_count * cap_member,), outer_count, jnp.int32)
        .at[member_place]
        .set(owner_group)
    )
    request_slot = request_slot.reshape(inner_count, cap_member)
    request_group = request_group.reshape(inner_count, cap_member)
    relay_slot, relay_group = (
        lax.all_to_all(request_slot, "inner", split_axis=0, concat_axis=0, tiled=True),
        lax.all_to_all(request_group, "inner", split_axis=0, concat_axis=0, tiled=True),
    )
    relay_slot = relay_slot.reshape(-1)
    relay_group = relay_group.reshape(-1)
    entry_index = jnp.arange(relay_slot.shape[0], dtype=jnp.int32)
    ahead = (relay_group[:, None] == relay_group[None, :]) & (
        entry_index[None, :] < entry_index[:, None]
    )
    group_place = relay_group * cap_group + jnp.sum(ahead.astype(jnp.int32), 1)
    asking = (
        jnp.full((outer_count * cap_group,), -1, jnp.int32)
        .at[group_place]
        .set(relay_slot, mode="drop")
    )
    asking = asking.reshape(outer_count, cap_group)
    asked = lax.all_to_all(asking, "outer", split_axis=0, concat_axis=0, tiled=True)
    looked = jnp.take(queue, jnp.maximum(asked, 0), axis=0)
    looked = jnp.where((asked >= 0)[..., None], looked, jnp.zeros((), jnp.bfloat16))
    answered = lax.all_to_all(looked, "outer", split_axis=0, concat_axis=0, tiled=True)
    answered = answered.reshape(outer_count * cap_group, feature_width)
    relayed = jnp.take(answered, jnp.minimum(group_place, outer_count * cap_group - 1), axis=0)
    relayed = jnp.where((relay_slot >= 0)[:, None], relayed, jnp.zeros((), jnp.bfloat16))
    relayed = relayed.reshape(inner_count, cap_member, feature_width)
    returned = lax.all_to_all(relayed, "inner", split_axis=0, concat_axis=0, tiled=True)
    fetched = jnp.take(
        returned.reshape(inner_count * cap_member, feature_width), member_place, axis=0
    ).astype(jnp.float32)
    neighbour = (fetched * lax.rsqrt(jnp.sum(fetched * fetched, 1, keepdims=True) + EPS)).astype(
        jnp.bfloat16
    )
    predicted = pred.astype(jnp.float32)
    inverse = lax.rsqrt(jnp.sum(predicted * predicted, 1, keepdims=True) + EPS)
    queries = (predicted * inverse).astype(jnp.bfloat16)
    outer_at = lax.axis_index("outer")
    inner_at = lax.axis_index("inner")
    row_block = lax.all_gather(neighbour, "inner", axis=0, tiled=True)
    exponent = block_exp(row_block, lax.all_gather(queries, "outer", axis=0, tiled=True))
    row_total = lax.psum(jnp.sum(exponent, 1), "inner")
    column_total = lax.psum(jnp.sum(exponent, 0), "outer")
    weights = mixed_weights(
        exponent, row_total, column_total, inner_at * rows_dev, outer_at * rows_dev, rows_dev
    )
    dquery = lax.psum_scatter(
        column_terms(weights, row_block), "outer", scatter_dimension=0, tiled=True
    )
    dquery = dquery * INV_TAU
    radial = jnp.sum(predicted * dquery, 1, keepdims=True)
    return inverse * dquery - predicted * inverse * inverse * inverse * radial


def solution(mesh):
    in_specs = (
        P(("outer", "inner"), None),
        P(("outer", "inner"), None),
        P(("outer", "inner"), None),
        P(("outer", "inner")),
    )
    out_specs = P(("outer", "inner"), None)
    return jax.shard_map(shards, mesh=mesh, in_specs=in_specs, out_specs=out_specs, check_vma=False)
```

profile of v0, /device:TPU:8, one launch (start us, length us, event | category | flops | bytes accessed | tf_op | source)
XLA Modules:
  0.0 657.6 jit_solution(4606644193703662262)
XLA Ops:
  6.5 0.7 fusion.29
  7.2 0.7 and_select_fusion
  7.9 0.2 convert_reduce_fusion.1
  8.0 0.7 and_bitcast_fusion
  8.7 1.1 scatter_custom_fusion
  9.8 0.7 all_to_all.24
  10.5 14.6 %all-to-all-start = ((s32[64,1,4]{2,1,0:T(1,128)}), s32[64,1,4]{2,1,0:T(1,128)S(1)}, u32[]{:S(2)}, u32[]{:S(2)}) async-start(s32[64,1,4]{2,1,0:T(1,128)} %bitcast.5), calls=%async_computation | async-start | bytes 65536 | tf_op jit(solution)/shard_map/all_to_all | solution.py:58
  25.1 1.0 scatter_custom_fusion.1
  26.1 0.7 all_to_all.26
  26.8 9.3 %all-to-all-done = s32[64,1,4]{2,1,0:T(1,128)S(1)} async-done(((s32[64,1,4]{2,1,0:T(1,128)}), s32[64,1,4]{2,1,0:T(1,128)S(1)}, u32[]{:S(2)}, u32[]{:S(2)}) %all-to-all-start) | async-done | bytes 1056 | tf_op jit(solution)/shard_map/all_to_all | solution.py:58
  36.1 5.5 all-to-all-start.1
  41.6 0.6 broadcast.284
  42.2 0.8 reduce.11
  43.0 0.1 reshape.245
  43.1 9.5 %all-to-all-done.1 = s32[64,1,4]{2,1,0:T(1,128)S(1)} async-done(((s32[64,1,4]{2,1,0:T(1,128)}), s32[64,1,4]{2,1,0:T(1,128)S(1)}, u32[]{:S(2)}, u32[]{:S(2)}) %all-to-all-start.1) | async-done | bytes 1056 | tf_op jit(solution)/shard_map/all_to_all | solution.py:59
  52.5 0.8 reduce.10
  53.3 0.1 reshape.197
  53.4 0.2 convert_reduce_fusion
  53.8 0.1 mul.124
  53.9 0.1 reduce_sum.72
  54.0 1.4 scatter_custom_fusion.2
  55.4 0.7 all_to_all.28
  56.1 3.2 all-to-all-start.2
  59.5 3.5 all-to-all-done.2
  63.1 3.9 gather_fusion
  67.1 0.8 select_select_fusion.1
  67.9 3.4 all-to-all-start.3
  71.3 0.1 copy.20
  71.4 0.1 copy.24
  71.6 5.7 all-to-all-done.3
  77.3 1.2 gather_fusion.1
  78.5 1.0 select_select_fusion
  79.5 5.5 all-to-all-start.4
  85.1 12.9 %all-to-all-done.4 = bf16[64,4,512]{2,1,0:T(4,128)(2,1)S(1)} async-done(((bf16[64,4,512]{2,1,0:T(4,128)(2,1)}), bf16[64,4,512]{2,1,0:T(4,128)(2,1)S(1)}, u32[]{:S(2)}, u32[]{:S(2)}) %all-to-all-start.4) | async-done | bytes 262176 | tf_op jit(solution)/shard_map/all_to_all | solution.py:82
  98.1 0.8 gather_fusion.2
  99.0 0.2 fusion.8
  99.1 0.8 fusion.9
  100.1 1.0 fusion.10
  101.1 1.0 fusion.4
  102.1 6.7 %all_gather.7 = bf16[512,512]{1,0:T(8,128)(2,1)S(1)} all-gather(bf16[128,512]{1,0:T(8,128)(2,1)S(1)} %fusion.4), channel_id=1, replica_groups=mesh['outer'=4,'inner'=64] {'outer'}, dimensions={0}, use_global_device_ids=true | all-gather | bytes 655360 | tf_op jit(solution)/shard_map/all_gather | solution.py:95
  108.8 136.2 %all-gather.2.cloned.1.call-done = bf16[8192,512]{1,0:T(8,128)(2,1)} async-done(((bf16[128,512]{1,0:T(8,128)(2,1)}), bf16[8192,512]{1,0:T(8,128)(2,1)}) %all-gather.2.cloned.1.call-update) | async-done | bytes 8388624 | tf_op jit(solution)/shard_map/all_gather | solution.py:94
  245.0 11.7 %fusion.1 = (f32[8192]{0:T(1024)S(1)}, f32[512]{0:T(512)S(1)}, f32[8192,512]{1,0:T(8,128)}) fusion(bf16[8192,512]{1,0:T(8,128)(2,1)} %all-gather.2.cloned.1.call-done, bf16[512,512]{1,0:T(8,128)(2,1)S(1)} %all_gather.7), kind=kOutput, calls=%fused_computation.9 | convolution fusion | flops 4307541504 | bytes 25724928 | tf_op jit(solution)/shard_map/rd,cd->rc/dot_general | solution.py:12
  256.7 326.1 %psum.14 = f32[8192]{0:T(1024)S(1)} all-reduce(f32[8192]{0:T(1024)S(1)} %get-tuple-element.5), channel_id=1, replica_groups=mesh['outer'=4,'inner'=64] {'inner'}, use_global_device_ids=true, to_apply=%region_8.9 | all-reduce | flops 8192 | bytes 65536 | tf_op jit(solution)/shard_map/psum | solution.py:96
  582.8 5.6 psum.15
  588.4 15.2 %fusion.2 = f32[512,512]{1,0:T(8,128)} fusion(bf16[8192,512]{1,0:T(8,128)(2,1)} %all-gather.2.cloned.1.call-done, f32[8192,512]{1,0:T(8,128)} %get-tuple-element.17, s32[512]{0:T(512)S(1)} %iota_subtract_fusion.1, f32[512]{0:T(512)S(1)} %psum.15, f32[8192]{0:T(1024)S(1)} %psum.14, s32[8192]{0:T(1024)S(1)} %iota_subtract_fusion, ...), kind=kOutput, calls=%fused_computation.10 | convolution fusion | flops 4341104640 | bytes 26300416 | tf_op jit(solution)/shard_map/dot_general | solution.py:29
  603.7 44.3 %reduce-scatter.2.cloned.1.call-done = f32[128,512]{1,0:T(8,128)} async-done(((f32[512,512]{1,0:T(8,128)}), f32[128,512]{1,0:T(8,128)}) %reduce-scatter.2.cloned.1.call-update) | async-done | bytes 262160 | tf_op jit(solution)/shard_map/reduce_scatter | solution.py:101
  647.9 1.1 fusion.11
  649.0 1.8 fusion.7
  (28 shorter events, 0.8 us)
Async XLA Ops:
  10.5 25.6 %all-to-all-start = ((s32[64,1,4]{2,1,0:T(1,128)}), s32[64,1,4]{2,1,0:T(1,128)S(1)}, u32[]{:S(2)}, u32[]{:S(2)}) async-start(s32[64,1,4]{2,1,0:T(1,128)} %bitcast.5), calls=%async_computation | async-start | bytes 65536 | tf_op jit(solution)/shard_map/all_to_all | solution.py:58
  36.1 16.4 %all-to-all-start.1 = ((s32[64,1,4]{2,1,0:T(1,128)}), s32[64,1,4]{2,1,0:T(1,128)S(1)}, u32[]{:S(2)}, u32[]{:S(2)}) async-start(s32[64,1,4]{2,1,0:T(1,128)} %bitcast.7), calls=%async_computation.1 | async-start | bytes 65536 | tf_op jit(solution)/shard_map/all_to_all | solution.py:59
  56.1 6.9 %all-to-all-start.2 = ((s32[4,1,64]{2,1,0:T(1,128)}), s32[4,1,64]{2,1,0:T(1,128)S(1)}, u32[]{:S(2)}, u32[]{:S(2)}) async-start(s32[4,1,64]{2,1,0:T(1,128)} %all_to_all.28), calls=%async_computation.2 | async-start | bytes 4096 | tf_op jit(solution)/shard_map/all_to_all | solution.py:74
  67.9 9.4 %all-to-all-start.3 = ((bf16[4,64,512]{2,1,0:T(8,128)(2,1)}), bf16[4,64,512]{2,1,0:T(8,128)(2,1)S(1)}, u32[]{:S(2)}, u32[]{:S(2)}) async-start(bf16[4,64,512]{2,1,0:T(8,128)(2,1)} %select_select_fusion.1), calls=%async_computation.3 | async-start | bytes 524288 | tf_op jit(solution)/shard_map/all_to_all | solution.py:77
  79.5 18.5 %all-to-all-start.4 = ((bf16[64,4,512]{2,1,0:T(4,128)(2,1)}), bf16[64,4,512]{2,1,0:T(4,128)(2,1)S(1)}, u32[]{:S(2)}, u32[]{:S(2)}) async-start(bf16[64,4,512]{2,1,0:T(4,128)(2,1)} %select_select_fusion), calls=%async_computation.4 | async-start | bytes 524288 | tf_op jit(solution)/shard_map/all_to_all | solution.py:82
  85.0 160.0 %all-gather.2.cloned.1.call-start = ((), (), s32[]{:S(2)}) async-start(), calls=%async_computation.6 | async-start | bytes 8519680 | tf_op jit(solution)/shard_map/all_gather | solution.py:94
  99.9 548.0 %reduce-scatter.2.cloned.1.call-start = ((), (), s32[]{:S(2)}) async-start(), calls=%async_computation.7 | async-start | bytes 1310720 | tf_op jit(solution)/shard_map/reduce_scatter | solution.py:101
  588.4 59.5 %copy-start = (bf16[128,512]{1,0:T(8,128)(2,1)S(1)}, bf16[128,512]{1,0:T(8,128)(2,1)}, u32[]{:S(2)}) copy-start(bf16[128,512]{1,0:T(8,128)(2,1)} %param.5) | copy-start | bytes 393220
Sparse Core Ops, SparseCore 0:
  100.1 144.8 all-gather.1
  603.8 44.1 reduce-scatter.1
where the time goes:
time: 660 us; the launch traced here: 658 us
  blocking collectives  338 us (51%)
  waiting for transfers between devices  221 us (33%)
  starting transfers between devices  32.3 us (5%)
  matrix products  26.9 us (4%)
  between operations  13.6 us (2%)
  local copies, waits for them, and re-layouts  13.3 us (2%)
  other arithmetic  11.7 us (2%)
    psum x1, blocking collectives, shards(): row_total = lax.psum(jnp.sum(exponent, 1), 'inner')  326 us
    all_gather x1, waiting for transfers between devices, shards(): row_block = lax.all_gather(neighbour, 'inner', axis=0, tiled=True)  136 us
    reduce_scatter x1, waiting for transfers between devices, shards(): lax.psum_scatter(column_terms(weights, row_block), 'outer', scatter_dimen...  44.3 us
    dot_general x1, matrix products, column_terms(): lax.dot_general(weights, row_block, (((0,), (0,)), ((), ())), preferred_e...  15.2 us
    all_to_all x1, starting transfers between devices, shards(): lax.all_to_all(request_slot, 'inner', split_axis=0, concat_axis=0, tiled=...  14.6 us
  transfers between devices with their start and end apart: 7, of which 7 were waited for; matrix products, arithmetic and copies ran while one was open for 1% of the time, Pallas kernels for 0%

commit v1 on v0

v1 whole, which is shorter than its diff:
```python
import jax
import jax.numpy as jnp
import numpy as np
from jax import lax
from jax.sharding import Mesh
from jax.sharding import PartitionSpec as P

EPS = 1e-06
INV_TAU = 10.0

ALL = ("xl", "c", "y", "z", "xh")
INNER = ("y", "z", "xh")
OUTER = ("xl", "c")
ROWS = ("c", "y", "z")
COLS = ("xl", "xh")


def block_exp(row_block, column_block):
    return jnp.exp(
        jnp.einsum("rd,cd->rc", row_block, column_block, preferred_element_type=jnp.float32)
        * INV_TAU
    )


def mixed_weights(exponent, row_total, column_total, row_first, column_first, rows_dev):
    row_offset = jnp.arange(exponent.shape[0], dtype=jnp.int32)[:, None] - row_first
    column_offset = jnp.arange(exponent.shape[1], dtype=jnp.int32)[None, :] - column_first
    diagonal = ((row_offset == column_offset) & (row_offset >= 0) & (row_offset < rows_dev)).astype(
        jnp.float32
    )
    return (
        0.5 * (exponent / row_total[:, None] + exponent / column_total[None, :]) - diagonal
    ).astype(jnp.bfloat16)


def column_terms(weights, row_block):
    return lax.dot_general(
        weights, row_block, (((0,), (0,)), ((), ())), preferred_element_type=jnp.float32
    )


def tree_sum(value, axes):
    for axis in axes:
        size = lax.axis_size(axis)
        step = 1
        while step < size:
            pairs = [(i, i ^ step) for i in range(size)]
            value = value + lax.ppermute(value, axis, pairs)
            step *= 2
    return value


def fetch_rows(queue, owner, slot):
    outer_count = lax.axis_size(OUTER)
    inner_count = lax.axis_size(INNER)
    rows_dev = slot.shape[0]
    feature_width = queue.shape[1]
    cap_member = max(2, 2 * rows_dev // inner_count)
    cap_group = inner_count * cap_member // outer_count
    owners_of = owner[:, 0]
    owner_member = owners_of % inner_count
    owner_group = owners_of // inner_count
    position = jnp.arange(rows_dev, dtype=jnp.int32)
    earlier = (owner_member[:, None] == owner_member[None, :]) & (
        position[None, :] < position[:, None]
    )
    member_place = owner_member * cap_member + jnp.sum(earlier.astype(jnp.int32), 1)
    request = jnp.stack(
        [
            jnp.full((inner_count * cap_member,), -1, jnp.int32).at[member_place].set(slot),
            jnp.full((inner_count * cap_member,), outer_count, jnp.int32)
            .at[member_place]
            .set(owner_group),
        ],
        1,
    ).reshape(inner_count, cap_member, 2)
    relay = lax.all_to_all(request, INNER, split_axis=0, concat_axis=0, tiled=True)
    relay_slot = relay[:, :, 0].reshape(-1)
    relay_group = relay[:, :, 1].reshape(-1)
    entry_index = jnp.arange(relay_slot.shape[0], dtype=jnp.int32)
    ahead = (relay_group[:, None] == relay_group[None, :]) & (
        entry_index[None, :] < entry_index[:, None]
    )
    group_place = relay_group * cap_group + jnp.sum(ahead.astype(jnp.int32), 1)
    asking = (
        jnp.full((outer_count * cap_group,), -1, jnp.int32)
        .at[group_place]
        .set(relay_slot, mode="drop")
    )
    asking = asking.reshape(outer_count, cap_group)
    asked = lax.all_to_all(asking, OUTER, split_axis=0, concat_axis=0, tiled=True)
    looked = jnp.take(queue, jnp.maximum(asked, 0), axis=0)
    looked = jnp.where((asked >= 0)[..., None], looked, jnp.zeros((), jnp.bfloat16))
    answered = lax.all_to_all(looked, OUTER, split_axis=0, concat_axis=0, tiled=True)
    answered = answered.reshape(outer_count * cap_group, feature_width)
    relayed = jnp.take(answered, jnp.minimum(group_place, outer_count * cap_group - 1), axis=0)
    relayed = jnp.where((relay_slot >= 0)[:, None], relayed, jnp.zeros((), jnp.bfloat16))
    relayed = relayed.reshape(inner_count, cap_member, feature_width)
    returned = lax.all_to_all(relayed, INNER, split_axis=0, concat_axis=0, tiled=True)
    return jnp.take(
        returned.reshape(inner_count * cap_member, feature_width), member_place, axis=0
    ).astype(jnp.float32)


def shards(queue, pred, owner, slot):
    rows_dev = pred.shape[0]
    fetched = fetch_rows(queue, owner, slot)
    neighbour = (fetched * lax.rsqrt(jnp.sum(fetched * fetched, 1, keepdims=True) + EPS)).astype(
        jnp.bfloat16
    )
    predicted = pred.astype(jnp.float32)
    inverse = lax.rsqrt(jnp.sum(predicted * predicted, 1, keepdims=True) + EPS)
    queries = (predicted * inverse).astype(jnp.bfloat16)
    row_at = lax.axis_index(ROWS)
    column_at = lax.axis_index(COLS)
    row_block = lax.all_gather(neighbour, ROWS, axis=0, tiled=True)
    exponent = block_exp(row_block, lax.all_gather(queries, COLS, axis=0, tiled=True))
    row_total = tree_sum(jnp.sum(exponent, 1), ROWS)
    column_total = lax.psum(jnp.sum(exponent, 0), COLS)
    weights = mixed_weights(
        exponent, row_total, column_total, row_at * rows_dev, column_at * rows_dev, rows_dev
    )
    dquery = lax.psum_scatter(
        column_terms(weights, row_block), COLS, scatter_dimension=0, tiled=True
    )
    dquery = dquery * INV_TAU
    radial = jnp.sum(predicted * dquery, 1, keepdims=True)
    return inverse * dquery - predicted * inverse * inverse * inverse * radial


def solution(mesh):
    axes = dict(zip(mesh.axis_names, mesh.devices.shape))
    outer, inner = axes["outer"], axes["inner"]
    fine = Mesh(
        np.asarray(mesh.devices).reshape(2, outer // 2, inner // 16, 8, 2), ALL
    )
    spec = P(ALL, None)
    in_specs = (spec, spec, spec, P(ALL))
    return jax.shard_map(shards, mesh=fine, in_specs=in_specs, out_specs=spec, check_vma=False)
```

time: 660 us -> 260 us (0.39)
  blocking collectives: 338 us -> 51.6 us
  waiting for transfers between devices: 221 us -> 124 us
  starting transfers between devices: 32.3 us -> 21.2 us
    psum x2 -> x1, blocking collectives: 332 us -> 10.7 us  [shards(): column_total = lax.psum(jnp.sum(exponent, 0), COLS)]
    all_gather x1, waiting for transfers between devices: 136 us -> 59.2 us  [shards(): row_block = lax.all_gather(neighbour, ROWS, axis=0, tiled=True)]
    all_to_all x0 -> x1, blocking collectives: none -> 25.4 us  [fetch_rows(): lax.all_to_all(request, INNER, split_axis=0, concat_axis=0, tiled=True)]
    all_to_all x5 -> x3, starting transfers between devices: 32.2 us -> 12.1 us  [the longest x1 5.51 us: fetch_rows(): lax.all_to_all(relayed, INNER, split_axis=0, concat_axis=0, tiled=True)]
    all_to_all x5 -> x3, waiting for transfers between devices: 40.9 us -> 22.2 us  [the longest x1 12.9 us: fetch_rows(): lax.all_to_all(relayed, INNER, split_axis=0, concat_axis=0, tiled=True)]
    reduce_scatter x1, waiting for transfers between devices: 44.3 us -> 29.3 us  [shards(): lax.psum_scatter(column_terms(weights, row_block), COLS, scatter_dimensio...]
    ppermute x0 -> x6, waiting for transfers between devices: none -> 13.1 us  [tree_sum(): value = value + lax.ppermute(value, axis, pairs)]
    ppermute x0 -> x6, starting transfers between devices: none -> 8.96 us  [tree_sum(): value = value + lax.ppermute(value, axis, pairs)]
  transfers between devices with their start and end apart: 7 -> 11, of which waited for: 7 -> 10; matrix products, arithmetic and copies ran while one was open for 1% -> 1% of each run, Pallas kernels for 0% -> 0%
where the time goes in v1:
time: 260 us; the launch traced here: 259 us
  waiting for transfers between devices  124 us (48%)
  blocking collectives  51.6 us (20%)
  matrix products  26.7 us (10%)
  starting transfers between devices  21.2 us (8%)
  between operations  13.6 us (5%)
  local copies, waits for them, and re-layouts  11.7 us (4%)
  other arithmetic  10.2 us (4%)
    all_gather x1, waiting for transfers between devices, shards(): row_block = lax.all_gather(neighbour, ROWS, axis=0, tiled=True)  59.2 us
    reduce_scatter x1, waiting for transfers between devices, shards(): lax.psum_scatter(column_terms(weights, row_block), COLS, scatter_dimensio...  29.3 us
    all_to_all x1, blocking collectives, fetch_rows(): lax.all_to_all(request, INNER, split_axis=0, concat_axis=0, tiled=True)  25.4 us
    all_gather x1, blocking collectives, shards(): lax.all_gather(queries, COLS, axis=0, tiled=True)  15.5 us
    dot_general x1, matrix products, column_terms(): lax.dot_general(weights, row_block, (((0,), (0,)), ((), ())), preferred_e...  15 us
    ppermute x6, waiting for transfers between devices, tree_sum(): value = value + lax.ppermute(value, axis, pairs)  13.1 us
    all_to_all x1, waiting for transfers between devices, fetch_rows(): lax.all_to_all(relayed, INNER, split_axis=0, concat_axis=0, tiled=True)  12.9 us
    dot_general x1, matrix products, block_exp(): jnp.einsum('rd,cd->rc', row_block, column_block, preferred_element_type=j...  11.7 us
  transfers between devices with their start and end apart: 11, of which 10 were waited for; matrix products, arithmetic and copies ran while one was open for 1% of the time, Pallas kernels for 0%

profile of v1, /device:TPU:8, one launch (start us, length us, event | category | flops | bytes accessed | tf_op | source)
XLA Modules:
  0.0 258.8 jit_solution(308880161691059964)
XLA Ops:
  6.5 0.7 fusion.29
  7.2 0.7 and_select_fusion
  7.9 0.2 convert_reduce_fusion.1
  8.0 0.7 and_bitcast_fusion
  8.7 1.1 scatter_custom_fusion
  9.9 1.0 scatter_custom_fusion.1
  11.1 25.4 %all_to_all.24 = s32[64,4,2]{1,2,0:T(2,128)S(1)} all-to-all(s32[64,4,2]{1,2,0:T(2,128)S(1)} %copy.19), channel_id=1, replica_groups=mesh['xl'=2,'c'=2,'y'=4,'z'=8,'xh'=2] {'y','z','xh'}, dimensions={0} | all-to-all | bytes 4096 | tf_op jit(solution)/shard_map/all_to_all | solution.py:77
  36.5 0.2 slice_reduce_fusion.1
  36.9 0.2 convert_reduce_fusion
  37.3 0.1 mul.133
  37.5 1.4 scatter_custom_fusion.2
  38.9 0.7 all_to_all.16
  39.6 3.2 %all-to-all-start.1 = ((s32[4,1,64]{2,1,0:T(1,128)}), s32[4,1,64]{2,1,0:T(1,128)S(1)}, u32[]{:S(2)}, u32[]{:S(2)}) async-start(s32[4,1,64]{2,1,0:T(1,128)} %all_to_all.16), calls=%async_computation.1 | async-start | bytes 4096 | tf_op jit(solution)/shard_map/all_to_all | solution.py:91
  43.0 3.5 %all-to-all-done.1 = s32[4,1,64]{2,1,0:T(1,128)S(1)} async-done(((s32[4,1,64]{2,1,0:T(1,128)}), s32[4,1,64]{2,1,0:T(1,128)S(1)}, u32[]{:S(2)}, u32[]{:S(2)}) %all-to-all-start.1) | async-done | bytes 1056 | tf_op jit(solution)/shard_map/all_to_all | solution.py:91
  46.6 3.9 %gather_fusion = bf16[256,512]{1,0:T(8,128)(2,1)S(1)} fusion(bf16[4096,512]{1,0:T(8,128)(2,1)} %param.4, s32[1024]{0:T(1024)S(1)} %pad_clamp_fusion.2), kind=kCustom, calls=%fused_computation | custom fusion | bytes 525312 | tf_op jit(solution)/shard_map/jit(_take)/gather | solution.py:92
  50.6 0.8 select_select_fusion.1
  51.4 3.4 %all-to-all-start.2 = ((bf16[4,64,512]{2,1,0:T(8,128)(2,1)}), bf16[4,64,512]{2,1,0:T(8,128)(2,1)S(1)}, u32[]{:S(2)}, u32[]{:S(2)}) async-start(bf16[4,64,512]{2,1,0:T(8,128)(2,1)} %select_select_fusion.1), calls=%async_computation.2 | async-start | bytes 524288 | tf_op jit(solution)/shard_map/all_to_all | solution.py:94
  54.9 0.1 copy.21
  55.0 0.1 copy.25
  55.1 5.7 %all-to-all-done.2 = bf16[4,64,512]{2,1,0:T(8,128)(2,1)S(1)} async-done(((bf16[4,64,512]{2,1,0:T(8,128)(2,1)}), bf16[4,64,512]{2,1,0:T(8,128)(2,1)S(1)}, u32[]{:S(2)}, u32[]{:S(2)}) %all-to-all-start.2) | async-done | bytes 262176 | tf_op jit(solution)/shard_map/all_to_all | solution.py:94
  60.8 1.2 gather_fusion.1
  62.0 1.0 select_select_fusion
  63.1 5.5 %all-to-all-start.3 = ((bf16[64,4,512]{2,1,0:T(4,128)(2,1)}), bf16[64,4,512]{2,1,0:T(4,128)(2,1)S(1)}, u32[]{:S(2)}, u32[]{:S(2)}) async-start(bf16[64,4,512]{2,1,0:T(4,128)(2,1)} %select_select_fusion), calls=%async_computation.3 | async-start | bytes 524288 | tf_op jit(solution)/shard_map/all_to_all | solution.py:99
  68.6 12.9 %all-to-all-done.3 = bf16[64,4,512]{2,1,0:T(4,128)(2,1)S(1)} async-done(((bf16[64,4,512]{2,1,0:T(4,128)(2,1)}), bf16[64,4,512]{2,1,0:T(4,128)(2,1)S(1)}, u32[]{:S(2)}, u32[]{:S(2)}) %all-to-all-start.3) | async-done | bytes 262176 | tf_op jit(solution)/shard_map/all_to_all | solution.py:99
  81.6 0.8 gather_fusion.2
  82.5 0.2 fusion.8
  82.7 0.8 fusion.9
  83.5 1.0 fusion.10
  84.6 1.0 fusion.4
  85.6 15.5 %all_gather.7 = bf16[512,512]{1,0:T(8,128)(2,1)S(1)} all-gather(bf16[128,512]{1,0:T(8,128)(2,1)S(1)} %fusion.4), channel_id=1, replica_groups=mesh['xl'=2,'c'=2,'y'=4,'z'=8,'xh'=2] {'xl','xh'}, dimensions={0}, use_global_device_ids=true | all-gather | bytes 655360 | tf_op jit(solution)/shard_map/all_gather | solution.py:117
  101.1 59.2 %all-gather.2.cloned.1.call-done = bf16[8192,512]{1,0:T(8,128)(2,1)} async-done(((bf16[128,512]{1,0:T(8,128)(2,1)}), bf16[8192,512]{1,0:T(8,128)(2,1)}) %all-gather.2.cloned.1.call-update) | async-done | bytes 8388624 | tf_op jit(solution)/shard_map/all_gather | solution.py:116
  160.2 11.7 %fusion.1 = (f32[8192]{0:T(1024)S(1)}, f32[512]{0:T(512)S(1)}, f32[8192,512]{1,0:T(8,128)}) fusion(bf16[8192,512]{1,0:T(8,128)(2,1)} %all-gather.2.cloned.1.call-done, bf16[512,512]{1,0:T(8,128)(2,1)S(1)} %all_gather.7), kind=kOutput, calls=%fused_computation.9 | convolution fusion | flops 4307541504 | bytes 25724928 | tf_op jit(solution)/shard_map/rd,cd->rc/dot_general | solution.py:20
  171.9 0.2 collective-permute-start
  172.2 1.0 collective-permute-done
  173.1 1.8 collective-permute-start.1
  175.0 2.1 collective-permute-done.1
  177.1 1.5 collective-permute-start.2
  178.6 3.9 %collective-permute-done.2 = f32[8192]{0:T(1024)S(1)} collective-permute-done((f32[8192]{0:T(1024)S(1)}, f32[8192]{0:T(1024)S(1)}, u32[]{:S(2)}, u32[]{:S(2)}) %collective-permute-start.2) | collective-permute-done | bytes 32800 | tf_op jit(solution)/shard_map/ppermute | solution.py:48
  182.5 1.3 collective-permute-start.3
  183.7 2.7 %collective-permute-done.3 = f32[8192]{0:T(1024)S(1)} collective-permute-done((f32[8192]{0:T(1024)S(1)}, f32[8192]{0:T(1024)S(1)}, u32[]{:S(2)}, u32[]{:S(2)}) %collective-permute-start.3) | collective-permute-done | bytes 32800 | tf_op jit(solution)/shard_map/ppermute | solution.py:48
  186.4 1.3 collective-permute-start.4
  187.7 3.5 %collective-permute-done.4 = f32[8192]{0:T(1024)S(1)} collective-permute-done((f32[8192]{0:T(1024)S(1)}, f32[8192]{0:T(1024)S(1)}, u32[]{:S(2)}, u32[]{:S(2)}) %collective-permute-start.4) | collective-permute-done | bytes 32800 | tf_op jit(solution)/shard_map/ppermute | solution.py:48
  191.2 2.8 %collective-permute-start.5 = (f32[8192]{0:T(1024)S(1)}, f32[8192]{0:T(1024)S(1)}, u32[]{:S(2)}, u32[]{:S(2)}) collective-permute-start(f32[8192]{0:T(1024)S(1)} %add.157), channel_id=1, source_target_pairs={{0,8},{2,10},{4,12},{6,14},{8,0},{10,2},{12,4},{14,6},{1,9},{3,11}... | collective-permute-start | bytes 98312 | tf_op jit(solution)/shard_map/ppermute | solution.py:48
  194.1 10.7 %psum.7 = f32[512]{0:T(512)S(1)} all-reduce(f32[512]{0:T(512)S(1)} %get-tuple-element.6), channel_id=1, replica_groups=mesh['xl'=2,'c'=2,'y'=4,'z'=8,'xh'=2] {'xl','xh'}, use_global_device_ids=true, to_apply=%region_9.10 | all-reduce | flops 512 | bytes 4096 | tf_op jit(solution)/shard_map/psum | solution.py:119
  204.8 15.0 %fusion.2 = f32[512,512]{1,0:T(8,128)} fusion(bf16[8192,512]{1,0:T(8,128)(2,1)} %all-gather.2.cloned.1.call-done, f32[8192,512]{1,0:T(8,128)} %get-tuple-element.21, s32[512]{0:T(512)S(1)} %iota_subtract_fusion.1, f32[512]{0:T(512)S(1)} %psum.7, f32[8192]{0:T(1024)S(1)} %add.158, s32[8192]{0:T(1024)S(1)} %iota_subtract_fusion, ...), kind=kOutput, calls=%fused_computation.10 | convolution fusion | flops 4341104640 | bytes 26300416 | tf_op jit(solution)/shard_map/dot_general | solution.py:37
  219.9 29.3 %reduce-scatter.2.cloned.1.call-done = f32[128,512]{1,0:T(8,128)} async-done(((f32[512,512]{1,0:T(8,128)}), f32[128,512]{1,0:T(8,128)}) %reduce-scatter.2.cloned.1.call-update) | async-done | bytes 262160 | tf_op jit(solution)/shard_map/reduce_scatter | solution.py:123
  249.1 1.1 fusion.11
  250.2 1.8 fusion.7
  (42 shorter events, 1.4 us)
Async XLA Ops:
  39.6 6.9 %all-to-all-start.1 = ((s32[4,1,64]{2,1,0:T(1,128)}), s32[4,1,64]{2,1,0:T(1,128)S(1)}, u32[]{:S(2)}, u32[]{:S(2)}) async-start(s32[4,1,64]{2,1,0:T(1,128)} %all_to_all.16), calls=%async_computation.1 | async-start | bytes 4096 | tf_op jit(solution)/shard_map/all_to_all | solution.py:91
  51.4 9.4 %all-to-all-start.2 = ((bf16[4,64,512]{2,1,0:T(8,128)(2,1)}), bf16[4,64,512]{2,1,0:T(8,128)(2,1)S(1)}, u32[]{:S(2)}, u32[]{:S(2)}) async-start(bf16[4,64,512]{2,1,0:T(8,128)(2,1)} %select_select_fusion.1), calls=%async_computation.2 | async-start | bytes 524288 | tf_op jit(solution)/shard_map/all_to_all | solution.py:94
  63.1 18.5 %all-to-all-start.3 = ((bf16[64,4,512]{2,1,0:T(4,128)(2,1)}), bf16[64,4,512]{2,1,0:T(4,128)(2,1)S(1)}, u32[]{:S(2)}, u32[]{:S(2)}) async-start(bf16[64,4,512]{2,1,0:T(4,128)(2,1)} %select_select_fusion), calls=%async_computation.3 | async-start | bytes 524288 | tf_op jit(solution)/shard_map/all_to_all | solution.py:99
  68.6 91.7 %all-gather.2.cloned.1.call-start = ((), (), s32[]{:S(2)}) async-start(), calls=%async_computation.5 | async-start | bytes 8519680 | tf_op jit(solution)/shard_map/all_gather | solution.py:116
  83.5 165.6 %reduce-scatter.2.cloned.1.call-start = ((), (), s32[]{:S(2)}) async-start(), calls=%async_computation.6 | async-start | bytes 1310720 | tf_op jit(solution)/shard_map/reduce_scatter | solution.py:123
  171.9 1.2 collective-permute-start
  173.1 3.9 %collective-permute-start.1 = (f32[8192]{0:T(1024)S(1)}, f32[8192]{0:T(1024)S(1)}, u32[]{:S(2)}, u32[]{:S(2)}) collective-permute-start(f32[8192]{0:T(1024)S(1)} %add.153), channel_id=1, source_target_pairs={{0,16},{16,0},{32,48},{48,32},{1,17},{17,1},{33,49},{49,33},{2,18}... | collective-permute-start | bytes 98312 | tf_op jit(solution)/shard_map/ppermute | solution.py:48
  177.1 5.4 %collective-permute-start.2 = (f32[8192]{0:T(1024)S(1)}, f32[8192]{0:T(1024)S(1)}, u32[]{:S(2)}, u32[]{:S(2)}) collective-permute-start(f32[8192]{0:T(1024)S(1)} %add.154), channel_id=1, source_target_pairs={{0,32},{16,48},{32,0},{48,16},{1,33},{17,49},{33,1},{49,17},{2,34}... | collective-permute-start | bytes 98312 | tf_op jit(solution)/shard_map/ppermute | solution.py:48
  182.5 3.9 %collective-permute-start.3 = (f32[8192]{0:T(1024)S(1)}, f32[8192]{0:T(1024)S(1)}, u32[]{:S(2)}, u32[]{:S(2)}) collective-permute-start(f32[8192]{0:T(1024)S(1)} %add.155), channel_id=1, source_target_pairs={{0,2},{2,0},{4,6},{6,4},{8,10},{10,8},{12,14},{14,12},{1,3},{3,1},... | collective-permute-start | bytes 98312 | tf_op jit(solution)/shard_map/ppermute | solution.py:48
  186.4 4.8 %collective-permute-start.4 = (f32[8192]{0:T(1024)S(1)}, f32[8192]{0:T(1024)S(1)}, u32[]{:S(2)}, u32[]{:S(2)}) collective-permute-start(f32[8192]{0:T(1024)S(1)} %add.156), channel_id=1, source_target_pairs={{0,4},{2,6},{4,0},{6,2},{8,12},{10,14},{12,8},{14,10},{1,5},{3,7},... | collective-permute-start | bytes 98312 | tf_op jit(solution)/shard_map/ppermute | solution.py:48
  191.2 13.6 %collective-permute-start.5 = (f32[8192]{0:T(1024)S(1)}, f32[8192]{0:T(1024)S(1)}, u32[]{:S(2)}, u32[]{:S(2)}) collective-permute-start(f32[8192]{0:T(1024)S(1)} %add.157), channel_id=1, source_target_pairs={{0,8},{2,10},{4,12},{6,14},{8,0},{10,2},{12,4},{14,6},{1,9},{3,11}... | collective-permute-start | bytes 98312 | tf_op jit(solution)/shard_map/ppermute | solution.py:48
  204.8 44.3 %copy-start = (bf16[128,512]{1,0:T(8,128)(2,1)S(1)}, bf16[128,512]{1,0:T(8,128)(2,1)}, u32[]{:S(2)}) copy-start(bf16[128,512]{1,0:T(8,128)(2,1)} %param.5) | copy-start | bytes 393220
Sparse Core Ops, SparseCore 0:
  83.6 76.5 all-gather.1
  220.0 29.0 reduce-scatter.1

commit v2 on v1

--- a/solution.py
+++ b/solution.py
@@ -102,6 +102,32 @@
     ).astype(jnp.float32)
 
 
+def ring_pairs(size, step):
+    return [(i, (i + step) % size) for i in range(size)]
+
+
+def gather_columns(value, axes):
+    size = lax.axis_size(axes)
+    me = lax.axis_index(axes)
+    parts = [value] + [lax.ppermute(value, axes, ring_pairs(size, k)) for k in range(1, size)]
+    source = (me - jnp.arange(size, dtype=jnp.int32)) % size
+    return jnp.take(jnp.stack(parts), source, axis=0).reshape((-1,) + value.shape[1:])
+
+
+def scatter_columns(weights, row_block, axes, rows_dev):
+    size = lax.axis_size(axes)
+    me = lax.axis_index(axes)
+    total = None
+    for k in list(range(1, size)) + [0]:
+        target = (me + k) % size
+        piece = lax.dynamic_slice_in_dim(weights, target * rows_dev, rows_dev, axis=1)
+        part = column_terms(piece, row_block)
+        if k:
+            part = lax.ppermute(part, axes, ring_pairs(size, k))
+        total = part if total is None else total + part
+    return total
+
+
 def shards(queue, pred, owner, slot):
     rows_dev = pred.shape[0]
     fetched = fetch_rows(queue, owner, slot)
@@ -114,15 +140,13 @@
     row_at = lax.axis_index(ROWS)
     column_at = lax.axis_index(COLS)
     row_block = lax.all_gather(neighbour, ROWS, axis=0, tiled=True)
-    exponent = block_exp(row_block, lax.all_gather(queries, COLS, axis=0, tiled=True))
+    exponent = block_exp(row_block, gather_columns(queries, COLS))
     row_total = tree_sum(jnp.sum(exponent, 1), ROWS)
-    column_total = lax.psum(jnp.sum(exponent, 0), COLS)
+    column_total = tree_sum(jnp.sum(exponent, 0), COLS)
     weights = mixed_weights(
         exponent, row_total, column_total, row_at * rows_dev, column_at * rows_dev, rows_dev
     )
-    dquery = lax.psum_scatter(
-        column_terms(weights, row_block), COLS, scatter_dimension=0, tiled=True
-    )
+    dquery = scatter_columns(weights, row_block, COLS, rows_dev)
     dquery = dquery * INV_TAU
     radial = jnp.sum(predicted * dquery, 1, keepdims=True)
     return inverse * dquery - predicted * inverse * inverse * inverse * radial

time: 260 us -> 249 us (0.958)
  blocking collectives: 51.6 us -> 25.4 us
  starting transfers between devices: 21.2 us -> 34.3 us
  waiting for transfers between devices: 124 us -> 115 us
  other arithmetic: 10.2 us -> 18.8 us
    reduce_scatter x1 -> x0, waiting for transfers between devices: 29.3 us -> none  [shards(): lax.psum_scatter(column_terms(weights, row_block), COLS, scatter_dimensio...]
    all_gather x1 -> x0, blocking collectives: 15.5 us -> none  [shards(): lax.all_gather(queries, COLS, axis=0, tiled=True)]
    ppermute x0 -> x6, waiting for transfers between devices: none -> 12.9 us  [the longest x3 7.37 us: scatter_columns(): part = lax.ppermute(part, axes, ring_pairs(size, k))]
    convert_element_type x0 -> x1, other arithmetic: none -> 12.1 us  [mixed_weights(): return (0.5 * (exponent / row_total[:, None] + exponent / column_total[No...]
    psum x1 -> x0, blocking collectives: 10.7 us -> none  [shards(): column_total = lax.psum(jnp.sum(exponent, 0), COLS)]
    ppermute x0 -> x6, starting transfers between devices: none -> 8.53 us  [the longest x3 5.12 us: scatter_columns(): part = lax.ppermute(part, axes, ring_pairs(size, k))]
    all_gather x1, waiting for transfers between devices: 59.2 us -> 66.6 us  [shards(): row_block = lax.all_gather(neighbour, ROWS, axis=0, tiled=True)]
    ppermute x6 -> x8, starting transfers between devices: 8.96 us -> 13.5 us  [tree_sum(): value = value + lax.ppermute(value, axis, pairs)]
  transfers between devices with their start and end apart: 11 -> 18, of which waited for: 10 -> 14; matrix products, arithmetic and copies ran while one was open for 1% -> 2% of each run, Pallas kernels for 0% -> 0%
where the time goes in v2:
time: 249 us; the launch traced here: 248 us
  waiting for transfers between devices  115 us (46%)
  starting transfers between devices  34.3 us (14%)
  matrix products  27.5 us (11%)
  blocking collectives  25.4 us (10%)
  other arithmetic  18.8 us (8%)
  between operations  13.7 us (6%)
  local copies, waits for them, and re-layouts  12.4 us (5%)
    all_gather x1, waiting for transfers between devices, shards(): row_block = lax.all_gather(neighbour, ROWS, axis=0, tiled=True)  66.6 us
    all_to_all x1, blocking collectives, fetch_rows(): lax.all_to_all(request, INNER, split_axis=0, concat_axis=0, tiled=True)  25.4 us
    dot_general x4, matrix products, column_terms(): lax.dot_general(weights, row_block, (((0,), (0,)), ((), ())), preferred_e...  15.9 us
    ppermute x8, waiting for transfers between devices, tree_sum(): value = value + lax.ppermute(value, axis, pairs)  13.7 us
    ppermute x8, starting transfers between devices, tree_sum(): value = value + lax.ppermute(value, axis, pairs)  13.5 us
    all_to_all x1, waiting for transfers between devices, fetch_rows(): lax.all_to_all(relayed, INNER, split_axis=0, concat_axis=0, tiled=True)  12.9 us
    convert_element_type x1, other arithmetic, mixed_weights(): return (0.5 * (exponent / row_total[:, None] + exponent / column_total[No...  12.1 us
    dot_general x1, matrix products, block_exp(): jnp.einsum('rd,cd->rc', row_block, column_block, preferred_element_type=j...  11.7 us
  transfers between devices with their start and end apart: 18, of which 14 were waited for; matrix products, arithmetic and copies ran while one was open for 2% of the time, Pallas kernels for 0%

profile of v2, /device:TPU:8, one launch (start us, length us, event | category | flops | bytes accessed | tf_op | source)
XLA Modules:
  0.0 247.5 jit_solution(16135470003443653496)
XLA Ops:
  6.5 0.7 and_select_fusion.2
  8.1 0.7 and_bitcast_fusion
  8.8 1.0 scatter_custom_fusion.1
  9.8 1.1 scatter_custom_fusion
  11.1 25.4 %all_to_all.24 = s32[64,4,2]{1,2,0:T(2,128)S(1)} all-to-all(s32[64,4,2]{1,2,0:T(2,128)S(1)} %copy.19), channel_id=1, replica_groups=mesh['xl'=2,'c'=2,'y'=4,'z'=8,'xh'=2] {'y','z','xh'}, dimensions={0} | all-to-all | bytes 4096 | tf_op jit(solution)/shard_map/all_to_all | solution.py:77
  37.6 1.4 scatter_custom_fusion.2
  39.6 3.2 %all-to-all-start.1 = ((s32[4,1,64]{2,1,0:T(1,128)}), s32[4,1,64]{2,1,0:T(1,128)S(1)}, u32[]{:S(2)}, u32[]{:S(2)}) async-start(s32[4,1,64]{2,1,0:T(1,128)} %all_to_all.16), calls=%async_computation.1 | async-start | bytes 4096 | tf_op jit(solution)/shard_map/all_to_all | solution.py:91
  43.0 3.5 %all-to-all-done.1 = s32[4,1,64]{2,1,0:T(1,128)S(1)} async-done(((s32[4,1,64]{2,1,0:T(1,128)}), s32[4,1,64]{2,1,0:T(1,128)S(1)}, u32[]{:S(2)}, u32[]{:S(2)}) %all-to-all-start.1) | async-done | bytes 1056 | tf_op jit(solution)/shard_map/all_to_all | solution.py:91
  46.7 3.9 %gather_fusion = bf16[256,512]{1,0:T(8,128)(2,1)S(1)} fusion(bf16[4096,512]{1,0:T(8,128)(2,1)} %param.4, s32[1024]{0:T(1024)S(1)} %pad_clamp_fusion.3), kind=kCustom, calls=%fused_computation | custom fusion | bytes 525312 | tf_op jit(solution)/shard_map/jit(_take)/gather | solution.py:92
  50.6 0.8 select_select_fusion.1
  51.5 3.4 %all-to-all-start.2 = ((bf16[4,64,512]{2,1,0:T(8,128)(2,1)}), bf16[4,64,512]{2,1,0:T(8,128)(2,1)S(1)}, u32[]{:S(2)}, u32[]{:S(2)}) async-start(bf16[4,64,512]{2,1,0:T(8,128)(2,1)} %select_select_fusion.1), calls=%async_computation.2 | async-start | bytes 524288 | tf_op jit(solution)/shard_map/all_to_all | solution.py:94
  55.1 5.7 %all-to-all-done.2 = bf16[4,64,512]{2,1,0:T(8,128)(2,1)S(1)} async-done(((bf16[4,64,512]{2,1,0:T(8,128)(2,1)}), bf16[4,64,512]{2,1,0:T(8,128)(2,1)S(1)}, u32[]{:S(2)}, u32[]{:S(2)}) %all-to-all-start.2) | async-done | bytes 262176 | tf_op jit(solution)/shard_map/all_to_all | solution.py:94
  60.9 1.2 gather_fusion.1
  62.1 1.0 select_select_fusion
  63.1 5.5 %all-to-all-start.3 = ((bf16[64,4,512]{2,1,0:T(4,128)(2,1)}), bf16[64,4,512]{2,1,0:T(4,128)(2,1)S(1)}, u32[]{:S(2)}, u32[]{:S(2)}) async-start(bf16[64,4,512]{2,1,0:T(4,128)(2,1)} %select_select_fusion), calls=%async_computation.3 | async-start | bytes 524288 | tf_op jit(solution)/shard_map/all_to_all | solution.py:99
  68.7 12.9 %all-to-all-done.3 = bf16[64,4,512]{2,1,0:T(4,128)(2,1)S(1)} async-done(((bf16[64,4,512]{2,1,0:T(4,128)(2,1)}), bf16[64,4,512]{2,1,0:T(4,128)(2,1)S(1)}, u32[]{:S(2)}, u32[]{:S(2)}) %all-to-all-start.3) | async-done | bytes 262176 | tf_op jit(solution)/shard_map/all_to_all | solution.py:99
  81.7 0.8 gather_fusion.2
  82.7 0.8 fusion.16
  83.7 1.0 collective-permute-start
  84.8 0.7 collective-permute-start.1
  85.5 1.6 collective-permute-start.2
  87.4 3.4 %collective-permute-done = bf16[128,512]{1,0:T(8,128)(2,1)S(1)} collective-permute-done((bf16[128,512]{1,0:T(8,128)(2,1)S(1)}, bf16[128,512]{1,0:T(8,128)(2,1)S(1)}, u32[]{:S(2)}, u32[]{:S(2)}) %collective-permute-start) | collective-permute-done | bytes 131104 | tf_op jit(solution)/shard_map/ppermute | solution.py:112
  90.8 2.1 collective-permute-done.2
  93.7 66.6 %all-gather.2.cloned.1.call-done = bf16[8192,512]{1,0:T(8,128)(2,1)} async-done(((bf16[128,512]{1,0:T(8,128)(2,1)}), bf16[8192,512]{1,0:T(8,128)(2,1)}) %all-gather.2.cloned.1.call-update) | async-done | bytes 8388624 | tf_op jit(solution)/shard_map/all_gather | solution.py:142
  160.3 11.7 %fusion.1 = (f32[8192]{0:T(1024)S(1)}, f32[512]{0:T(512)S(1)}, f32[8192,512]{1,0:T(8,128)}) fusion(bf16[8192,512]{1,0:T(8,128)(2,1)} %all-gather.2.cloned.1.call-done, bf16[512,512]{1,0:T(8,128)(2,1)S(1)} %bitcast_select_fusion), kind=kOutput, calls=%fused_computation.10 | convolution fusion | flops 4307541504 | bytes 25724928 | tf_op jit(solution)/shard_map/rd,cd->rc/dot_general | solution.py:20
  172.2 1.0 collective-permute-done.3
  173.2 1.8 collective-permute-start.4
  175.0 2.1 collective-permute-done.4
  177.1 1.5 collective-permute-start.5
  178.6 3.9 %collective-permute-done.5 = f32[8192]{0:T(1024)S(1)} collective-permute-done((f32[8192]{0:T(1024)S(1)}, f32[8192]{0:T(1024)S(1)}, u32[]{:S(2)}, u32[]{:S(2)}) %collective-permute-start.5) | collective-permute-done | bytes 32800 | tf_op jit(solution)/shard_map/ppermute | solution.py:48
  182.5 1.2 collective-permute-start.6
  183.8 2.7 %collective-permute-done.6 = f32[8192]{0:T(1024)S(1)} collective-permute-done((f32[8192]{0:T(1024)S(1)}, f32[8192]{0:T(1024)S(1)}, u32[]{:S(2)}, u32[]{:S(2)}) %collective-permute-start.6) | collective-permute-done | bytes 32800 | tf_op jit(solution)/shard_map/ppermute | solution.py:48
  186.4 1.3 collective-permute-start.7
  187.8 1.6 collective-permute-start.9
  189.3 1.9 collective-permute-done.7
  191.3 2.8 %collective-permute-start.8 = (f32[8192]{0:T(1024)S(1)}, f32[8192]{0:T(1024)S(1)}, u32[]{:S(2)}, u32[]{:S(2)}) collective-permute-start(f32[8192]{0:T(1024)S(1)} %add.241), channel_id=1, source_target_pairs={{0,8},{2,10},{4,12},{6,14},{8,0},{10,2},{12,4},{14,6},{1,9},{3,11}... | collective-permute-start | bytes 98312 | tf_op jit(solution)/shard_map/ppermute | solution.py:48
  194.1 3.1 %collective-permute-start.10 = (f32[512]{0:T(512)S(1)}, f32[512]{0:T(512)S(1)}, u32[]{:S(2)}, u32[]{:S(2)}) collective-permute-start(f32[512]{0:T(512)S(1)} %add.243), channel_id=1, source_target_pairs={{0,1},{1,0},{2,3},{3,2},{4,5},{5,4},{6,7},{7,6},{8,9},{9,8},{10,11... | collective-permute-start | bytes 6152 | tf_op jit(solution)/shard_map/ppermute | solution.py:48
  197.1 2.1 collective-permute-done.10
  199.3 12.1 %subtract_convert_fusion = bf16[8192,512]{1,0:T(8,128)(2,1)S(1)} fusion(f32[8192,512]{1,0:T(8,128)} %get-tuple-element.21, s32[512]{0:T(512)S(1)} %iota_subtract_fusion.1, f32[512]{0:T(512)S(1)} %add.244, f32[8192]{0:T(1024)S(1)} %add.242, s32[8192]{0:T(1024)S(1)} %iota_subtract_fusion, pred[8192]{0:T(1024)(128)(4,1)S(1)} %get-tuple-element.26, ...), kind=kLoop, calls=%fused_computation.7 | loop fusion | flops 46137344 | bytes 25251840 | tf_op jit(solution)/shard_map/convert_element_type | solution.py:33
  211.4 7.8 %fusion.6 = f32[128,512]{1,0:T(8,128)S(1)} fusion(bf16[8192,512]{1,0:T(8,128)(2,1)} %all-gather.2.cloned.1.call-done, bf16[8192,512]{1,0:T(8,128)(2,1)S(1)} %subtract_convert_fusion, s32[]{:T(128)S(6)} %select_n.169), kind=kOutput, calls=%fused_computation.15 | convolution fusion | flops 1073741824 | bytes 10747908 | tf_op jit(solution)/shard_map/dot_general | solution.py:37
  219.2 1.5 collective-permute-start.12
  220.7 1.3 fusion.8
  222.1 3.0 %collective-permute-start.11 = (f32[128,512]{1,0:T(8,128)S(1)}, f32[128,512]{1,0:T(8,128)S(1)}, u32[]{:S(2)}, u32[]{:S(2)}) collective-permute-start(f32[128,512]{1,0:T(8,128)S(1)} %fusion.8), channel_id=1, source_target_pairs={{0,1},{1,128},{128,129},{129,0},{2,3},{3,130},{130,131},{131,2},{4... | collective-permute-start | bytes 786440 | tf_op jit(solution)/shard_map/ppermute | solution.py:126
  225.1 1.3 fusion.4
  227.0 4.1 %collective-permute-done.11 = f32[128,512]{1,0:T(8,128)S(1)} collective-permute-done((f32[128,512]{1,0:T(8,128)S(1)}, f32[128,512]{1,0:T(8,128)S(1)}, u32[]{:S(2)}, u32[]{:S(2)}) %collective-permute-start.11) | collective-permute-done | bytes 262176 | tf_op jit(solution)/shard_map/ppermute | solution.py:126
  231.1 3.3 %collective-permute-done.13 = f32[128,512]{1,0:T(8,128)S(1)} collective-permute-done((f32[128,512]{1,0:T(8,128)S(1)}, f32[128,512]{1,0:T(8,128)S(1)}, u32[]{:S(2)}, u32[]{:S(2)}) %collective-permute-start.13) | collective-permute-done | bytes 262176 | tf_op jit(solution)/shard_map/ppermute | solution.py:126
  234.4 5.4 %fusion.18 = (f32[128]{0:T(128)S(1)}, f32[128,512]{1,0:T(8,128)S(1)}) fusion(bf16[128,512]{1,0:T(8,128)(2,1)S(1)} %copy-done.2, bf16[8192,512]{1,0:T(8,128)(2,1)} %all-gather.2.cloned.1.call-done, bf16[8192,512]{1,0:T(8,128)(2,1)} %copy-done.1, s32[]{:T(128)S(6)} %select_n.173, f32[128,512]{1,0:T(8,128)S(1)} %collective-permute-done.13, ...), kind=kOutput, calls=%fused_computation.34 | convolution fusion | flops 1074200448 | bytes 11665924 | tf_op jit(solution)/shard_map/dot_general | solution.py:37
  239.8 0.8 fusion.14
  (70 shorter events, 5.8 us)
Async XLA Ops:
  6.5 77.0 %copy-start.2 = (bf16[128,512]{1,0:T(8,128)(2,1)S(1)}, bf16[128,512]{1,0:T(8,128)(2,1)}, u32[]{:S(2)}) copy-start(bf16[128,512]{1,0:T(8,128)(2,1)} %param.5) | copy-start | bytes 393220
  39.6 6.9 %all-to-all-start.1 = ((s32[4,1,64]{2,1,0:T(1,128)}), s32[4,1,64]{2,1,0:T(1,128)S(1)}, u32[]{:S(2)}, u32[]{:S(2)}) async-start(s32[4,1,64]{2,1,0:T(1,128)} %all_to_all.16), calls=%async_computation.1 | async-start | bytes 4096 | tf_op jit(solution)/shard_map/all_to_all | solution.py:91
  51.5 9.4 %all-to-all-start.2 = ((bf16[4,64,512]{2,1,0:T(8,128)(2,1)}), bf16[4,64,512]{2,1,0:T(8,128)(2,1)S(1)}, u32[]{:S(2)}, u32[]{:S(2)}) async-start(bf16[4,64,512]{2,1,0:T(8,128)(2,1)} %select_select_fusion.1), calls=%async_computation.2 | async-start | bytes 524288 | tf_op jit(solution)/shard_map/all_to_all | solution.py:94
  63.1 18.5 %all-to-all-start.3 = ((bf16[64,4,512]{2,1,0:T(4,128)(2,1)}), bf16[64,4,512]{2,1,0:T(4,128)(2,1)S(1)}, u32[]{:S(2)}, u32[]{:S(2)}) async-start(bf16[64,4,512]{2,1,0:T(4,128)(2,1)} %select_select_fusion), calls=%async_computation.3 | async-start | bytes 524288 | tf_op jit(solution)/shard_map/all_to_all | solution.py:99
  68.6 91.7 %all-gather.2.cloned.1.call-start = ((), (), s32[]{:S(2)}) async-start(), calls=%async_computation.4 | async-start | bytes 8519680 | tf_op jit(solution)/shard_map/all_gather | solution.py:142
  83.7 7.0 %collective-permute-start = (bf16[128,512]{1,0:T(8,128)(2,1)S(1)}, bf16[128,512]{1,0:T(8,128)(2,1)S(1)}, u32[]{:S(2)}, u32[]{:S(2)}) collective-permute-start(bf16[128,512]{1,0:T(8,128)(2,1)S(1)} %fusion.11), channel_id=1, source_target_pairs={{0,1},{1,128},{128,129},{129,0},{2,3},{3,130},{130,131},{131,2},{4... | collective-permute-start | bytes 393224 | tf_op jit(solution)/shard_map/ppermute | solution.py:112
  84.8 6.0 %collective-permute-start.1 = (bf16[128,512]{1,0:T(8,128)(2,1)S(1)}, bf16[128,512]{1,0:T(8,128)(2,1)S(1)}, u32[]{:S(2)}, u32[]{:S(2)}) collective-permute-start(bf16[128,512]{1,0:T(8,128)(2,1)S(1)} %fusion.11), channel_id=1, source_target_pairs={{0,128},{1,129},{128,0},{129,1},{2,130},{3,131},{130,2},{131,3},{4... | collective-permute-start | bytes 393224 | tf_op jit(solution)/shard_map/ppermute | solution.py:112
  85.5 7.3 %collective-permute-start.2 = (bf16[128,512]{1,0:T(8,128)(2,1)S(1)}, bf16[128,512]{1,0:T(8,128)(2,1)S(1)}, u32[]{:S(2)}, u32[]{:S(2)}) collective-permute-start(bf16[128,512]{1,0:T(8,128)(2,1)S(1)} %fusion.11), channel_id=1, source_target_pairs={{0,129},{1,0},{128,1},{129,128},{2,131},{3,2},{130,3},{131,130},{4... | collective-permute-start | bytes 393224 | tf_op jit(solution)/shard_map/ppermute | solution.py:112
  172.0 1.2 collective-permute-start.3
  173.2 3.9 %collective-permute-start.4 = (f32[8192]{0:T(1024)S(1)}, f32[8192]{0:T(1024)S(1)}, u32[]{:S(2)}, u32[]{:S(2)}) collective-permute-start(f32[8192]{0:T(1024)S(1)} %add.237), channel_id=1, source_target_pairs={{0,16},{16,0},{32,48},{48,32},{1,17},{17,1},{33,49},{49,33},{2,18}... | collective-permute-start | bytes 98312 | tf_op jit(solution)/shard_map/ppermute | solution.py:48
  177.1 5.4 %collective-permute-start.5 = (f32[8192]{0:T(1024)S(1)}, f32[8192]{0:T(1024)S(1)}, u32[]{:S(2)}, u32[]{:S(2)}) collective-permute-start(f32[8192]{0:T(1024)S(1)} %add.238), channel_id=1, source_target_pairs={{0,32},{16,48},{32,0},{48,16},{1,33},{17,49},{33,1},{49,17},{2,34}... | collective-permute-start | bytes 98312 | tf_op jit(solution)/shard_map/ppermute | solution.py:48
  182.5 3.9 %collective-permute-start.6 = (f32[8192]{0:T(1024)S(1)}, f32[8192]{0:T(1024)S(1)}, u32[]{:S(2)}, u32[]{:S(2)}) collective-permute-start(f32[8192]{0:T(1024)S(1)} %add.239), channel_id=1, source_target_pairs={{0,2},{2,0},{4,6},{6,4},{8,10},{10,8},{12,14},{14,12},{1,3},{3,1},... | collective-permute-start | bytes 98312 | tf_op jit(solution)/shard_map/ppermute | solution.py:48
  186.4 4.8 %collective-permute-start.7 = (f32[8192]{0:T(1024)S(1)}, f32[8192]{0:T(1024)S(1)}, u32[]{:S(2)}, u32[]{:S(2)}) collective-permute-start(f32[8192]{0:T(1024)S(1)} %add.240), channel_id=1, source_target_pairs={{0,4},{2,6},{4,0},{6,2},{8,12},{10,14},{12,8},{14,10},{1,5},{3,7},... | collective-permute-start | bytes 98312 | tf_op jit(solution)/shard_map/ppermute | solution.py:48
  187.8 6.3 %collective-permute-start.9 = (f32[512]{0:T(512)S(1)}, f32[512]{0:T(512)S(1)}, u32[]{:S(2)}, u32[]{:S(2)}) collective-permute-start(f32[512]{0:T(512)S(1)} %get-tuple-element.6), channel_id=1, source_target_pairs={{0,128},{128,0},{1,129},{129,1},{2,130},{130,2},{3,131},{131,3},{4... | collective-permute-start | bytes 6152 | tf_op jit(solution)/shard_map/ppermute | solution.py:48
  191.3 8.0 %collective-permute-start.8 = (f32[8192]{0:T(1024)S(1)}, f32[8192]{0:T(1024)S(1)}, u32[]{:S(2)}, u32[]{:S(2)}) collective-permute-start(f32[8192]{0:T(1024)S(1)} %add.241), channel_id=1, source_target_pairs={{0,8},{2,10},{4,12},{6,14},{8,0},{10,2},{12,4},{14,6},{1,9},{3,11}... | collective-permute-start | bytes 98312 | tf_op jit(solution)/shard_map/ppermute | solution.py:48
  194.1 5.2 %collective-permute-start.10 = (f32[512]{0:T(512)S(1)}, f32[512]{0:T(512)S(1)}, u32[]{:S(2)}, u32[]{:S(2)}) collective-permute-start(f32[512]{0:T(512)S(1)} %add.243), channel_id=1, source_target_pairs={{0,1},{1,0},{2,3},{3,2},{4,5},{5,4},{6,7},{7,6},{8,9},{9,8},{10,11... | collective-permute-start | bytes 6152 | tf_op jit(solution)/shard_map/ppermute | solution.py:48
  211.4 13.7 %copy-start.1 = (bf16[8192,512]{1,0:T(8,128)(2,1)}, bf16[8192,512]{1,0:T(8,128)(2,1)S(1)}, u32[]{:S(2)}) copy-start(bf16[8192,512]{1,0:T(8,128)(2,1)S(1)} %subtract_convert_fusion) | copy-start | bytes 25165828
  211.4 9.3 %copy-start = (bf16[8192,512]{1,0:T(8,128)(2,1)S(1)}, bf16[8192,512]{1,0:T(8,128)(2,1)}, u32[]{:S(2)}) copy-start(bf16[8192,512]{1,0:T(8,128)(2,1)} %all-gather.2.cloned.1.call-done) | copy-start | bytes 25165828
  219.2 7.8 %collective-permute-start.12 = (f32[128,512]{1,0:T(8,128)S(1)}, f32[128,512]{1,0:T(8,128)S(1)}, u32[]{:S(2)}, u32[]{:S(2)}) collective-permute-start(f32[128,512]{1,0:T(8,128)S(1)} %fusion.6), channel_id=1, source_target_pairs={{0,128},{1,129},{128,0},{129,1},{2,130},{3,131},{130,2},{131,3},{4... | collective-permute-start | bytes 786440 | tf_op jit(solution)/shard_map/ppermute | solution.py:126
  222.1 9.1 %collective-permute-start.11 = (f32[128,512]{1,0:T(8,128)S(1)}, f32[128,512]{1,0:T(8,128)S(1)}, u32[]{:S(2)}, u32[]{:S(2)}) collective-permute-start(f32[128,512]{1,0:T(8,128)S(1)} %fusion.8), channel_id=1, source_target_pairs={{0,1},{1,128},{128,129},{129,0},{2,3},{3,130},{130,131},{131,2},{4... | collective-permute-start | bytes 786440 | tf_op jit(solution)/shard_map/ppermute | solution.py:126
  226.4 8.0 %collective-permute-start.13 = (f32[128,512]{1,0:T(8,128)S(1)}, f32[128,512]{1,0:T(8,128)S(1)}, u32[]{:S(2)}, u32[]{:S(2)}) collective-permute-start(f32[128,512]{1,0:T(8,128)S(1)} %fusion.4), channel_id=1, source_target_pairs={{0,129},{1,0},{128,1},{129,128},{2,131},{3,2},{130,3},{131,130},{4... | collective-permute-start | bytes 786440 | tf_op jit(solution)/shard_map/ppermute | solution.py:126
Sparse Core Ops, SparseCore 0:
  83.6 76.5 all-gather.1

commit v3 on v2

--- a/solution.py
+++ b/solution.py
@@ -42,11 +42,12 @@
 def tree_sum(value, axes):
     for axis in axes:
         size = lax.axis_size(axis)
-        step = 1
-        while step < size:
-            pairs = [(i, i ^ step) for i in range(size)]
-            value = value + lax.ppermute(value, axis, pairs)
-            step *= 2
+        me = lax.axis_index(axis)
+        parts = [value] + [lax.ppermute(value, axis, ring_pairs(size, k)) for k in range(1, size)]
+        ordered = jnp.take(jnp.stack(parts), (me - jnp.arange(size, dtype=jnp.int32)) % size, axis=0)
+        value = ordered[0]
+        for k in range(1, size):
+            value = value + ordered[k]
     return value
 
 
@@ -117,14 +118,12 @@
 def scatter_columns(weights, row_block, axes, rows_dev):
     size = lax.axis_size(axes)
     me = lax.axis_index(axes)
-    total = None
-    for k in list(range(1, size)) + [0]:
+    terms = column_terms(weights, row_block)
+    total = lax.dynamic_slice_in_dim(terms, me * rows_dev, rows_dev, axis=0)
+    for k in range(1, size):
         target = (me + k) % size
-        piece = lax.dynamic_slice_in_dim(weights, target * rows_dev, rows_dev, axis=1)
-        part = column_terms(piece, row_block)
-        if k:
-            part = lax.ppermute(part, axes, ring_pairs(size, k))
-        total = part if total is None else total + part
+        piece = lax.dynamic_slice_in_dim(terms, target * rows_dev, rows_dev, axis=0)
+        total = total + lax.ppermute(piece, axes, ring_pairs(size, k))
     return total
 
 

time: 249 us -> 243 us (0.976)
  other arithmetic: 18.8 us -> 6.95 us
  starting transfers between devices: 34.3 us -> 41.5 us
  local copies, waits for them, and re-layouts: 12.4 us -> 18 us
  waiting for transfers between devices: 115 us -> 110 us
    convert_element_type x1 -> x0, other arithmetic: 12.1 us -> none  [mixed_weights(): return (0.5 * (exponent / row_total[:, None] + exponent / column_total[No...]
    ppermute x11 -> x16, starting transfers between devices: 18.7 us -> 26 us  [the longest x13 22.6 us: tree_sum(): lax.ppermute(value, axis, ring_pairs(size, k))]
    ppermute x11 -> x16, waiting for transfers between devices: 21.1 us -> 17.3 us  [the longest x13 8.66 us: tree_sum(): lax.ppermute(value, axis, ring_pairs(size, k))]
    gather x0 -> x5, local copies, waits for them, and re-layouts: none -> 2.95 us  [tree_sum(): jnp.take(jnp.stack(parts), (me - jnp.arange(size, dtype=jnp.int32)) % siz...]
    dot_general x4 -> x1, matrix products: 15.9 us -> 15.1 us  [column_terms(): lax.dot_general(weights, row_block, (((0,), (0,)), ((), ())), preferred_e...]
  transfers between devices with their start and end apart: 18 -> 23, of which waited for: 14 -> 14; matrix products, arithmetic and copies ran while one was open for 2% -> 2% of each run, Pallas kernels for 0% -> 0%
where the time goes in v3:
time: 243 us
  waiting for transfers between devices  110 us (45%)
  starting transfers between devices  41.5 us (17%)
  matrix products  26.7 us (11%)
  blocking collectives  25.4 us (10%)
  local copies, waits for them, and re-layouts  18 us (7%)
  between operations  13.9 us (6%)
  other arithmetic  6.95 us (3%)
    all_gather x1, waiting for transfers between devices, shards(): row_block = lax.all_gather(neighbour, ROWS, axis=0, tiled=True)  65.4 us
    all_to_all x1, blocking collectives, fetch_rows(): lax.all_to_all(request, INNER, split_axis=0, concat_axis=0, tiled=True)  25.4 us
    ppermute x13, starting transfers between devices, tree_sum(): lax.ppermute(value, axis, ring_pairs(size, k))  22.6 us
    dot_general x1, matrix products, column_terms(): lax.dot_general(weights, row_block, (((0,), (0,)), ((), ())), preferred_e...  15.1 us
    all_to_all x1, waiting for transfers between devices, fetch_rows(): lax.all_to_all(relayed, INNER, split_axis=0, concat_axis=0, tiled=True)  12.9 us
    dot_general x1, matrix products, block_exp(): jnp.einsum('rd,cd->rc', row_block, column_block, preferred_element_type=j...  11.7 us
    ppermute x13, waiting for transfers between devices, tree_sum(): lax.ppermute(value, axis, ring_pairs(size, k))  8.66 us
    ppermute x3, waiting for transfers between devices, scatter_columns(): total = total + lax.ppermute(piece, axes, ring_pairs(size, k))  8.61 us
  transfers between devices with their start and end apart: 23, of which 14 were waited for; matrix products, arithmetic and copies ran while one was open for 2% of the time, Pallas kernels for 0%

profile of v3, /device:TPU:8, one launch (start us, length us, event | category | flops | bytes accessed | tf_op | source)
XLA Modules:
  0.0 242.6 jit_solution(12669318020438396320)
XLA Ops:
  6.5 0.7 and_select_fusion.10
  8.0 0.7 and_bitcast_fusion
  8.7 1.0 scatter_custom_fusion.1
  9.8 1.1 scatter_custom_fusion
  11.1 25.4 %all_to_all.24 = s32[64,4,2]{1,2,0:T(2,128)S(1)} all-to-all(s32[64,4,2]{1,2,0:T(2,128)S(1)} %copy.33), channel_id=1, replica_groups=mesh['xl'=2,'c'=2,'y'=4,'z'=8,'xh'=2] {'y','z','xh'}, dimensions={0} | all-to-all | bytes 4096 | tf_op jit(solution)/shard_map/all_to_all | solution.py:78
  37.5 1.4 scatter_custom_fusion.2
  39.6 3.2 %all-to-all-start.1 = ((s32[4,1,64]{2,1,0:T(1,128)}), s32[4,1,64]{2,1,0:T(1,128)S(1)}, u32[]{:S(2)}, u32[]{:S(2)}) async-start(s32[4,1,64]{2,1,0:T(1,128)} %all_to_all.16), calls=%async_computation.1 | async-start | bytes 4096 | tf_op jit(solution)/shard_map/all_to_all | solution.py:92
  43.0 3.5 %all-to-all-done.1 = s32[4,1,64]{2,1,0:T(1,128)S(1)} async-done(((s32[4,1,64]{2,1,0:T(1,128)}), s32[4,1,64]{2,1,0:T(1,128)S(1)}, u32[]{:S(2)}, u32[]{:S(2)}) %all-to-all-start.1) | async-done | bytes 1056 | tf_op jit(solution)/shard_map/all_to_all | solution.py:92
  46.6 3.9 %gather_fusion = bf16[256,512]{1,0:T(8,128)(2,1)S(1)} fusion(bf16[4096,512]{1,0:T(8,128)(2,1)} %param.6, s32[1024]{0:T(1024)S(1)} %pad_clamp_fusion.8), kind=kCustom, calls=%fused_computation.2 | custom fusion | bytes 525312 | tf_op jit(solution)/shard_map/jit(_take)/gather | solution.py:93
  50.6 0.8 select_select_fusion.1
  51.4 3.4 %all-to-all-start.2 = ((bf16[4,64,512]{2,1,0:T(8,128)(2,1)}), bf16[4,64,512]{2,1,0:T(8,128)(2,1)S(1)}, u32[]{:S(2)}, u32[]{:S(2)}) async-start(bf16[4,64,512]{2,1,0:T(8,128)(2,1)} %select_select_fusion.1), calls=%async_computation.2 | async-start | bytes 524288 | tf_op jit(solution)/shard_map/all_to_all | solution.py:95
  55.1 5.7 %all-to-all-done.2 = bf16[4,64,512]{2,1,0:T(8,128)(2,1)S(1)} async-done(((bf16[4,64,512]{2,1,0:T(8,128)(2,1)}), bf16[4,64,512]{2,1,0:T(8,128)(2,1)S(1)}, u32[]{:S(2)}, u32[]{:S(2)}) %all-to-all-start.2) | async-done | bytes 262176 | tf_op jit(solution)/shard_map/all_to_all | solution.py:95
  60.8 1.2 gather_fusion.1
  62.0 1.0 select_select_fusion
  63.1 5.5 %all-to-all-start.3 = ((bf16[64,4,512]{2,1,0:T(4,128)(2,1)}), bf16[64,4,512]{2,1,0:T(4,128)(2,1)S(1)}, u32[]{:S(2)}, u32[]{:S(2)}) async-start(bf16[64,4,512]{2,1,0:T(4,128)(2,1)} %select_select_fusion), calls=%async_computation.3 | async-start | bytes 524288 | tf_op jit(solution)/shard_map/all_to_all | solution.py:100
  68.6 12.9 %all-to-all-done.3 = bf16[64,4,512]{2,1,0:T(4,128)(2,1)S(1)} async-done(((bf16[64,4,512]{2,1,0:T(4,128)(2,1)}), bf16[64,4,512]{2,1,0:T(4,128)(2,1)S(1)}, u32[]{:S(2)}, u32[]{:S(2)}) %all-to-all-start.3) | async-done | bytes 262176 | tf_op jit(solution)/shard_map/all_to_all | solution.py:100
  81.6 0.8 gather_fusion.2
  82.7 0.8 fusion.9
  83.5 1.0 copy.42
  84.6 1.0 collective-permute-start
  85.7 0.7 collective-permute-start.1
  86.4 1.6 collective-permute-start.2
  88.5 3.2 %collective-permute-done = bf16[128,512]{0,1:T(8,128)(2,1)S(1)} collective-permute-done((bf16[128,512]{0,1:T(8,128)(2,1)S(1)}, bf16[128,512]{0,1:T(8,128)(2,1)S(1)}, u32[]{:S(2)}, u32[]{:S(2)}) %collective-permute-start) | collective-permute-done | bytes 131104 | tf_op jit(solution)/shard_map/ppermute | solution.py:113
  91.7 2.1 collective-permute-done.2
  94.9 65.4 %all-gather.2.cloned.1.call-done = bf16[8192,512]{1,0:T(8,128)(2,1)} async-done(((bf16[128,512]{1,0:T(8,128)(2,1)}), bf16[8192,512]{1,0:T(8,128)(2,1)}) %all-gather.2.cloned.1.call-update) | async-done | bytes 8388624 | tf_op jit(solution)/shard_map/all_gather | solution.py:141
  160.2 11.7 %fusion.1 = (f32[8192]{0:T(1024)S(1)}, f32[512]{0:T(512)S(1)}, f32[8192,512]{1,0:T(8,128)}) fusion(bf16[8192,512]{1,0:T(8,128)(2,1)} %all-gather.2.cloned.1.call-done, bf16[512,512]{1,0:T(8,128)(2,1)S(1)} %bitcast_select_fusion), kind=kOutput, calls=%fused_computation.15 | convolution fusion | flops 4307541504 | bytes 25724928 | tf_op jit(solution)/shard_map/rd,cd->rc/dot_general | solution.py:20
  171.9 1.5 collective-permute-start.14
  173.4 2.1 collective-permute-done.14
  176.2 3.0 %collective-permute-start.15 = (f32[512]{0:T(512)S(1)}, f32[512]{0:T(512)S(1)}, u32[]{:S(2)}, u32[]{:S(2)}) collective-permute-start(f32[512]{0:T(512)S(1)} %bitcast.115), channel_id=1, source_target_pairs={{0,1},{1,0},{2,3},{3,2},{4,5},{5,4},{6,7},{7,6},{8,9},{9,8},{10,11... | collective-permute-start | bytes 6152 | tf_op jit(solution)/shard_map/ppermute | solution.py:46
  180.0 1.3 collective-permute-start.4
  181.3 2.7 %collective-permute-start.5 = (f32[8192]{0:T(1024)S(1)}, f32[8192]{0:T(1024)S(1)}, u32[]{:S(2)}, u32[]{:S(2)}) collective-permute-start(f32[8192]{0:T(1024)S(1)} %bitcast.96), channel_id=1, source_target_pairs={{0,32},{16,48},{32,0},{48,16},{1,33},{17,49},{33,1},{49,17},{2,34}... | collective-permute-start | bytes 98312 | tf_op jit(solution)/shard_map/ppermute | solution.py:46
  184.8 1.9 collective-permute-done.5
  186.7 1.2 collective-permute-done.6
  188.8 1.3 collective-permute-start.7
  190.1 2.1 collective-permute-start.8
  192.3 1.7 collective-permute-start.9
  193.9 2.6 %collective-permute-start.10 = (f32[8192]{0:T(1024)S(1)}, f32[8192]{0:T(1024)S(1)}, u32[]{:S(2)}, u32[]{:S(2)}) collective-permute-start(f32[8192]{0:T(1024)S(1)} %bitcast.91), channel_id=1, source_target_pairs={{0,8},{2,10},{4,12},{6,14},{8,0},{10,2},{12,4},{14,6},{1,9},{3,11}... | collective-permute-start | bytes 98312 | tf_op jit(solution)/shard_map/ppermute | solution.py:46
  196.6 3.1 %collective-permute-start.11 = (f32[8192]{0:T(1024)S(1)}, f32[8192]{0:T(1024)S(1)}, u32[]{:S(2)}, u32[]{:S(2)}) collective-permute-start(f32[8192]{0:T(1024)S(1)} %bitcast.92), channel_id=1, source_target_pairs={{0,10},{2,12},{4,14},{6,0},{8,2},{10,4},{12,6},{14,8},{1,11},{3,13... | collective-permute-start | bytes 98312 | tf_op jit(solution)/shard_map/ppermute | solution.py:46
  199.7 2.7 %collective-permute-start.12 = (f32[8192]{0:T(1024)S(1)}, f32[8192]{0:T(1024)S(1)}, u32[]{:S(2)}, u32[]{:S(2)}) collective-permute-start(f32[8192]{0:T(1024)S(1)} %bitcast.93), channel_id=1, source_target_pairs={{0,12},{2,14},{4,0},{6,2},{8,4},{10,6},{12,8},{14,10},{1,13},{3,15... | collective-permute-start | bytes 98312 | tf_op jit(solution)/shard_map/ppermute | solution.py:46
  202.9 1.6 collective-permute-done.12
  204.5 1.8 collective-permute-done.13
  207.6 15.1 %fusion.2 = f32[512,512]{0,1:T(8,128)S(1)} fusion(bf16[8192,512]{1,0:T(8,128)(2,1)} %all-gather.2.cloned.1.call-done, f32[8192,512]{1,0:T(8,128)} %get-tuple-element.27, s32[512]{0:T(512)S(1)} %iota_subtract_fusion.1, f32[512]{0:T(512)S(1)} %bitcast.117, f32[8192]{0:T(1024)S(1)} %bitcast.108, s32[8192]{0:T(1024)S(1)} %iota_subtract_fusion, ...), kind=kOutput, calls=%fused_computation.16 | convolution fusion | flops 4341104640 | bytes 26300416 | tf_op jit(solution)/shard_map/dot_general | solution.py:37
  223.4 1.5 collective-permute-start.17
  224.9 1.2 collective-permute-start.18
  226.1 5.0 %collective-permute-done.16 = f32[128,512]{0,1:T(8,128)S(1)} collective-permute-done((f32[128,512]{0,1:T(8,128)S(1)}, f32[128,512]{0,1:T(8,128)S(1)}, u32[]{:S(2)}, u32[]{:S(2)}) %collective-permute-start.16) | collective-permute-done | bytes 262176 | tf_op jit(solution)/shard_map/ppermute | solution.py:126
  231.1 0.9 collective-permute-done.17
  232.1 2.7 %collective-permute-done.18 = f32[128,512]{0,1:T(8,128)S(1)} collective-permute-done((f32[128,512]{0,1:T(8,128)S(1)}, f32[128,512]{0,1:T(8,128)S(1)}, u32[]{:S(2)}, u32[]{:S(2)}) %collective-permute-start.18) | collective-permute-done | bytes 262176 | tf_op jit(solution)/shard_map/ppermute | solution.py:126
  234.9 0.8 copy.44
  (100 shorter events, 11.1 us)
Async XLA Ops:
  39.6 6.9 %all-to-all-start.1 = ((s32[4,1,64]{2,1,0:T(1,128)}), s32[4,1,64]{2,1,0:T(1,128)S(1)}, u32[]{:S(2)}, u32[]{:S(2)}) async-start(s32[4,1,64]{2,1,0:T(1,128)} %all_to_all.16), calls=%async_computation.1 | async-start | bytes 4096 | tf_op jit(solution)/shard_map/all_to_all | solution.py:92
  51.4 9.4 %all-to-all-start.2 = ((bf16[4,64,512]{2,1,0:T(8,128)(2,1)}), bf16[4,64,512]{2,1,0:T(8,128)(2,1)S(1)}, u32[]{:S(2)}, u32[]{:S(2)}) async-start(bf16[4,64,512]{2,1,0:T(8,128)(2,1)} %select_select_fusion.1), calls=%async_computation.2 | async-start | bytes 524288 | tf_op jit(solution)/shard_map/all_to_all | solution.py:95
  63.1 18.5 %all-to-all-start.3 = ((bf16[64,4,512]{2,1,0:T(4,128)(2,1)}), bf16[64,4,512]{2,1,0:T(4,128)(2,1)S(1)}, u32[]{:S(2)}, u32[]{:S(2)}) async-start(bf16[64,4,512]{2,1,0:T(4,128)(2,1)} %select_select_fusion), calls=%async_computation.3 | async-start | bytes 524288 | tf_op jit(solution)/shard_map/all_to_all | solution.py:100
  68.6 91.7 %all-gather.2.cloned.1.call-start = ((), (), s32[]{:S(2)}) async-start(), calls=%async_computation.4 | async-start | bytes 8519680 | tf_op jit(solution)/shard_map/all_gather | solution.py:141
  84.6 7.0 %collective-permute-start = (bf16[128,512]{0,1:T(8,128)(2,1)S(1)}, bf16[128,512]{0,1:T(8,128)(2,1)S(1)}, u32[]{:S(2)}, u32[]{:S(2)}) collective-permute-start(bf16[128,512]{0,1:T(8,128)(2,1)S(1)} %fusion.4), channel_id=1, source_target_pairs={{0,1},{1,128},{128,129},{129,0},{2,3},{3,130},{130,131},{131,2},{4... | collective-permute-start | bytes 393224 | tf_op jit(solution)/shard_map/ppermute | solution.py:113
  85.7 6.0 %collective-permute-start.1 = (bf16[128,512]{0,1:T(8,128)(2,1)S(1)}, bf16[128,512]{0,1:T(8,128)(2,1)S(1)}, u32[]{:S(2)}, u32[]{:S(2)}) collective-permute-start(bf16[128,512]{0,1:T(8,128)(2,1)S(1)} %fusion.4), channel_id=1, source_target_pairs={{0,128},{1,129},{128,0},{129,1},{2,130},{3,131},{130,2},{131,3},{4... | collective-permute-start | bytes 393224 | tf_op jit(solution)/shard_map/ppermute | solution.py:113
  86.4 7.3 %collective-permute-start.2 = (bf16[128,512]{0,1:T(8,128)(2,1)S(1)}, bf16[128,512]{0,1:T(8,128)(2,1)S(1)}, u32[]{:S(2)}, u32[]{:S(2)}) collective-permute-start(bf16[128,512]{0,1:T(8,128)(2,1)S(1)} %fusion.4), channel_id=1, source_target_pairs={{0,129},{1,0},{128,1},{129,128},{2,131},{3,2},{130,3},{131,130},{4... | collective-permute-start | bytes 393224 | tf_op jit(solution)/shard_map/ppermute | solution.py:113
  171.9 3.6 %collective-permute-start.14 = (f32[512]{0:T(512)S(1)}, f32[512]{0:T(512)S(1)}, u32[]{:S(2)}, u32[]{:S(2)}) collective-permute-start(f32[512]{0:T(512)S(1)} %get-tuple-element.7), channel_id=1, source_target_pairs={{0,128},{128,0},{1,129},{129,1},{2,130},{130,2},{3,131},{131,3},{4... | collective-permute-start | bytes 6152 | tf_op jit(solution)/shard_map/ppermute | solution.py:46
  173.4 5.8 %collective-permute-start.3 = (f32[8192]{0:T(1024)S(1)}, f32[8192]{0:T(1024)S(1)}, u32[]{:S(2)}, u32[]{:S(2)}) collective-permute-start(f32[8192]{0:T(1024)S(1)} %get-tuple-element.6), channel_id=1, source_target_pairs={{0,64},{64,0},{1,65},{65,1},{2,66},{66,2},{3,67},{67,3},{4,68},{68... | collective-permute-start | bytes 98312 | tf_op jit(solution)/shard_map/ppermute | solution.py:46
  176.2 8.0 %collective-permute-start.15 = (f32[512]{0:T(512)S(1)}, f32[512]{0:T(512)S(1)}, u32[]{:S(2)}, u32[]{:S(2)}) collective-permute-start(f32[512]{0:T(512)S(1)} %bitcast.115), channel_id=1, source_target_pairs={{0,1},{1,0},{2,3},{3,2},{4,5},{5,4},{6,7},{7,6},{8,9},{9,8},{10,11... | collective-permute-start | bytes 6152 | tf_op jit(solution)/shard_map/ppermute | solution.py:46
  180.0 4.8 %collective-permute-start.4 = (f32[8192]{0:T(1024)S(1)}, f32[8192]{0:T(1024)S(1)}, u32[]{:S(2)}, u32[]{:S(2)}) collective-permute-start(f32[8192]{0:T(1024)S(1)} %bitcast.95), channel_id=1, source_target_pairs={{0,16},{16,32},{32,48},{48,0},{1,17},{17,33},{33,49},{49,1},{2,18}... | collective-permute-start | bytes 98312 | tf_op jit(solution)/shard_map/ppermute | solution.py:46
  181.3 5.4 %collective-permute-start.5 = (f32[8192]{0:T(1024)S(1)}, f32[8192]{0:T(1024)S(1)}, u32[]{:S(2)}, u32[]{:S(2)}) collective-permute-start(f32[8192]{0:T(1024)S(1)} %bitcast.96), channel_id=1, source_target_pairs={{0,32},{16,48},{32,0},{48,16},{1,33},{17,49},{33,1},{49,17},{2,34}... | collective-permute-start | bytes 98312 | tf_op jit(solution)/shard_map/ppermute | solution.py:46
  184.0 3.9 %collective-permute-start.6 = (f32[8192]{0:T(1024)S(1)}, f32[8192]{0:T(1024)S(1)}, u32[]{:S(2)}, u32[]{:S(2)}) collective-permute-start(f32[8192]{0:T(1024)S(1)} %bitcast.97), channel_id=1, source_target_pairs={{0,48},{16,0},{32,16},{48,32},{1,49},{17,1},{33,17},{49,33},{2,50}... | collective-permute-start | bytes 98312 | tf_op jit(solution)/shard_map/ppermute | solution.py:46
  188.8 10.8 %collective-permute-start.7 = (f32[8192]{0:T(1024)S(1)}, f32[8192]{0:T(1024)S(1)}, u32[]{:S(2)}, u32[]{:S(2)}) collective-permute-start(f32[8192]{0:T(1024)S(1)} %bitcast.88), channel_id=1, source_target_pairs={{0,2},{2,4},{4,6},{6,8},{8,10},{10,12},{12,14},{14,0},{1,3},{3,5},... | collective-permute-start | bytes 98312 | tf_op jit(solution)/shard_map/ppermute | solution.py:46
  190.1 12.2 %collective-permute-start.8 = (f32[8192]{0:T(1024)S(1)}, f32[8192]{0:T(1024)S(1)}, u32[]{:S(2)}, u32[]{:S(2)}) collective-permute-start(f32[8192]{0:T(1024)S(1)} %bitcast.89), channel_id=1, source_target_pairs={{0,4},{2,6},{4,8},{6,10},{8,12},{10,14},{12,0},{14,2},{1,5},{3,7},... | collective-permute-start | bytes 98312 | tf_op jit(solution)/shard_map/ppermute | solution.py:46
  192.3 10.6 %collective-permute-start.9 = (f32[8192]{0:T(1024)S(1)}, f32[8192]{0:T(1024)S(1)}, u32[]{:S(2)}, u32[]{:S(2)}) collective-permute-start(f32[8192]{0:T(1024)S(1)} %bitcast.90), channel_id=1, source_target_pairs={{0,6},{2,8},{4,10},{6,12},{8,14},{10,0},{12,2},{14,4},{1,7},{3,9},... | collective-permute-start | bytes 98312 | tf_op jit(solution)/shard_map/ppermute | solution.py:46
  193.9 8.9 %collective-permute-start.10 = (f32[8192]{0:T(1024)S(1)}, f32[8192]{0:T(1024)S(1)}, u32[]{:S(2)}, u32[]{:S(2)}) collective-permute-start(f32[8192]{0:T(1024)S(1)} %bitcast.91), channel_id=1, source_target_pairs={{0,8},{2,10},{4,12},{6,14},{8,0},{10,2},{12,4},{14,6},{1,9},{3,11}... | collective-permute-start | bytes 98312 | tf_op jit(solution)/shard_map/ppermute | solution.py:46
  196.6 6.3 %collective-permute-start.11 = (f32[8192]{0:T(1024)S(1)}, f32[8192]{0:T(1024)S(1)}, u32[]{:S(2)}, u32[]{:S(2)}) collective-permute-start(f32[8192]{0:T(1024)S(1)} %bitcast.92), channel_id=1, source_target_pairs={{0,10},{2,12},{4,14},{6,0},{8,2},{10,4},{12,6},{14,8},{1,11},{3,13... | collective-permute-start | bytes 98312 | tf_op jit(solution)/shard_map/ppermute | solution.py:46
  199.7 4.8 %collective-permute-start.12 = (f32[8192]{0:T(1024)S(1)}, f32[8192]{0:T(1024)S(1)}, u32[]{:S(2)}, u32[]{:S(2)}) collective-permute-start(f32[8192]{0:T(1024)S(1)} %bitcast.93), channel_id=1, source_target_pairs={{0,12},{2,14},{4,0},{6,2},{8,4},{10,6},{12,8},{14,10},{1,13},{3,15... | collective-permute-start | bytes 98312 | tf_op jit(solution)/shard_map/ppermute | solution.py:46
  202.4 3.9 %collective-permute-start.13 = (f32[8192]{0:T(1024)S(1)}, f32[8192]{0:T(1024)S(1)}, u32[]{:S(2)}, u32[]{:S(2)}) collective-permute-start(f32[8192]{0:T(1024)S(1)} %bitcast.94), channel_id=1, source_target_pairs={{0,14},{2,0},{4,2},{6,4},{8,6},{10,8},{12,10},{14,12},{1,15},{3,1}... | collective-permute-start | bytes 98312 | tf_op jit(solution)/shard_map/ppermute | solution.py:46
  222.8 8.3 %collective-permute-start.16 = (f32[128,512]{0,1:T(8,128)S(1)}, f32[128,512]{0,1:T(8,128)S(1)}, u32[]{:S(2)}, u32[]{:S(2)}) collective-permute-start(f32[128,512]{0,1:T(8,128)S(1)} %get-tuple-element.14), channel_id=1, source_target_pairs={{0,1},{1,128},{128,129},{129,0},{2,3},{3,130},{130,131},{131,2},{4... | collective-permute-start | bytes 786440 | tf_op jit(solution)/shard_map/ppermute | solution.py:126
  223.4 8.6 %collective-permute-start.17 = (f32[128,512]{0,1:T(8,128)S(1)}, f32[128,512]{0,1:T(8,128)S(1)}, u32[]{:S(2)}, u32[]{:S(2)}) collective-permute-start(f32[128,512]{0,1:T(8,128)S(1)} %get-tuple-element.16), channel_id=1, source_target_pairs={{0,128},{1,129},{128,0},{129,1},{2,130},{3,131},{130,2},{131,3},{4... | collective-permute-start | bytes 786440 | tf_op jit(solution)/shard_map/ppermute | solution.py:126
  224.9 9.8 %collective-permute-start.18 = (f32[128,512]{0,1:T(8,128)S(1)}, f32[128,512]{0,1:T(8,128)S(1)}, u32[]{:S(2)}, u32[]{:S(2)}) collective-permute-start(f32[128,512]{0,1:T(8,128)S(1)} %get-tuple-element.15), channel_id=1, source_target_pairs={{0,129},{1,0},{128,1},{129,128},{2,131},{3,2},{130,3},{131,130},{4... | collective-permute-start | bytes 786440 | tf_op jit(solution)/shard_map/ppermute | solution.py:126
Sparse Core Ops, SparseCore 0:
  83.6 76.5 all-gather.1

commit v4 on v3

--- a/solution.py
+++ b/solution.py
@@ -42,12 +42,11 @@
 def tree_sum(value, axes):
     for axis in axes:
         size = lax.axis_size(axis)
-        me = lax.axis_index(axis)
-        parts = [value] + [lax.ppermute(value, axis, ring_pairs(size, k)) for k in range(1, size)]
-        ordered = jnp.take(jnp.stack(parts), (me - jnp.arange(size, dtype=jnp.int32)) % size, axis=0)
-        value = ordered[0]
-        for k in range(1, size):
-            value = value + ordered[k]
+        step = 1
+        while step < size:
+            pairs = [(i, i ^ step) for i in range(size)]
+            value = value + lax.ppermute(value, axis, pairs)
+            step *= 2
     return value
 
 

time: 243 us -> 236 us (0.971)
  starting transfers between devices: 41.5 us -> 33.3 us
  waiting for transfers between devices: 110 us -> 115 us
  local copies, waits for them, and re-layouts: 18 us -> 14.7 us
    ppermute x13 -> x8, starting transfers between devices: 22.6 us -> 13.5 us  [tree_sum(): value = value + lax.ppermute(value, axis, pairs)]
    ppermute x13 -> x8, waiting for transfers between devices: 8.66 us -> 13.7 us  [tree_sum(): value = value + lax.ppermute(value, axis, pairs)]
    gather x5 -> x0, local copies, waits for them, and re-layouts: 2.95 us -> none  [tree_sum(): jnp.take(jnp.stack(parts), (me - jnp.arange(size, dtype=jnp.int32)) % siz...]
  transfers between devices with their start and end apart: 23 -> 18, of which waited for: 14 -> 15; matrix products, arithmetic and copies ran while one was open for 2% -> 1% of each run, Pallas kernels for 0% -> 0%
where the time goes in v4:
time: 236 us; the launch traced here: 234 us
  waiting for transfers between devices  115 us (49%)
  starting transfers between devices  33.3 us (14%)
  matrix products  26.8 us (11%)
  blocking collectives  25.4 us (11%)
  local copies, waits for them, and re-layouts  14.7 us (6%)
  between operations  13.7 us (6%)
  other arithmetic  5.9 us (2%)
    all_gather x1, waiting for transfers between devices, shards(): row_block = lax.all_gather(neighbour, ROWS, axis=0, tiled=True)  65.4 us
    all_to_all x1, blocking collectives, fetch_rows(): lax.all_to_all(request, INNER, split_axis=0, concat_axis=0, tiled=True)  25.4 us
    dot_general x1, matrix products, column_terms(): lax.dot_general(weights, row_block, (((0,), (0,)), ((), ())), preferred_e...  15.1 us
    ppermute x8, waiting for transfers between devices, tree_sum(): value = value + lax.ppermute(value, axis, pairs)  13.7 us
    ppermute x8, starting transfers between devices, tree_sum(): value = value + lax.ppermute(value, axis, pairs)  13.5 us
    all_to_all x1, waiting for transfers between devices, fetch_rows(): lax.all_to_all(relayed, INNER, split_axis=0, concat_axis=0, tiled=True)  12.9 us
    dot_general x1, matrix products, block_exp(): jnp.einsum('rd,cd->rc', row_block, column_block, preferred_element_type=j...  11.7 us
    ppermute x3, waiting for transfers between devices, scatter_columns(): total = total + lax.ppermute(piece, axes, ring_pairs(size, k))  7.75 us
  transfers between devices with their start and end apart: 18, of which 15 were waited for; matrix products, arithmetic and copies ran while one was open for 1% of the time, Pallas kernels for 0%

profile of v4, /device:TPU:8, one launch (start us, length us, event | category | flops | bytes accessed | tf_op | source)
XLA Modules:
  0.0 234.2 jit_solution(553410106297389727)
XLA Ops:
  6.5 0.7 and_select_fusion.2
  7.2 0.7 fusion.33
  8.0 0.7 and_bitcast_fusion
  8.7 1.0 scatter_custom_fusion.1
  9.8 1.1 scatter_custom_fusion
  11.1 25.4 %all_to_all.24 = s32[64,4,2]{1,2,0:T(2,128)S(1)} all-to-all(s32[64,4,2]{1,2,0:T(2,128)S(1)} %copy.33), channel_id=1, replica_groups=mesh['xl'=2,'c'=2,'y'=4,'z'=8,'xh'=2] {'y','z','xh'}, dimensions={0} | all-to-all | bytes 4096 | tf_op jit(solution)/shard_map/all_to_all | solution.py:77
  37.5 1.4 scatter_custom_fusion.2
  38.9 0.7 all_to_all.16
  39.6 3.2 %all-to-all-start.1 = ((s32[4,1,64]{2,1,0:T(1,128)}), s32[4,1,64]{2,1,0:T(1,128)S(1)}, u32[]{:S(2)}, u32[]{:S(2)}) async-start(s32[4,1,64]{2,1,0:T(1,128)} %all_to_all.16), calls=%async_computation.1 | async-start | bytes 4096 | tf_op jit(solution)/shard_map/all_to_all | solution.py:91
  43.0 3.5 %all-to-all-done.1 = s32[4,1,64]{2,1,0:T(1,128)S(1)} async-done(((s32[4,1,64]{2,1,0:T(1,128)}), s32[4,1,64]{2,1,0:T(1,128)S(1)}, u32[]{:S(2)}, u32[]{:S(2)}) %all-to-all-start.1) | async-done | bytes 1056 | tf_op jit(solution)/shard_map/all_to_all | solution.py:91
  46.6 3.9 %gather_fusion = bf16[256,512]{1,0:T(8,128)(2,1)S(1)} fusion(bf16[4096,512]{1,0:T(8,128)(2,1)} %param.4, s32[1024]{0:T(1024)S(1)} %pad_clamp_fusion.3), kind=kCustom, calls=%fused_computation | custom fusion | bytes 525312 | tf_op jit(solution)/shard_map/jit(_take)/gather | solution.py:92
  50.6 0.8 select_select_fusion.1
  51.4 3.4 %all-to-all-start.2 = ((bf16[4,64,512]{2,1,0:T(8,128)(2,1)}), bf16[4,64,512]{2,1,0:T(8,128)(2,1)S(1)}, u32[]{:S(2)}, u32[]{:S(2)}) async-start(bf16[4,64,512]{2,1,0:T(8,128)(2,1)} %select_select_fusion.1), calls=%async_computation.2 | async-start | bytes 524288 | tf_op jit(solution)/shard_map/all_to_all | solution.py:94
  55.1 5.7 %all-to-all-done.2 = bf16[4,64,512]{2,1,0:T(8,128)(2,1)S(1)} async-done(((bf16[4,64,512]{2,1,0:T(8,128)(2,1)}), bf16[4,64,512]{2,1,0:T(8,128)(2,1)S(1)}, u32[]{:S(2)}, u32[]{:S(2)}) %all-to-all-start.2) | async-done | bytes 262176 | tf_op jit(solution)/shard_map/all_to_all | solution.py:94
  60.8 1.2 gather_fusion.1
  62.0 1.0 select_select_fusion
  63.1 5.5 %all-to-all-start.3 = ((bf16[64,4,512]{2,1,0:T(4,128)(2,1)}), bf16[64,4,512]{2,1,0:T(4,128)(2,1)S(1)}, u32[]{:S(2)}, u32[]{:S(2)}) async-start(bf16[64,4,512]{2,1,0:T(4,128)(2,1)} %select_select_fusion), calls=%async_computation.3 | async-start | bytes 524288 | tf_op jit(solution)/shard_map/all_to_all | solution.py:99
  68.6 12.9 %all-to-all-done.3 = bf16[64,4,512]{2,1,0:T(4,128)(2,1)S(1)} async-done(((bf16[64,4,512]{2,1,0:T(4,128)(2,1)}), bf16[64,4,512]{2,1,0:T(4,128)(2,1)S(1)}, u32[]{:S(2)}, u32[]{:S(2)}) %all-to-all-start.3) | async-done | bytes 262176 | tf_op jit(solution)/shard_map/all_to_all | solution.py:99
  81.6 0.8 gather_fusion.2
  82.7 0.8 fusion.9
  83.5 1.0 copy.42
  84.6 1.0 collective-permute-start
  85.7 0.7 collective-permute-start.1
  86.4 1.6 collective-permute-start.2
  88.2 3.5 %collective-permute-done = bf16[128,512]{0,1:T(8,128)(2,1)S(1)} collective-permute-done((bf16[128,512]{0,1:T(8,128)(2,1)S(1)}, bf16[128,512]{0,1:T(8,128)(2,1)S(1)}, u32[]{:S(2)}, u32[]{:S(2)}) %collective-permute-start) | collective-permute-done | bytes 131104 | tf_op jit(solution)/shard_map/ppermute | solution.py:112
  91.7 2.1 collective-permute-done.2
  93.8 0.6 gather_fusion.3
  94.9 65.4 %all-gather.2.cloned.1.call-done = bf16[8192,512]{1,0:T(8,128)(2,1)} async-done(((bf16[128,512]{1,0:T(8,128)(2,1)}), bf16[8192,512]{1,0:T(8,128)(2,1)}) %all-gather.2.cloned.1.call-update) | async-done | bytes 8388624 | tf_op jit(solution)/shard_map/all_gather | solution.py:140
  160.2 11.7 %fusion.1 = (f32[8192]{0:T(1024)S(1)}, f32[512]{0:T(512)S(1)}, f32[8192,512]{1,0:T(8,128)}) fusion(bf16[8192,512]{1,0:T(8,128)(2,1)} %all-gather.2.cloned.1.call-done, bf16[512,512]{1,0:T(8,128)(2,1)S(1)} %bitcast_select_fusion), kind=kOutput, calls=%fused_computation.10 | convolution fusion | flops 4307541504 | bytes 25724928 | tf_op jit(solution)/shard_map/rd,cd->rc/dot_general | solution.py:20
  172.2 1.0 collective-permute-done.3
  173.1 1.8 collective-permute-start.4
  175.0 2.1 collective-permute-done.4
  177.1 1.5 collective-permute-start.5
  178.5 3.9 %collective-permute-done.5 = f32[8192]{0:T(1024)S(1)} collective-permute-done((f32[8192]{0:T(1024)S(1)}, f32[8192]{0:T(1024)S(1)}, u32[]{:S(2)}, u32[]{:S(2)}) %collective-permute-start.5) | collective-permute-done | bytes 32800 | tf_op jit(solution)/shard_map/ppermute | solution.py:48
  182.5 1.2 collective-permute-start.6
  183.7 2.7 %collective-permute-done.6 = f32[8192]{0:T(1024)S(1)} collective-permute-done((f32[8192]{0:T(1024)S(1)}, f32[8192]{0:T(1024)S(1)}, u32[]{:S(2)}, u32[]{:S(2)}) %collective-permute-start.6) | collective-permute-done | bytes 32800 | tf_op jit(solution)/shard_map/ppermute | solution.py:48
  186.4 1.3 collective-permute-start.7
  187.8 1.5 collective-permute-start.9
  189.3 1.9 collective-permute-done.7
  191.2 2.8 %collective-permute-start.8 = (f32[8192]{0:T(1024)S(1)}, f32[8192]{0:T(1024)S(1)}, u32[]{:S(2)}, u32[]{:S(2)}) collective-permute-start(f32[8192]{0:T(1024)S(1)} %add.238), channel_id=1, source_target_pairs={{0,8},{2,10},{4,12},{6,14},{8,0},{10,2},{12,4},{14,6},{1,9},{3,11}... | collective-permute-start | bytes 98312 | tf_op jit(solution)/shard_map/ppermute | solution.py:48
  194.1 3.1 %collective-permute-start.10 = (f32[512]{0:T(512)S(1)}, f32[512]{0:T(512)S(1)}, u32[]{:S(2)}, u32[]{:S(2)}) collective-permute-start(f32[512]{0:T(512)S(1)} %add.240), channel_id=1, source_target_pairs={{0,1},{1,0},{2,3},{3,2},{4,5},{5,4},{6,7},{7,6},{8,9},{9,8},{10,11... | collective-permute-start | bytes 6152 | tf_op jit(solution)/shard_map/ppermute | solution.py:48
  197.1 2.1 collective-permute-done.10
  199.3 15.1 %fusion.2 = f32[512,512]{0,1:T(8,128)S(1)} fusion(bf16[8192,512]{1,0:T(8,128)(2,1)} %all-gather.2.cloned.1.call-done, f32[8192,512]{1,0:T(8,128)} %get-tuple-element.26, s32[512]{0:T(512)S(1)} %iota_subtract_fusion.1, f32[512]{0:T(512)S(1)} %add.241, f32[8192]{0:T(1024)S(1)} %add.239, s32[8192]{0:T(1024)S(1)} %iota_subtract_fusion, ...), kind=kOutput, calls=%fused_computation.11 | convolution fusion | flops 4341104640 | bytes 26300416 | tf_op jit(solution)/shard_map/dot_general | solution.py:37
  214.5 3.0 %collective-permute-start.11 = (f32[128,512]{0,1:T(8,128)S(1)}, f32[128,512]{0,1:T(8,128)S(1)}, u32[]{:S(2)}, u32[]{:S(2)}) collective-permute-start(f32[128,512]{0,1:T(8,128)S(1)} %get-tuple-element.13), channel_id=1, source_target_pairs={{0,1},{1,128},{128,129},{129,0},{2,3},{3,130},{130,131},{131,2},{4... | collective-permute-start | bytes 786440 | tf_op jit(solution)/shard_map/ppermute | solution.py:125
  218.6 3.7 %collective-permute-done.11 = f32[128,512]{0,1:T(8,128)S(1)} collective-permute-done((f32[128,512]{0,1:T(8,128)S(1)}, f32[128,512]{0,1:T(8,128)S(1)}, u32[]{:S(2)}, u32[]{:S(2)}) %collective-permute-start.11) | collective-permute-done | bytes 262176 | tf_op jit(solution)/shard_map/ppermute | solution.py:125
  222.3 2.9 %collective-permute-done.12 = f32[128,512]{0,1:T(8,128)S(1)} collective-permute-done((f32[128,512]{0,1:T(8,128)S(1)}, f32[128,512]{0,1:T(8,128)S(1)}, u32[]{:S(2)}, u32[]{:S(2)}) %collective-permute-start.12) | collective-permute-done | bytes 262176 | tf_op jit(solution)/shard_map/ppermute | solution.py:125
  225.3 1.1 collective-permute-done.13
  226.6 0.8 copy.44
  (65 shorter events, 4.8 us)
Async XLA Ops:
  39.6 6.9 %all-to-all-start.1 = ((s32[4,1,64]{2,1,0:T(1,128)}), s32[4,1,64]{2,1,0:T(1,128)S(1)}, u32[]{:S(2)}, u32[]{:S(2)}) async-start(s32[4,1,64]{2,1,0:T(1,128)} %all_to_all.16), calls=%async_computation.1 | async-start | bytes 4096 | tf_op jit(solution)/shard_map/all_to_all | solution.py:91
  51.4 9.4 %all-to-all-start.2 = ((bf16[4,64,512]{2,1,0:T(8,128)(2,1)}), bf16[4,64,512]{2,1,0:T(8,128)(2,1)S(1)}, u32[]{:S(2)}, u32[]{:S(2)}) async-start(bf16[4,64,512]{2,1,0:T(8,128)(2,1)} %select_select_fusion.1), calls=%async_computation.2 | async-start | bytes 524288 | tf_op jit(solution)/shard_map/all_to_all | solution.py:94
  63.1 18.5 %all-to-all-start.3 = ((bf16[64,4,512]{2,1,0:T(4,128)(2,1)}), bf16[64,4,512]{2,1,0:T(4,128)(2,1)S(1)}, u32[]{:S(2)}, u32[]{:S(2)}) async-start(bf16[64,4,512]{2,1,0:T(4,128)(2,1)} %select_select_fusion), calls=%async_computation.3 | async-start | bytes 524288 | tf_op jit(solution)/shard_map/all_to_all | solution.py:99
  68.6 91.7 %all-gather.2.cloned.1.call-start = ((), (), s32[]{:S(2)}) async-start(), calls=%async_computation.4 | async-start | bytes 8519680 | tf_op jit(solution)/shard_map/all_gather | solution.py:140
  84.6 7.0 %collective-permute-start = (bf16[128,512]{0,1:T(8,128)(2,1)S(1)}, bf16[128,512]{0,1:T(8,128)(2,1)S(1)}, u32[]{:S(2)}, u32[]{:S(2)}) collective-permute-start(bf16[128,512]{0,1:T(8,128)(2,1)S(1)} %fusion.4), channel_id=1, source_target_pairs={{0,1},{1,128},{128,129},{129,0},{2,3},{3,130},{130,131},{131,2},{4... | collective-permute-start | bytes 393224 | tf_op jit(solution)/shard_map/ppermute | solution.py:112
  85.7 6.0 %collective-permute-start.1 = (bf16[128,512]{0,1:T(8,128)(2,1)S(1)}, bf16[128,512]{0,1:T(8,128)(2,1)S(1)}, u32[]{:S(2)}, u32[]{:S(2)}) collective-permute-start(bf16[128,512]{0,1:T(8,128)(2,1)S(1)} %fusion.4), channel_id=1, source_target_pairs={{0,128},{1,129},{128,0},{129,1},{2,130},{3,131},{130,2},{131,3},{4... | collective-permute-start | bytes 393224 | tf_op jit(solution)/shard_map/ppermute | solution.py:112
  86.4 7.3 %collective-permute-start.2 = (bf16[128,512]{0,1:T(8,128)(2,1)S(1)}, bf16[128,512]{0,1:T(8,128)(2,1)S(1)}, u32[]{:S(2)}, u32[]{:S(2)}) collective-permute-start(bf16[128,512]{0,1:T(8,128)(2,1)S(1)} %fusion.4), channel_id=1, source_target_pairs={{0,129},{1,0},{128,1},{129,128},{2,131},{3,2},{130,3},{131,130},{4... | collective-permute-start | bytes 393224 | tf_op jit(solution)/shard_map/ppermute | solution.py:112
  171.9 1.2 collective-permute-start.3
  173.1 3.9 %collective-permute-start.4 = (f32[8192]{0:T(1024)S(1)}, f32[8192]{0:T(1024)S(1)}, u32[]{:S(2)}, u32[]{:S(2)}) collective-permute-start(f32[8192]{0:T(1024)S(1)} %add.234), channel_id=1, source_target_pairs={{0,16},{16,0},{32,48},{48,32},{1,17},{17,1},{33,49},{49,33},{2,18}... | collective-permute-start | bytes 98312 | tf_op jit(solution)/shard_map/ppermute | solution.py:48
  177.1 5.4 %collective-permute-start.5 = (f32[8192]{0:T(1024)S(1)}, f32[8192]{0:T(1024)S(1)}, u32[]{:S(2)}, u32[]{:S(2)}) collective-permute-start(f32[8192]{0:T(1024)S(1)} %add.235), channel_id=1, source_target_pairs={{0,32},{16,48},{32,0},{48,16},{1,33},{17,49},{33,1},{49,17},{2,34}... | collective-permute-start | bytes 98312 | tf_op jit(solution)/shard_map/ppermute | solution.py:48
  182.5 3.9 %collective-permute-start.6 = (f32[8192]{0:T(1024)S(1)}, f32[8192]{0:T(1024)S(1)}, u32[]{:S(2)}, u32[]{:S(2)}) collective-permute-start(f32[8192]{0:T(1024)S(1)} %add.236), channel_id=1, source_target_pairs={{0,2},{2,0},{4,6},{6,4},{8,10},{10,8},{12,14},{14,12},{1,3},{3,1},... | collective-permute-start | bytes 98312 | tf_op jit(solution)/shard_map/ppermute | solution.py:48
  186.4 4.8 %collective-permute-start.7 = (f32[8192]{0:T(1024)S(1)}, f32[8192]{0:T(1024)S(1)}, u32[]{:S(2)}, u32[]{:S(2)}) collective-permute-start(f32[8192]{0:T(1024)S(1)} %add.237), channel_id=1, source_target_pairs={{0,4},{2,6},{4,0},{6,2},{8,12},{10,14},{12,8},{14,10},{1,5},{3,7},... | collective-permute-start | bytes 98312 | tf_op jit(solution)/shard_map/ppermute | solution.py:48
  187.8 6.3 %collective-permute-start.9 = (f32[512]{0:T(512)S(1)}, f32[512]{0:T(512)S(1)}, u32[]{:S(2)}, u32[]{:S(2)}) collective-permute-start(f32[512]{0:T(512)S(1)} %get-tuple-element.6), channel_id=1, source_target_pairs={{0,128},{128,0},{1,129},{129,1},{2,130},{130,2},{3,131},{131,3},{4... | collective-permute-start | bytes 6152 | tf_op jit(solution)/shard_map/ppermute | solution.py:48
  191.2 8.0 %collective-permute-start.8 = (f32[8192]{0:T(1024)S(1)}, f32[8192]{0:T(1024)S(1)}, u32[]{:S(2)}, u32[]{:S(2)}) collective-permute-start(f32[8192]{0:T(1024)S(1)} %add.238), channel_id=1, source_target_pairs={{0,8},{2,10},{4,12},{6,14},{8,0},{10,2},{12,4},{14,6},{1,9},{3,11}... | collective-permute-start | bytes 98312 | tf_op jit(solution)/shard_map/ppermute | solution.py:48
  194.1 5.2 %collective-permute-start.10 = (f32[512]{0:T(512)S(1)}, f32[512]{0:T(512)S(1)}, u32[]{:S(2)}, u32[]{:S(2)}) collective-permute-start(f32[512]{0:T(512)S(1)} %add.240), channel_id=1, source_target_pairs={{0,1},{1,0},{2,3},{3,2},{4,5},{5,4},{6,7},{7,6},{8,9},{9,8},{10,11... | collective-permute-start | bytes 6152 | tf_op jit(solution)/shard_map/ppermute | solution.py:48
  214.5 7.9 %collective-permute-start.11 = (f32[128,512]{0,1:T(8,128)S(1)}, f32[128,512]{0,1:T(8,128)S(1)}, u32[]{:S(2)}, u32[]{:S(2)}) collective-permute-start(f32[128,512]{0,1:T(8,128)S(1)} %get-tuple-element.13), channel_id=1, source_target_pairs={{0,1},{1,128},{128,129},{129,0},{2,3},{3,130},{130,131},{131,2},{4... | collective-permute-start | bytes 786440 | tf_op jit(solution)/shard_map/ppermute | solution.py:125
  217.5 7.8 %collective-permute-start.12 = (f32[128,512]{0,1:T(8,128)S(1)}, f32[128,512]{0,1:T(8,128)S(1)}, u32[]{:S(2)}, u32[]{:S(2)}) collective-permute-start(f32[128,512]{0,1:T(8,128)S(1)} %get-tuple-element.15), channel_id=1, source_target_pairs={{0,128},{1,129},{128,0},{129,1},{2,130},{3,131},{130,2},{131,3},{4... | collective-permute-start | bytes 786440 | tf_op jit(solution)/shard_map/ppermute | solution.py:125
  218.1 8.3 %collective-permute-start.13 = (f32[128,512]{0,1:T(8,128)S(1)}, f32[128,512]{0,1:T(8,128)S(1)}, u32[]{:S(2)}, u32[]{:S(2)}) collective-permute-start(f32[128,512]{0,1:T(8,128)S(1)} %get-tuple-element.14), channel_id=1, source_target_pairs={{0,129},{1,0},{128,1},{129,128},{2,131},{3,2},{130,3},{131,130},{4... | collective-permute-start | bytes 786440 | tf_op jit(solution)/shard_map/ppermute | solution.py:125
Sparse Core Ops, SparseCore 0:
  83.6 76.5 all-gather.1

commit v5 on v4

--- a/solution.py
+++ b/solution.py
@@ -28,9 +28,9 @@
     diagonal = ((row_offset == column_offset) & (row_offset >= 0) & (row_offset < rows_dev)).astype(
         jnp.float32
     )
-    return (
-        0.5 * (exponent / row_total[:, None] + exponent / column_total[None, :]) - diagonal
-    ).astype(jnp.bfloat16)
+    row_scale = 0.5 / row_total
+    column_scale = 0.5 / column_total
+    return (exponent * (row_scale[:, None] + column_scale[None, :]) - diagonal).astype(jnp.bfloat16)
 
 
 def column_terms(weights, row_block):

time: 236 us -> 235 us (level)
  no operation moved by 1% of the time
where the time goes in v5:
time: 235 us; the launch traced here: 233 us
  waiting for transfers between devices  114 us (49%)
  starting transfers between devices  33.3 us (14%)
  matrix products  25.6 us (11%)
  blocking collectives  25.4 us (11%)
  local copies, waits for them, and re-layouts  14.7 us (6%)
  between operations  13.7 us (6%)
  other arithmetic  5.91 us (3%)
    all_gather x1, waiting for transfers between devices, shards(): row_block = lax.all_gather(neighbour, ROWS, axis=0, tiled=True)  65.4 us
    all_to_all x1, blocking collectives, fetch_rows(): lax.all_to_all(request, INNER, split_axis=0, concat_axis=0, tiled=True)  25.4 us
    dot_general x1, matrix products, column_terms(): lax.dot_general(weights, row_block, (((0,), (0,)), ((), ())), preferred_e...  13.9 us
    ppermute x8, starting transfers between devices, tree_sum(): value = value + lax.ppermute(value, axis, pairs)  13.6 us
    ppermute x8, waiting for transfers between devices, tree_sum(): value = value + lax.ppermute(value, axis, pairs)  13.5 us
    all_to_all x1, waiting for transfers between devices, fetch_rows(): lax.all_to_all(relayed, INNER, split_axis=0, concat_axis=0, tiled=True)  12.9 us
    dot_general x1, matrix products, block_exp(): jnp.einsum('rd,cd->rc', row_block, column_block, preferred_element_type=j...  11.7 us
    ppermute x3, waiting for transfers between devices, scatter_columns(): total = total + lax.ppermute(piece, axes, ring_pairs(size, k))  7.75 us
  transfers between devices with their start and end apart: 18, of which 15 were waited for; matrix products, arithmetic and copies ran while one was open for 1% of the time, Pallas kernels for 0%

profile of v5, /device:TPU:8, one launch (start us, length us, event | category | flops | bytes accessed | tf_op | source)
XLA Modules:
  0.0 232.9 jit_solution(9370098182705231778)
XLA Ops:
  6.5 0.7 and_select_fusion.2
  7.2 0.7 fusion.32
  8.0 0.7 and_bitcast_fusion
  8.7 1.0 scatter_custom_fusion.1
  9.8 1.1 scatter_custom_fusion
  11.1 25.4 %all_to_all.24 = s32[64,4,2]{1,2,0:T(2,128)S(1)} all-to-all(s32[64,4,2]{1,2,0:T(2,128)S(1)} %copy.33), channel_id=1, replica_groups=mesh['xl'=2,'c'=2,'y'=4,'z'=8,'xh'=2] {'y','z','xh'}, dimensions={0} | all-to-all | bytes 4096 | tf_op jit(solution)/shard_map/all_to_all | solution.py:77
  37.5 1.4 scatter_custom_fusion.2
  38.9 0.7 all_to_all.16
  39.6 3.2 %all-to-all-start.1 = ((s32[4,1,64]{2,1,0:T(1,128)}), s32[4,1,64]{2,1,0:T(1,128)S(1)}, u32[]{:S(2)}, u32[]{:S(2)}) async-start(s32[4,1,64]{2,1,0:T(1,128)} %all_to_all.16), calls=%async_computation.1 | async-start | bytes 4096 | tf_op jit(solution)/shard_map/all_to_all | solution.py:91
  43.0 3.5 %all-to-all-done.1 = s32[4,1,64]{2,1,0:T(1,128)S(1)} async-done(((s32[4,1,64]{2,1,0:T(1,128)}), s32[4,1,64]{2,1,0:T(1,128)S(1)}, u32[]{:S(2)}, u32[]{:S(2)}) %all-to-all-start.1) | async-done | bytes 1056 | tf_op jit(solution)/shard_map/all_to_all | solution.py:91
  46.6 3.9 %gather_fusion = bf16[256,512]{1,0:T(8,128)(2,1)S(1)} fusion(bf16[4096,512]{1,0:T(8,128)(2,1)} %param.4, s32[1024]{0:T(1024)S(1)} %pad_clamp_fusion.3), kind=kCustom, calls=%fused_computation | custom fusion | bytes 525312 | tf_op jit(solution)/shard_map/jit(_take)/gather | solution.py:92
  50.6 0.8 select_select_fusion.1
  51.4 3.4 %all-to-all-start.2 = ((bf16[4,64,512]{2,1,0:T(8,128)(2,1)}), bf16[4,64,512]{2,1,0:T(8,128)(2,1)S(1)}, u32[]{:S(2)}, u32[]{:S(2)}) async-start(bf16[4,64,512]{2,1,0:T(8,128)(2,1)} %select_select_fusion.1), calls=%async_computation.2 | async-start | bytes 524288 | tf_op jit(solution)/shard_map/all_to_all | solution.py:94
  55.1 5.7 %all-to-all-done.2 = bf16[4,64,512]{2,1,0:T(8,128)(2,1)S(1)} async-done(((bf16[4,64,512]{2,1,0:T(8,128)(2,1)}), bf16[4,64,512]{2,1,0:T(8,128)(2,1)S(1)}, u32[]{:S(2)}, u32[]{:S(2)}) %all-to-all-start.2) | async-done | bytes 262176 | tf_op jit(solution)/shard_map/all_to_all | solution.py:94
  60.8 1.2 gather_fusion.1
  62.0 1.0 select_select_fusion
  63.1 5.5 %all-to-all-start.3 = ((bf16[64,4,512]{2,1,0:T(4,128)(2,1)}), bf16[64,4,512]{2,1,0:T(4,128)(2,1)S(1)}, u32[]{:S(2)}, u32[]{:S(2)}) async-start(bf16[64,4,512]{2,1,0:T(4,128)(2,1)} %select_select_fusion), calls=%async_computation.3 | async-start | bytes 524288 | tf_op jit(solution)/shard_map/all_to_all | solution.py:99
  68.6 12.9 %all-to-all-done.3 = bf16[64,4,512]{2,1,0:T(4,128)(2,1)S(1)} async-done(((bf16[64,4,512]{2,1,0:T(4,128)(2,1)}), bf16[64,4,512]{2,1,0:T(4,128)(2,1)S(1)}, u32[]{:S(2)}, u32[]{:S(2)}) %all-to-all-start.3) | async-done | bytes 262176 | tf_op jit(solution)/shard_map/all_to_all | solution.py:99
  81.6 0.8 gather_fusion.2
  82.7 0.8 fusion.9
  83.5 1.0 copy.42
  84.6 1.0 collective-permute-start
  85.7 0.7 collective-permute-start.1
  86.4 1.6 collective-permute-start.2
  88.2 3.5 %collective-permute-done = bf16[128,512]{0,1:T(8,128)(2,1)S(1)} collective-permute-done((bf16[128,512]{0,1:T(8,128)(2,1)S(1)}, bf16[128,512]{0,1:T(8,128)(2,1)S(1)}, u32[]{:S(2)}, u32[]{:S(2)}) %collective-permute-start) | collective-permute-done | bytes 131104 | tf_op jit(solution)/shard_map/ppermute | solution.py:112
  91.7 2.1 collective-permute-done.2
  93.8 0.6 gather_fusion.3
  94.9 65.4 %all-gather.2.cloned.1.call-done = bf16[8192,512]{1,0:T(8,128)(2,1)} async-done(((bf16[128,512]{1,0:T(8,128)(2,1)}), bf16[8192,512]{1,0:T(8,128)(2,1)}) %all-gather.2.cloned.1.call-update) | async-done | bytes 8388624 | tf_op jit(solution)/shard_map/all_gather | solution.py:140
  160.2 11.7 %fusion.1 = (f32[8192]{0:T(1024)S(1)}, f32[512]{0:T(512)S(1)}, f32[8192,512]{1,0:T(8,128)}) fusion(bf16[8192,512]{1,0:T(8,128)(2,1)} %all-gather.2.cloned.1.call-done, bf16[512,512]{1,0:T(8,128)(2,1)S(1)} %bitcast_select_fusion), kind=kOutput, calls=%fused_computation.10 | convolution fusion | flops 4307541504 | bytes 25724928 | tf_op jit(solution)/shard_map/rd,cd->rc/dot_general | solution.py:20
  172.2 1.0 collective-permute-done.3
  173.1 1.8 collective-permute-start.4
  175.0 2.1 collective-permute-done.4
  177.1 1.5 collective-permute-start.5
  178.6 3.9 %collective-permute-done.5 = f32[8192]{0:T(1024)S(1)} collective-permute-done((f32[8192]{0:T(1024)S(1)}, f32[8192]{0:T(1024)S(1)}, u32[]{:S(2)}, u32[]{:S(2)}) %collective-permute-start.5) | collective-permute-done | bytes 32800 | tf_op jit(solution)/shard_map/ppermute | solution.py:48
  182.5 1.2 collective-permute-start.6
  183.8 1.6 collective-permute-start.9
  185.3 1.1 collective-permute-done.6
  186.4 1.3 collective-permute-start.7
  187.7 3.1 %collective-permute-start.10 = (f32[512]{0:T(512)S(1)}, f32[512]{0:T(512)S(1)}, u32[]{:S(2)}, u32[]{:S(2)}) collective-permute-start(f32[512]{0:T(512)S(1)} %add.251), channel_id=1, source_target_pairs={{0,1},{1,0},{2,3},{3,2},{4,5},{5,4},{6,7},{7,6},{8,9},{9,8},{10,11... | collective-permute-start | bytes 6152 | tf_op jit(solution)/shard_map/ppermute | solution.py:48
  191.2 2.8 %collective-permute-start.8 = (f32[8192]{0:T(1024)S(1)}, f32[8192]{0:T(1024)S(1)}, u32[]{:S(2)}, u32[]{:S(2)}) collective-permute-start(f32[8192]{0:T(1024)S(1)} %add.248), channel_id=1, source_target_pairs={{0,8},{2,10},{4,12},{6,14},{8,0},{10,2},{12,4},{14,6},{1,9},{3,11}... | collective-permute-start | bytes 98312 | tf_op jit(solution)/shard_map/ppermute | solution.py:48
  194.1 5.0 %collective-permute-done.8 = f32[8192]{0:T(1024)S(1)} collective-permute-done((f32[8192]{0:T(1024)S(1)}, f32[8192]{0:T(1024)S(1)}, u32[]{:S(2)}, u32[]{:S(2)}) %collective-permute-start.8) | collective-permute-done | bytes 32800 | tf_op jit(solution)/shard_map/ppermute | solution.py:48
  199.1 13.9 %fusion.2 = f32[512,512]{0,1:T(8,128)S(1)} fusion(bf16[8192,512]{1,0:T(8,128)(2,1)} %all-gather.2.cloned.1.call-done, f32[8192,512]{1,0:T(8,128)} %get-tuple-element.26, s32[512]{0:T(512)S(1)} %iota_subtract_fusion.1, f32[512]{0:T(512)S(1)} %add_divide_fusion.1, f32[8192]{0:T(1024)S(1)} %add_divide_fusion, s32[8192]{0:T(1024)S(1)} %iota_subtract_fusion, ...), kind=kOutput, calls=%fused_computation.11 | convolution fusion | flops 4332716032 | bytes 26300416 | tf_op jit(solution)/shard_map/dot_general | solution.py:37
  213.1 3.1 %collective-permute-start.11 = (f32[128,512]{0,1:T(8,128)S(1)}, f32[128,512]{0,1:T(8,128)S(1)}, u32[]{:S(2)}, u32[]{:S(2)}) collective-permute-start(f32[128,512]{0,1:T(8,128)S(1)} %get-tuple-element.13), channel_id=1, source_target_pairs={{0,1},{1,128},{128,129},{129,0},{2,3},{3,130},{130,131},{131,2},{4... | collective-permute-start | bytes 786440 | tf_op jit(solution)/shard_map/ppermute | solution.py:125
  216.2 0.6 collective-permute-start.12
  217.3 4.4 %collective-permute-done.11 = f32[128,512]{0,1:T(8,128)S(1)} collective-permute-done((f32[128,512]{0,1:T(8,128)S(1)}, f32[128,512]{0,1:T(8,128)S(1)}, u32[]{:S(2)}, u32[]{:S(2)}) %collective-permute-start.11) | collective-permute-done | bytes 262176 | tf_op jit(solution)/shard_map/ppermute | solution.py:125
  221.7 2.2 collective-permute-done.12
  223.9 1.1 collective-permute-done.13
  225.2 0.8 copy.44
  (65 shorter events, 4.6 us)
Async XLA Ops:
  39.6 6.9 %all-to-all-start.1 = ((s32[4,1,64]{2,1,0:T(1,128)}), s32[4,1,64]{2,1,0:T(1,128)S(1)}, u32[]{:S(2)}, u32[]{:S(2)}) async-start(s32[4,1,64]{2,1,0:T(1,128)} %all_to_all.16), calls=%async_computation.1 | async-start | bytes 4096 | tf_op jit(solution)/shard_map/all_to_all | solution.py:91
  51.4 9.4 %all-to-all-start.2 = ((bf16[4,64,512]{2,1,0:T(8,128)(2,1)}), bf16[4,64,512]{2,1,0:T(8,128)(2,1)S(1)}, u32[]{:S(2)}, u32[]{:S(2)}) async-start(bf16[4,64,512]{2,1,0:T(8,128)(2,1)} %select_select_fusion.1), calls=%async_computation.2 | async-start | bytes 524288 | tf_op jit(solution)/shard_map/all_to_all | solution.py:94
  63.1 18.5 %all-to-all-start.3 = ((bf16[64,4,512]{2,1,0:T(4,128)(2,1)}), bf16[64,4,512]{2,1,0:T(4,128)(2,1)S(1)}, u32[]{:S(2)}, u32[]{:S(2)}) async-start(bf16[64,4,512]{2,1,0:T(4,128)(2,1)} %select_select_fusion), calls=%async_computation.3 | async-start | bytes 524288 | tf_op jit(solution)/shard_map/all_to_all | solution.py:99
  68.6 91.7 %all-gather.2.cloned.1.call-start = ((), (), s32[]{:S(2)}) async-start(), calls=%async_computation.4 | async-start | bytes 8519680 | tf_op jit(solution)/shard_map/all_gather | solution.py:140
  84.6 7.0 %collective-permute-start = (bf16[128,512]{0,1:T(8,128)(2,1)S(1)}, bf16[128,512]{0,1:T(8,128)(2,1)S(1)}, u32[]{:S(2)}, u32[]{:S(2)}) collective-permute-start(bf16[128,512]{0,1:T(8,128)(2,1)S(1)} %fusion.4), channel_id=1, source_target_pairs={{0,1},{1,128},{128,129},{129,0},{2,3},{3,130},{130,131},{131,2},{4... | collective-permute-start | bytes 393224 | tf_op jit(solution)/shard_map/ppermute | solution.py:112
  85.7 6.0 %collective-permute-start.1 = (bf16[128,512]{0,1:T(8,128)(2,1)S(1)}, bf16[128,512]{0,1:T(8,128)(2,1)S(1)}, u32[]{:S(2)}, u32[]{:S(2)}) collective-permute-start(bf16[128,512]{0,1:T(8,128)(2,1)S(1)} %fusion.4), channel_id=1, source_target_pairs={{0,128},{1,129},{128,0},{129,1},{2,130},{3,131},{130,2},{131,3},{4... | collective-permute-start | bytes 393224 | tf_op jit(solution)/shard_map/ppermute | solution.py:112
  86.4 7.3 %collective-permute-start.2 = (bf16[128,512]{0,1:T(8,128)(2,1)S(1)}, bf16[128,512]{0,1:T(8,128)(2,1)S(1)}, u32[]{:S(2)}, u32[]{:S(2)}) collective-permute-start(bf16[128,512]{0,1:T(8,128)(2,1)S(1)} %fusion.4), channel_id=1, source_target_pairs={{0,129},{1,0},{128,1},{129,128},{2,131},{3,2},{130,3},{131,130},{4... | collective-permute-start | bytes 393224 | tf_op jit(solution)/shard_map/ppermute | solution.py:112
  171.9 1.2 collective-permute-start.3
  173.1 3.9 %collective-permute-start.4 = (f32[8192]{0:T(1024)S(1)}, f32[8192]{0:T(1024)S(1)}, u32[]{:S(2)}, u32[]{:S(2)}) collective-permute-start(f32[8192]{0:T(1024)S(1)} %add.244), channel_id=1, source_target_pairs={{0,16},{16,0},{32,48},{48,32},{1,17},{17,1},{33,49},{49,33},{2,18}... | collective-permute-start | bytes 98312 | tf_op jit(solution)/shard_map/ppermute | solution.py:48
  177.1 5.4 %collective-permute-start.5 = (f32[8192]{0:T(1024)S(1)}, f32[8192]{0:T(1024)S(1)}, u32[]{:S(2)}, u32[]{:S(2)}) collective-permute-start(f32[8192]{0:T(1024)S(1)} %add.245), channel_id=1, source_target_pairs={{0,32},{16,48},{32,0},{48,16},{1,33},{17,49},{33,1},{49,17},{2,34}... | collective-permute-start | bytes 98312 | tf_op jit(solution)/shard_map/ppermute | solution.py:48
  182.5 3.9 %collective-permute-start.6 = (f32[8192]{0:T(1024)S(1)}, f32[8192]{0:T(1024)S(1)}, u32[]{:S(2)}, u32[]{:S(2)}) collective-permute-start(f32[8192]{0:T(1024)S(1)} %add.246), channel_id=1, source_target_pairs={{0,2},{2,0},{4,6},{6,4},{8,10},{10,8},{12,14},{14,12},{1,3},{3,1},... | collective-permute-start | bytes 98312 | tf_op jit(solution)/shard_map/ppermute | solution.py:48
  183.8 4.0 %collective-permute-start.9 = (f32[512]{0:T(512)S(1)}, f32[512]{0:T(512)S(1)}, u32[]{:S(2)}, u32[]{:S(2)}) collective-permute-start(f32[512]{0:T(512)S(1)} %get-tuple-element.6), channel_id=1, source_target_pairs={{0,128},{128,0},{1,129},{129,1},{2,130},{130,2},{3,131},{131,3},{4... | collective-permute-start | bytes 6152 | tf_op jit(solution)/shard_map/ppermute | solution.py:48
  186.4 4.8 %collective-permute-start.7 = (f32[8192]{0:T(1024)S(1)}, f32[8192]{0:T(1024)S(1)}, u32[]{:S(2)}, u32[]{:S(2)}) collective-permute-start(f32[8192]{0:T(1024)S(1)} %add.247), channel_id=1, source_target_pairs={{0,4},{2,6},{4,0},{6,2},{8,12},{10,14},{12,8},{14,10},{1,5},{3,7},... | collective-permute-start | bytes 98312 | tf_op jit(solution)/shard_map/ppermute | solution.py:48
  187.7 6.3 %collective-permute-start.10 = (f32[512]{0:T(512)S(1)}, f32[512]{0:T(512)S(1)}, u32[]{:S(2)}, u32[]{:S(2)}) collective-permute-start(f32[512]{0:T(512)S(1)} %add.251), channel_id=1, source_target_pairs={{0,1},{1,0},{2,3},{3,2},{4,5},{5,4},{6,7},{7,6},{8,9},{9,8},{10,11... | collective-permute-start | bytes 6152 | tf_op jit(solution)/shard_map/ppermute | solution.py:48
  191.2 7.8 %collective-permute-start.8 = (f32[8192]{0:T(1024)S(1)}, f32[8192]{0:T(1024)S(1)}, u32[]{:S(2)}, u32[]{:S(2)}) collective-permute-start(f32[8192]{0:T(1024)S(1)} %add.248), channel_id=1, source_target_pairs={{0,8},{2,10},{4,12},{6,14},{8,0},{10,2},{12,4},{14,6},{1,9},{3,11}... | collective-permute-start | bytes 98312 | tf_op jit(solution)/shard_map/ppermute | solution.py:48
  213.1 8.6 %collective-permute-start.11 = (f32[128,512]{0,1:T(8,128)S(1)}, f32[128,512]{0,1:T(8,128)S(1)}, u32[]{:S(2)}, u32[]{:S(2)}) collective-permute-start(f32[128,512]{0,1:T(8,128)S(1)} %get-tuple-element.13), channel_id=1, source_target_pairs={{0,1},{1,128},{128,129},{129,0},{2,3},{3,130},{130,131},{131,2},{4... | collective-permute-start | bytes 786440 | tf_op jit(solution)/shard_map/ppermute | solution.py:125
  216.2 7.7 %collective-permute-start.12 = (f32[128,512]{0,1:T(8,128)S(1)}, f32[128,512]{0,1:T(8,128)S(1)}, u32[]{:S(2)}, u32[]{:S(2)}) collective-permute-start(f32[128,512]{0,1:T(8,128)S(1)} %get-tuple-element.15), channel_id=1, source_target_pairs={{0,128},{1,129},{128,0},{129,1},{2,130},{3,131},{130,2},{131,3},{4... | collective-permute-start | bytes 786440 | tf_op jit(solution)/shard_map/ppermute | solution.py:125
  216.8 8.3 %collective-permute-start.13 = (f32[128,512]{0,1:T(8,128)S(1)}, f32[128,512]{0,1:T(8,128)S(1)}, u32[]{:S(2)}, u32[]{:S(2)}) collective-permute-start(f32[128,512]{0,1:T(8,128)S(1)} %get-tuple-element.14), channel_id=1, source_target_pairs={{0,129},{1,0},{128,1},{129,128},{2,131},{3,2},{130,3},{131,130},{4... | collective-permute-start | bytes 786440 | tf_op jit(solution)/shard_map/ppermute | solution.py:125
Sparse Core Ops, SparseCore 0:
  83.6 76.5 all-gather.1

commit v6 on v5

--- a/solution.py
+++ b/solution.py
@@ -42,6 +42,14 @@
 def tree_sum(value, axes):
     for axis in axes:
         size = lax.axis_size(axis)
+        if size == 4:
+            me = lax.axis_index(axis)
+            parts = [value] + [lax.ppermute(value, axis, ring_pairs(size, k)) for k in range(1, size)]
+            ordered = jnp.take(jnp.stack(parts), (me - jnp.arange(size, dtype=jnp.int32)) % size, axis=0)
+            value = ordered[0]
+            for k in range(1, size):
+                value = value + ordered[k]
+            continue
         step = 1
         while step < size:
             pairs = [(i, i ^ step) for i in range(size)]

time: 235 us -> 233 us (level)
    ppermute x8 -> x6, waiting for transfers between devices: 13.5 us -> 7.49 us  [tree_sum(): value = value + lax.ppermute(value, axis, pairs)]
    ppermute x0 -> x3, starting transfers between devices: none -> 4.11 us  [tree_sum(): lax.ppermute(value, axis, ring_pairs(size, k))]
    ppermute x0 -> x3, waiting for transfers between devices: none -> 3.68 us  [tree_sum(): lax.ppermute(value, axis, ring_pairs(size, k))]
    ppermute x8 -> x6, starting transfers between devices: 13.6 us -> 10.3 us  [tree_sum(): value = value + lax.ppermute(value, axis, pairs)]
  transfers between devices with their start and end apart: 18 -> 19, of which waited for: 15 -> 15; matrix products, arithmetic and copies ran while one was open for 1% -> 1% of each run, Pallas kernels for 0% -> 0%
where the time goes in v6:
time: 233 us
  waiting for transfers between devices  112 us (48%)
  starting transfers between devices  34.2 us (15%)
  matrix products  25.6 us (11%)
  blocking collectives  25.4 us (11%)
  local copies, waits for them, and re-layouts  15.3 us (7%)
  between operations  13.7 us (6%)
  other arithmetic  6.22 us (3%)
    all_gather x1, waiting for transfers between devices, shards(): row_block = lax.all_gather(neighbour, ROWS, axis=0, tiled=True)  65.4 us
    all_to_all x1, blocking collectives, fetch_rows(): lax.all_to_all(request, INNER, split_axis=0, concat_axis=0, tiled=True)  25.4 us
    dot_general x1, matrix products, column_terms(): lax.dot_general(weights, row_block, (((0,), (0,)), ((), ())), preferred_e...  13.9 us
    all_to_all x1, waiting for transfers between devices, fetch_rows(): lax.all_to_all(relayed, INNER, split_axis=0, concat_axis=0, tiled=True)  12.9 us
    dot_general x1, matrix products, block_exp(): jnp.einsum('rd,cd->rc', row_block, column_block, preferred_element_type=j...  11.7 us
    ppermute x6, starting transfers between devices, tree_sum(): value = value + lax.ppermute(value, axis, pairs)  10.3 us
    ppermute x3, waiting for transfers between devices, scatter_columns(): total = total + lax.ppermute(piece, axes, ring_pairs(size, k))  8.13 us
    ppermute x6, waiting for transfers between devices, tree_sum(): value = value + lax.ppermute(value, axis, pairs)  7.49 us
  transfers between devices with their start and end apart: 19, of which 15 were waited for; matrix products, arithmetic and copies ran while one was open for 1% of the time, Pallas kernels for 0%

profile of v6, /device:TPU:8, one launch (start us, length us, event | category | flops | bytes accessed | tf_op | source)
XLA Modules:
  0.0 232.8 jit_solution(8009846316517879004)
XLA Ops:
  6.5 0.7 and_select_fusion.4
  7.2 0.7 fusion.35
  8.0 0.7 and_bitcast_fusion
  8.7 1.0 scatter_custom_fusion.1
  9.8 1.1 scatter_custom_fusion
  11.1 25.4 %all_to_all.24 = s32[64,4,2]{1,2,0:T(2,128)S(1)} all-to-all(s32[64,4,2]{1,2,0:T(2,128)S(1)} %copy.33), channel_id=1, replica_groups=mesh['xl'=2,'c'=2,'y'=4,'z'=8,'xh'=2] {'y','z','xh'}, dimensions={0} | all-to-all | bytes 4096 | tf_op jit(solution)/shard_map/all_to_all | solution.py:85
  37.5 1.4 scatter_custom_fusion.2
  38.9 0.7 all_to_all.16
  39.6 3.2 %all-to-all-start.1 = ((s32[4,1,64]{2,1,0:T(1,128)}), s32[4,1,64]{2,1,0:T(1,128)S(1)}, u32[]{:S(2)}, u32[]{:S(2)}) async-start(s32[4,1,64]{2,1,0:T(1,128)} %all_to_all.16), calls=%async_computation.1 | async-start | bytes 4096 | tf_op jit(solution)/shard_map/all_to_all | solution.py:99
  43.0 3.5 %all-to-all-done.1 = s32[4,1,64]{2,1,0:T(1,128)S(1)} async-done(((s32[4,1,64]{2,1,0:T(1,128)}), s32[4,1,64]{2,1,0:T(1,128)S(1)}, u32[]{:S(2)}, u32[]{:S(2)}) %all-to-all-start.1) | async-done | bytes 1056 | tf_op jit(solution)/shard_map/all_to_all | solution.py:99
  46.6 3.9 %gather_fusion = bf16[256,512]{1,0:T(8,128)(2,1)S(1)} fusion(bf16[4096,512]{1,0:T(8,128)(2,1)} %param.4, s32[1024]{0:T(1024)S(1)} %pad_clamp_fusion.4), kind=kCustom, calls=%fused_computation | custom fusion | bytes 525312 | tf_op jit(solution)/shard_map/jit(_take)/gather | solution.py:100
  50.6 0.8 select_select_fusion.1
  51.4 3.4 %all-to-all-start.2 = ((bf16[4,64,512]{2,1,0:T(8,128)(2,1)}), bf16[4,64,512]{2,1,0:T(8,128)(2,1)S(1)}, u32[]{:S(2)}, u32[]{:S(2)}) async-start(bf16[4,64,512]{2,1,0:T(8,128)(2,1)} %select_select_fusion.1), calls=%async_computation.2 | async-start | bytes 524288 | tf_op jit(solution)/shard_map/all_to_all | solution.py:102
  55.1 5.7 %all-to-all-done.2 = bf16[4,64,512]{2,1,0:T(8,128)(2,1)S(1)} async-done(((bf16[4,64,512]{2,1,0:T(8,128)(2,1)}), bf16[4,64,512]{2,1,0:T(8,128)(2,1)S(1)}, u32[]{:S(2)}, u32[]{:S(2)}) %all-to-all-start.2) | async-done | bytes 262176 | tf_op jit(solution)/shard_map/all_to_all | solution.py:102
  60.8 1.2 gather_fusion.1
  62.0 1.0 select_select_fusion
  63.1 5.5 %all-to-all-start.3 = ((bf16[64,4,512]{2,1,0:T(4,128)(2,1)}), bf16[64,4,512]{2,1,0:T(4,128)(2,1)S(1)}, u32[]{:S(2)}, u32[]{:S(2)}) async-start(bf16[64,4,512]{2,1,0:T(4,128)(2,1)} %select_select_fusion), calls=%async_computation.3 | async-start | bytes 524288 | tf_op jit(solution)/shard_map/all_to_all | solution.py:107
  68.6 12.9 %all-to-all-done.3 = bf16[64,4,512]{2,1,0:T(4,128)(2,1)S(1)} async-done(((bf16[64,4,512]{2,1,0:T(4,128)(2,1)}), bf16[64,4,512]{2,1,0:T(4,128)(2,1)S(1)}, u32[]{:S(2)}, u32[]{:S(2)}) %all-to-all-start.3) | async-done | bytes 262176 | tf_op jit(solution)/shard_map/all_to_all | solution.py:107
  81.6 0.8 gather_fusion.2
  82.7 0.8 fusion.9
  83.5 1.0 copy.42
  84.6 1.0 collective-permute-start
  85.7 0.7 collective-permute-start.1
  86.4 1.6 collective-permute-start.2
  88.2 3.4 %collective-permute-done = bf16[128,512]{0,1:T(8,128)(2,1)S(1)} collective-permute-done((bf16[128,512]{0,1:T(8,128)(2,1)S(1)}, bf16[128,512]{0,1:T(8,128)(2,1)S(1)}, u32[]{:S(2)}, u32[]{:S(2)}) %collective-permute-start) | collective-permute-done | bytes 131104 | tf_op jit(solution)/shard_map/ppermute | solution.py:120
  91.7 2.1 collective-permute-done.2
  93.8 0.6 gather_fusion.3
  94.9 65.4 %all-gather.2.cloned.1.call-done = bf16[8192,512]{1,0:T(8,128)(2,1)} async-done(((bf16[128,512]{1,0:T(8,128)(2,1)}), bf16[8192,512]{1,0:T(8,128)(2,1)}) %all-gather.2.cloned.1.call-update) | async-done | bytes 8388624 | tf_op jit(solution)/shard_map/all_gather | solution.py:148
  160.2 11.7 %fusion.1 = (f32[8192]{0:T(1024)S(1)}, f32[512]{0:T(512)S(1)}, f32[8192,512]{1,0:T(8,128)}) fusion(bf16[8192,512]{1,0:T(8,128)(2,1)} %all-gather.2.cloned.1.call-done, bf16[512,512]{1,0:T(8,128)(2,1)S(1)} %bitcast_select_fusion), kind=kOutput, calls=%fused_computation.11 | convolution fusion | flops 4307541504 | bytes 25724928 | tf_op jit(solution)/shard_map/rd,cd->rc/dot_general | solution.py:20
  172.2 0.9 collective-permute-done.3
  173.1 1.2 collective-permute-start.4
  174.3 2.7 %collective-permute-start.5 = (f32[8192]{0:T(1024)S(1)}, f32[8192]{0:T(1024)S(1)}, u32[]{:S(2)}, u32[]{:S(2)}) collective-permute-start(f32[8192]{0:T(1024)S(1)} %add.284), channel_id=1, source_target_pairs={{0,32},{16,48},{32,0},{48,16},{1,33},{17,49},{33,1},{49,17},{2,34}... | collective-permute-start | bytes 98312 | tf_op jit(solution)/shard_map/ppermute | solution.py:47
  177.3 2.6 %collective-permute-done.5 = f32[8192]{0:T(1024)S(1)} collective-permute-done((f32[8192]{0:T(1024)S(1)}, f32[8192]{0:T(1024)S(1)}, u32[]{:S(2)}, u32[]{:S(2)}) %collective-permute-start.5) | collective-permute-done | bytes 32800 | tf_op jit(solution)/shard_map/ppermute | solution.py:47
  179.9 1.1 collective-permute-done.6
  181.1 0.6 gather_fusion.4
  181.9 1.3 collective-permute-start.7
  183.2 1.6 collective-permute-start.10
  184.8 1.1 collective-permute-done.7
  185.9 1.3 collective-permute-start.8
  187.2 3.1 %collective-permute-start.11 = (f32[512]{0:T(512)S(1)}, f32[512]{0:T(512)S(1)}, u32[]{:S(2)}, u32[]{:S(2)}) collective-permute-start(f32[512]{0:T(512)S(1)} %add.295), channel_id=1, source_target_pairs={{0,1},{1,0},{2,3},{3,2},{4,5},{5,4},{6,7},{7,6},{8,9},{9,8},{10,11... | collective-permute-start | bytes 6152 | tf_op jit(solution)/shard_map/ppermute | solution.py:56
  190.7 2.8 %collective-permute-start.9 = (f32[8192]{0:T(1024)S(1)}, f32[8192]{0:T(1024)S(1)}, u32[]{:S(2)}, u32[]{:S(2)}) collective-permute-start(f32[8192]{0:T(1024)S(1)} %add.292), channel_id=1, source_target_pairs={{0,8},{2,10},{4,12},{6,14},{8,0},{10,2},{12,4},{14,6},{1,9},{3,11}... | collective-permute-start | bytes 98312 | tf_op jit(solution)/shard_map/ppermute | solution.py:56
  193.5 5.0 %collective-permute-done.9 = f32[8192]{0:T(1024)S(1)} collective-permute-done((f32[8192]{0:T(1024)S(1)}, f32[8192]{0:T(1024)S(1)}, u32[]{:S(2)}, u32[]{:S(2)}) %collective-permute-start.9) | collective-permute-done | bytes 32800 | tf_op jit(solution)/shard_map/ppermute | solution.py:56
  198.5 13.9 %fusion.2 = f32[512,512]{0,1:T(8,128)S(1)} fusion(bf16[8192,512]{1,0:T(8,128)(2,1)} %all-gather.2.cloned.1.call-done, f32[8192,512]{1,0:T(8,128)} %get-tuple-element.26, s32[512]{0:T(512)S(1)} %iota_subtract_fusion.1, f32[512]{0:T(512)S(1)} %add_divide_fusion.1, f32[8192]{0:T(1024)S(1)} %add_divide_fusion, s32[8192]{0:T(1024)S(1)} %iota_subtract_fusion, ...), kind=kOutput, calls=%fused_computation.12 | convolution fusion | flops 4332716032 | bytes 26300416 | tf_op jit(solution)/shard_map/dot_general | solution.py:37
  212.6 3.1 %collective-permute-start.12 = (f32[128,512]{0,1:T(8,128)S(1)}, f32[128,512]{0,1:T(8,128)S(1)}, u32[]{:S(2)}, u32[]{:S(2)}) collective-permute-start(f32[128,512]{0,1:T(8,128)S(1)} %get-tuple-element.13), channel_id=1, source_target_pairs={{0,1},{1,128},{128,129},{129,0},{2,3},{3,130},{130,131},{131,2},{4... | collective-permute-start | bytes 786440 | tf_op jit(solution)/shard_map/ppermute | solution.py:133
  216.8 5.3 %collective-permute-done.12 = f32[128,512]{0,1:T(8,128)S(1)} collective-permute-done((f32[128,512]{0,1:T(8,128)S(1)}, f32[128,512]{0,1:T(8,128)S(1)}, u32[]{:S(2)}, u32[]{:S(2)}) %collective-permute-start.12) | collective-permute-done | bytes 262176 | tf_op jit(solution)/shard_map/ppermute | solution.py:133
  222.1 1.5 collective-permute-done.13
  223.6 1.3 collective-permute-done.14
  225.1 0.8 copy.44
  (71 shorter events, 5.7 us)
Async XLA Ops:
  39.6 6.9 %all-to-all-start.1 = ((s32[4,1,64]{2,1,0:T(1,128)}), s32[4,1,64]{2,1,0:T(1,128)S(1)}, u32[]{:S(2)}, u32[]{:S(2)}) async-start(s32[4,1,64]{2,1,0:T(1,128)} %all_to_all.16), calls=%async_computation.1 | async-start | bytes 4096 | tf_op jit(solution)/shard_map/all_to_all | solution.py:99
  51.4 9.4 %all-to-all-start.2 = ((bf16[4,64,512]{2,1,0:T(8,128)(2,1)}), bf16[4,64,512]{2,1,0:T(8,128)(2,1)S(1)}, u32[]{:S(2)}, u32[]{:S(2)}) async-start(bf16[4,64,512]{2,1,0:T(8,128)(2,1)} %select_select_fusion.1), calls=%async_computation.2 | async-start | bytes 524288 | tf_op jit(solution)/shard_map/all_to_all | solution.py:102
  63.1 18.5 %all-to-all-start.3 = ((bf16[64,4,512]{2,1,0:T(4,128)(2,1)}), bf16[64,4,512]{2,1,0:T(4,128)(2,1)S(1)}, u32[]{:S(2)}, u32[]{:S(2)}) async-start(bf16[64,4,512]{2,1,0:T(4,128)(2,1)} %select_select_fusion), calls=%async_computation.3 | async-start | bytes 524288 | tf_op jit(solution)/shard_map/all_to_all | solution.py:107
  68.6 91.7 %all-gather.2.cloned.1.call-start = ((), (), s32[]{:S(2)}) async-start(), calls=%async_computation.4 | async-start | bytes 8519680 | tf_op jit(solution)/shard_map/all_gather | solution.py:148
  84.6 7.0 %collective-permute-start = (bf16[128,512]{0,1:T(8,128)(2,1)S(1)}, bf16[128,512]{0,1:T(8,128)(2,1)S(1)}, u32[]{:S(2)}, u32[]{:S(2)}) collective-permute-start(bf16[128,512]{0,1:T(8,128)(2,1)S(1)} %fusion.4), channel_id=1, source_target_pairs={{0,1},{1,128},{128,129},{129,0},{2,3},{3,130},{130,131},{131,2},{4... | collective-permute-start | bytes 393224 | tf_op jit(solution)/shard_map/ppermute | solution.py:120
  85.7 6.0 %collective-permute-start.1 = (bf16[128,512]{0,1:T(8,128)(2,1)S(1)}, bf16[128,512]{0,1:T(8,128)(2,1)S(1)}, u32[]{:S(2)}, u32[]{:S(2)}) collective-permute-start(bf16[128,512]{0,1:T(8,128)(2,1)S(1)} %fusion.4), channel_id=1, source_target_pairs={{0,128},{1,129},{128,0},{129,1},{2,130},{3,131},{130,2},{131,3},{4... | collective-permute-start | bytes 393224 | tf_op jit(solution)/shard_map/ppermute | solution.py:120
  86.4 7.3 %collective-permute-start.2 = (bf16[128,512]{0,1:T(8,128)(2,1)S(1)}, bf16[128,512]{0,1:T(8,128)(2,1)S(1)}, u32[]{:S(2)}, u32[]{:S(2)}) collective-permute-start(bf16[128,512]{0,1:T(8,128)(2,1)S(1)} %fusion.4), channel_id=1, source_target_pairs={{0,129},{1,0},{128,1},{129,128},{2,131},{3,2},{130,3},{131,130},{4... | collective-permute-start | bytes 393224 | tf_op jit(solution)/shard_map/ppermute | solution.py:120
  171.9 1.2 collective-permute-start.3
  173.1 4.1 %collective-permute-start.4 = (f32[8192]{0:T(1024)S(1)}, f32[8192]{0:T(1024)S(1)}, u32[]{:S(2)}, u32[]{:S(2)}) collective-permute-start(f32[8192]{0:T(1024)S(1)} %add.284), channel_id=1, source_target_pairs={{0,16},{16,32},{32,48},{48,0},{1,17},{17,33},{33,49},{49,1},{2,18}... | collective-permute-start | bytes 98312 | tf_op jit(solution)/shard_map/ppermute | solution.py:47
  174.3 5.5 %collective-permute-start.5 = (f32[8192]{0:T(1024)S(1)}, f32[8192]{0:T(1024)S(1)}, u32[]{:S(2)}, u32[]{:S(2)}) collective-permute-start(f32[8192]{0:T(1024)S(1)} %add.284), channel_id=1, source_target_pairs={{0,32},{16,48},{32,0},{48,16},{1,33},{17,49},{33,1},{49,17},{2,34}... | collective-permute-start | bytes 98312 | tf_op jit(solution)/shard_map/ppermute | solution.py:47
  177.0 3.9 %collective-permute-start.6 = (f32[8192]{0:T(1024)S(1)}, f32[8192]{0:T(1024)S(1)}, u32[]{:S(2)}, u32[]{:S(2)}) collective-permute-start(f32[8192]{0:T(1024)S(1)} %add.284), channel_id=1, source_target_pairs={{0,48},{16,0},{32,16},{48,32},{1,49},{17,1},{33,17},{49,33},{2,50}... | collective-permute-start | bytes 98312 | tf_op jit(solution)/shard_map/ppermute | solution.py:47
  181.9 4.0 %collective-permute-start.7 = (f32[8192]{0:T(1024)S(1)}, f32[8192]{0:T(1024)S(1)}, u32[]{:S(2)}, u32[]{:S(2)}) collective-permute-start(f32[8192]{0:T(1024)S(1)} %bitcast.69), channel_id=1, source_target_pairs={{0,2},{2,0},{4,6},{6,4},{8,10},{10,8},{12,14},{14,12},{1,3},{3,1},... | collective-permute-start | bytes 98312 | tf_op jit(solution)/shard_map/ppermute | solution.py:56
  183.2 4.0 %collective-permute-start.10 = (f32[512]{0:T(512)S(1)}, f32[512]{0:T(512)S(1)}, u32[]{:S(2)}, u32[]{:S(2)}) collective-permute-start(f32[512]{0:T(512)S(1)} %get-tuple-element.6), channel_id=1, source_target_pairs={{0,128},{128,0},{1,129},{129,1},{2,130},{130,2},{3,131},{131,3},{4... | collective-permute-start | bytes 6152 | tf_op jit(solution)/shard_map/ppermute | solution.py:56
  185.9 4.8 %collective-permute-start.8 = (f32[8192]{0:T(1024)S(1)}, f32[8192]{0:T(1024)S(1)}, u32[]{:S(2)}, u32[]{:S(2)}) collective-permute-start(f32[8192]{0:T(1024)S(1)} %add.291), channel_id=1, source_target_pairs={{0,4},{2,6},{4,0},{6,2},{8,12},{10,14},{12,8},{14,10},{1,5},{3,7},... | collective-permute-start | bytes 98312 | tf_op jit(solution)/shard_map/ppermute | solution.py:56
  187.2 6.3 %collective-permute-start.11 = (f32[512]{0:T(512)S(1)}, f32[512]{0:T(512)S(1)}, u32[]{:S(2)}, u32[]{:S(2)}) collective-permute-start(f32[512]{0:T(512)S(1)} %add.295), channel_id=1, source_target_pairs={{0,1},{1,0},{2,3},{3,2},{4,5},{5,4},{6,7},{7,6},{8,9},{9,8},{10,11... | collective-permute-start | bytes 6152 | tf_op jit(solution)/shard_map/ppermute | solution.py:56
  190.7 7.8 %collective-permute-start.9 = (f32[8192]{0:T(1024)S(1)}, f32[8192]{0:T(1024)S(1)}, u32[]{:S(2)}, u32[]{:S(2)}) collective-permute-start(f32[8192]{0:T(1024)S(1)} %add.292), channel_id=1, source_target_pairs={{0,8},{2,10},{4,12},{6,14},{8,0},{10,2},{12,4},{14,6},{1,9},{3,11}... | collective-permute-start | bytes 98312 | tf_op jit(solution)/shard_map/ppermute | solution.py:56
  212.6 9.5 %collective-permute-start.12 = (f32[128,512]{0,1:T(8,128)S(1)}, f32[128,512]{0,1:T(8,128)S(1)}, u32[]{:S(2)}, u32[]{:S(2)}) collective-permute-start(f32[128,512]{0,1:T(8,128)S(1)} %get-tuple-element.13), channel_id=1, source_target_pairs={{0,1},{1,128},{128,129},{129,0},{2,3},{3,130},{130,131},{131,2},{4... | collective-permute-start | bytes 786440 | tf_op jit(solution)/shard_map/ppermute | solution.py:133
  215.7 7.9 %collective-permute-start.13 = (f32[128,512]{0,1:T(8,128)S(1)}, f32[128,512]{0,1:T(8,128)S(1)}, u32[]{:S(2)}, u32[]{:S(2)}) collective-permute-start(f32[128,512]{0,1:T(8,128)S(1)} %get-tuple-element.15), channel_id=1, source_target_pairs={{0,128},{1,129},{128,0},{129,1},{2,130},{3,131},{130,2},{131,3},{4... | collective-permute-start | bytes 786440 | tf_op jit(solution)/shard_map/ppermute | solution.py:133
  216.2 8.7 %collective-permute-start.14 = (f32[128,512]{0,1:T(8,128)S(1)}, f32[128,512]{0,1:T(8,128)S(1)}, u32[]{:S(2)}, u32[]{:S(2)}) collective-permute-start(f32[128,512]{0,1:T(8,128)S(1)} %get-tuple-element.14), channel_id=1, source_target_pairs={{0,129},{1,0},{128,1},{129,128},{2,131},{3,2},{130,3},{131,130},{4... | collective-permute-start | bytes 786440 | tf_op jit(solution)/shard_map/ppermute | solution.py:133
Sparse Core Ops, SparseCore 0:
  83.6 76.5 all-gather.1

commit v7 on v6

--- a/solution.py
+++ b/solution.py
@@ -130,7 +130,8 @@
     for k in range(1, size):
         target = (me + k) % size
         piece = lax.dynamic_slice_in_dim(terms, target * rows_dev, rows_dev, axis=0)
-        total = total + lax.ppermute(piece, axes, ring_pairs(size, k))
+        sent = lax.ppermute(piece.astype(jnp.bfloat16), axes, ring_pairs(size, k))
+        total = total + sent.astype(jnp.float32)
     return total
 
 

time: 233 us -> 231 us (level)
  no operation moved by 1% of the time
where the time goes in v7:
time: 231 us
  waiting for transfers between devices  110 us (48%)
  starting transfers between devices  34.2 us (15%)
  matrix products  25.6 us (11%)
  blocking collectives  25.4 us (11%)
  local copies, waits for them, and re-layouts  15.3 us (7%)
  between operations  13.7 us (6%)
  other arithmetic  6.28 us (3%)
    all_gather x1, waiting for transfers between devices, shards(): row_block = lax.all_gather(neighbour, ROWS, axis=0, tiled=True)  65.4 us
    all_to_all x1, blocking collectives, fetch_rows(): lax.all_to_all(request, INNER, split_axis=0, concat_axis=0, tiled=True)  25.4 us
    dot_general x1, matrix products, column_terms(): lax.dot_general(weights, row_block, (((0,), (0,)), ((), ())), preferred_e...  13.9 us
    all_to_all x1, waiting for transfers between devices, fetch_rows(): lax.all_to_all(relayed, INNER, split_axis=0, concat_axis=0, tiled=True)  12.9 us
    dot_general x1, matrix products, block_exp(): jnp.einsum('rd,cd->rc', row_block, column_block, preferred_element_type=j...  11.7 us
    ppermute x6, starting transfers between devices, tree_sum(): value = value + lax.ppermute(value, axis, pairs)  10.3 us
    ppermute x6, waiting for transfers between devices, tree_sum(): value = value + lax.ppermute(value, axis, pairs)  7.49 us
    ppermute x3, waiting for transfers between devices, scatter_columns(): sent = lax.ppermute(piece.astype(jnp.bfloat16), axes, ring_pairs(size, k))  5.91 us
  transfers between devices with their start and end apart: 19, of which 15 were waited for; matrix products, arithmetic and copies ran while one was open for 1% of the time, Pallas kernels for 0%

profile of v7, /device:TPU:8, one launch (start us, length us, event | category | flops | bytes accessed | tf_op | source)
XLA Modules:
  0.0 230.6 jit_solution(13713756704462232327)
XLA Ops:
  6.5 0.7 and_select_fusion.4
  7.2 0.7 fusion.35
  8.0 0.7 and_bitcast_fusion
  8.7 1.0 scatter_custom_fusion.1
  9.8 1.1 scatter_custom_fusion
  11.1 25.4 %all_to_all.24 = s32[64,4,2]{1,2,0:T(2,128)S(1)} all-to-all(s32[64,4,2]{1,2,0:T(2,128)S(1)} %copy.33), channel_id=1, replica_groups=mesh['xl'=2,'c'=2,'y'=4,'z'=8,'xh'=2] {'y','z','xh'}, dimensions={0} | all-to-all | bytes 4096 | tf_op jit(solution)/shard_map/all_to_all | solution.py:85
  37.5 1.4 scatter_custom_fusion.2
  38.9 0.7 all_to_all.16
  39.6 3.2 %all-to-all-start.1 = ((s32[4,1,64]{2,1,0:T(1,128)}), s32[4,1,64]{2,1,0:T(1,128)S(1)}, u32[]{:S(2)}, u32[]{:S(2)}) async-start(s32[4,1,64]{2,1,0:T(1,128)} %all_to_all.16), calls=%async_computation.1 | async-start | bytes 4096 | tf_op jit(solution)/shard_map/all_to_all | solution.py:99
  43.0 3.5 %all-to-all-done.1 = s32[4,1,64]{2,1,0:T(1,128)S(1)} async-done(((s32[4,1,64]{2,1,0:T(1,128)}), s32[4,1,64]{2,1,0:T(1,128)S(1)}, u32[]{:S(2)}, u32[]{:S(2)}) %all-to-all-start.1) | async-done | bytes 1056 | tf_op jit(solution)/shard_map/all_to_all | solution.py:99
  46.6 3.9 %gather_fusion = bf16[256,512]{1,0:T(8,128)(2,1)S(1)} fusion(bf16[4096,512]{1,0:T(8,128)(2,1)} %param.4, s32[1024]{0:T(1024)S(1)} %pad_clamp_fusion.4), kind=kCustom, calls=%fused_computation | custom fusion | bytes 525312 | tf_op jit(solution)/shard_map/jit(_take)/gather | solution.py:100
  50.6 0.8 select_select_fusion.1
  51.4 3.4 %all-to-all-start.2 = ((bf16[4,64,512]{2,1,0:T(8,128)(2,1)}), bf16[4,64,512]{2,1,0:T(8,128)(2,1)S(1)}, u32[]{:S(2)}, u32[]{:S(2)}) async-start(bf16[4,64,512]{2,1,0:T(8,128)(2,1)} %select_select_fusion.1), calls=%async_computation.2 | async-start | bytes 524288 | tf_op jit(solution)/shard_map/all_to_all | solution.py:102
  55.1 5.7 %all-to-all-done.2 = bf16[4,64,512]{2,1,0:T(8,128)(2,1)S(1)} async-done(((bf16[4,64,512]{2,1,0:T(8,128)(2,1)}), bf16[4,64,512]{2,1,0:T(8,128)(2,1)S(1)}, u32[]{:S(2)}, u32[]{:S(2)}) %all-to-all-start.2) | async-done | bytes 262176 | tf_op jit(solution)/shard_map/all_to_all | solution.py:102
  60.8 1.2 gather_fusion.1
  62.0 1.0 select_select_fusion
  63.1 5.5 %all-to-all-start.3 = ((bf16[64,4,512]{2,1,0:T(4,128)(2,1)}), bf16[64,4,512]{2,1,0:T(4,128)(2,1)S(1)}, u32[]{:S(2)}, u32[]{:S(2)}) async-start(bf16[64,4,512]{2,1,0:T(4,128)(2,1)} %select_select_fusion), calls=%async_computation.3 | async-start | bytes 524288 | tf_op jit(solution)/shard_map/all_to_all | solution.py:107
  68.6 12.9 %all-to-all-done.3 = bf16[64,4,512]{2,1,0:T(4,128)(2,1)S(1)} async-done(((bf16[64,4,512]{2,1,0:T(4,128)(2,1)}), bf16[64,4,512]{2,1,0:T(4,128)(2,1)S(1)}, u32[]{:S(2)}, u32[]{:S(2)}) %all-to-all-start.3) | async-done | bytes 262176 | tf_op jit(solution)/shard_map/all_to_all | solution.py:107
  81.6 0.8 gather_fusion.2
  82.7 0.8 fusion.9
  83.5 1.0 copy.42
  84.6 1.0 collective-permute-start
  85.7 0.7 collective-permute-start.1
  86.4 1.6 collective-permute-start.2
  88.2 3.4 %collective-permute-done = bf16[128,512]{0,1:T(8,128)(2,1)S(1)} collective-permute-done((bf16[128,512]{0,1:T(8,128)(2,1)S(1)}, bf16[128,512]{0,1:T(8,128)(2,1)S(1)}, u32[]{:S(2)}, u32[]{:S(2)}) %collective-permute-start) | collective-permute-done | bytes 131104 | tf_op jit(solution)/shard_map/ppermute | solution.py:120
  91.7 2.1 collective-permute-done.2
  93.8 0.6 gather_fusion.3
  94.9 65.4 %all-gather.2.cloned.1.call-done = bf16[8192,512]{1,0:T(8,128)(2,1)} async-done(((bf16[128,512]{1,0:T(8,128)(2,1)}), bf16[8192,512]{1,0:T(8,128)(2,1)}) %all-gather.2.cloned.1.call-update) | async-done | bytes 8388624 | tf_op jit(solution)/shard_map/all_gather | solution.py:149
  160.2 11.7 %fusion.1 = (f32[8192]{0:T(1024)S(1)}, f32[512]{0:T(512)S(1)}, f32[8192,512]{1,0:T(8,128)}) fusion(bf16[8192,512]{1,0:T(8,128)(2,1)} %all-gather.2.cloned.1.call-done, bf16[512,512]{1,0:T(8,128)(2,1)S(1)} %bitcast_select_fusion), kind=kOutput, calls=%fused_computation.11 | convolution fusion | flops 4307541504 | bytes 25724928 | tf_op jit(solution)/shard_map/rd,cd->rc/dot_general | solution.py:20
  172.2 0.9 collective-permute-done.3
  173.1 1.2 collective-permute-start.4
  174.3 2.7 %collective-permute-start.5 = (f32[8192]{0:T(1024)S(1)}, f32[8192]{0:T(1024)S(1)}, u32[]{:S(2)}, u32[]{:S(2)}) collective-permute-start(f32[8192]{0:T(1024)S(1)} %add.284), channel_id=1, source_target_pairs={{0,32},{16,48},{32,0},{48,16},{1,33},{17,49},{33,1},{49,17},{2,34}... | collective-permute-start | bytes 98312 | tf_op jit(solution)/shard_map/ppermute | solution.py:47
  177.3 2.6 %collective-permute-done.5 = f32[8192]{0:T(1024)S(1)} collective-permute-done((f32[8192]{0:T(1024)S(1)}, f32[8192]{0:T(1024)S(1)}, u32[]{:S(2)}, u32[]{:S(2)}) %collective-permute-start.5) | collective-permute-done | bytes 32800 | tf_op jit(solution)/shard_map/ppermute | solution.py:47
  179.9 1.1 collective-permute-done.6
  181.1 0.6 gather_fusion.4
  181.9 1.3 collective-permute-start.7
  183.2 1.6 collective-permute-start.10
  184.8 1.1 collective-permute-done.7
  185.9 1.3 collective-permute-start.8
  187.2 3.1 %collective-permute-start.11 = (f32[512]{0:T(512)S(1)}, f32[512]{0:T(512)S(1)}, u32[]{:S(2)}, u32[]{:S(2)}) collective-permute-start(f32[512]{0:T(512)S(1)} %add.295), channel_id=1, source_target_pairs={{0,1},{1,0},{2,3},{3,2},{4,5},{5,4},{6,7},{7,6},{8,9},{9,8},{10,11... | collective-permute-start | bytes 6152 | tf_op jit(solution)/shard_map/ppermute | solution.py:56
  190.7 2.8 %collective-permute-start.9 = (f32[8192]{0:T(1024)S(1)}, f32[8192]{0:T(1024)S(1)}, u32[]{:S(2)}, u32[]{:S(2)}) collective-permute-start(f32[8192]{0:T(1024)S(1)} %add.292), channel_id=1, source_target_pairs={{0,8},{2,10},{4,12},{6,14},{8,0},{10,2},{12,4},{14,6},{1,9},{3,11}... | collective-permute-start | bytes 98312 | tf_op jit(solution)/shard_map/ppermute | solution.py:56
  193.5 5.0 %collective-permute-done.9 = f32[8192]{0:T(1024)S(1)} collective-permute-done((f32[8192]{0:T(1024)S(1)}, f32[8192]{0:T(1024)S(1)}, u32[]{:S(2)}, u32[]{:S(2)}) %collective-permute-start.9) | collective-permute-done | bytes 32800 | tf_op jit(solution)/shard_map/ppermute | solution.py:56
  198.5 13.9 %fusion.2 = f32[512,512]{0,1:T(8,128)S(1)} fusion(bf16[8192,512]{1,0:T(8,128)(2,1)} %all-gather.2.cloned.1.call-done, f32[8192,512]{1,0:T(8,128)} %get-tuple-element.24, s32[512]{0:T(512)S(1)} %iota_subtract_fusion.1, f32[512]{0:T(512)S(1)} %add_divide_fusion.1, f32[8192]{0:T(1024)S(1)} %add_divide_fusion, s32[8192]{0:T(1024)S(1)} %iota_subtract_fusion, ...), kind=kOutput, calls=%fused_computation.12 | convolution fusion | flops 4332716032 | bytes 26300416 | tf_op jit(solution)/shard_map/dot_general | solution.py:37
  212.6 3.1 %collective-permute-start.12 = (bf16[128,512]{0,1:T(8,128)(2,1)S(1)}, bf16[128,512]{0,1:T(8,128)(2,1)S(1)}, u32[]{:S(2)}, u32[]{:S(2)}) collective-permute-start(bf16[128,512]{0,1:T(8,128)(2,1)S(1)} %get-tuple-element.11), channel_id=1, source_target_pairs={{0,1},{1,128},{128,129},{129,0},{2,3},{3,130},{130,131},{131,2},{4... | collective-permute-start | bytes 393224 | tf_op jit(solution)/shard_map/ppermute | solution.py:133
  216.8 2.1 collective-permute-done.12
  218.9 1.8 collective-permute-done.13
  220.6 2.1 collective-permute-done.14
  222.9 0.8 copy.44
  (71 shorter events, 5.8 us)
Async XLA Ops:
  39.6 6.9 %all-to-all-start.1 = ((s32[4,1,64]{2,1,0:T(1,128)}), s32[4,1,64]{2,1,0:T(1,128)S(1)}, u32[]{:S(2)}, u32[]{:S(2)}) async-start(s32[4,1,64]{2,1,0:T(1,128)} %all_to_all.16), calls=%async_computation.1 | async-start | bytes 4096 | tf_op jit(solution)/shard_map/all_to_all | solution.py:99
  51.4 9.4 %all-to-all-start.2 = ((bf16[4,64,512]{2,1,0:T(8,128)(2,1)}), bf16[4,64,512]{2,1,0:T(8,128)(2,1)S(1)}, u32[]{:S(2)}, u32[]{:S(2)}) async-start(bf16[4,64,512]{2,1,0:T(8,128)(2,1)} %select_select_fusion.1), calls=%async_computation.2 | async-start | bytes 524288 | tf_op jit(solution)/shard_map/all_to_all | solution.py:102
  63.1 18.5 %all-to-all-start.3 = ((bf16[64,4,512]{2,1,0:T(4,128)(2,1)}), bf16[64,4,512]{2,1,0:T(4,128)(2,1)S(1)}, u32[]{:S(2)}, u32[]{:S(2)}) async-start(bf16[64,4,512]{2,1,0:T(4,128)(2,1)} %select_select_fusion), calls=%async_computation.3 | async-start | bytes 524288 | tf_op jit(solution)/shard_map/all_to_all | solution.py:107
  68.6 91.7 %all-gather.2.cloned.1.call-start = ((), (), s32[]{:S(2)}) async-start(), calls=%async_computation.4 | async-start | bytes 8519680 | tf_op jit(solution)/shard_map/all_gather | solution.py:149
  84.6 7.0 %collective-permute-start = (bf16[128,512]{0,1:T(8,128)(2,1)S(1)}, bf16[128,512]{0,1:T(8,128)(2,1)S(1)}, u32[]{:S(2)}, u32[]{:S(2)}) collective-permute-start(bf16[128,512]{0,1:T(8,128)(2,1)S(1)} %fusion.4), channel_id=1, source_target_pairs={{0,1},{1,128},{128,129},{129,0},{2,3},{3,130},{130,131},{131,2},{4... | collective-permute-start | bytes 393224 | tf_op jit(solution)/shard_map/ppermute | solution.py:120
  85.7 6.0 %collective-permute-start.1 = (bf16[128,512]{0,1:T(8,128)(2,1)S(1)}, bf16[128,512]{0,1:T(8,128)(2,1)S(1)}, u32[]{:S(2)}, u32[]{:S(2)}) collective-permute-start(bf16[128,512]{0,1:T(8,128)(2,1)S(1)} %fusion.4), channel_id=1, source_target_pairs={{0,128},{1,129},{128,0},{129,1},{2,130},{3,131},{130,2},{131,3},{4... | collective-permute-start | bytes 393224 | tf_op jit(solution)/shard_map/ppermute | solution.py:120
  86.4 7.3 %collective-permute-start.2 = (bf16[128,512]{0,1:T(8,128)(2,1)S(1)}, bf16[128,512]{0,1:T(8,128)(2,1)S(1)}, u32[]{:S(2)}, u32[]{:S(2)}) collective-permute-start(bf16[128,512]{0,1:T(8,128)(2,1)S(1)} %fusion.4), channel_id=1, source_target_pairs={{0,129},{1,0},{128,1},{129,128},{2,131},{3,2},{130,3},{131,130},{4... | collective-permute-start | bytes 393224 | tf_op jit(solution)/shard_map/ppermute | solution.py:120
  171.9 1.2 collective-permute-start.3
  173.1 4.1 %collective-permute-start.4 = (f32[8192]{0:T(1024)S(1)}, f32[8192]{0:T(1024)S(1)}, u32[]{:S(2)}, u32[]{:S(2)}) collective-permute-start(f32[8192]{0:T(1024)S(1)} %add.284), channel_id=1, source_target_pairs={{0,16},{16,32},{32,48},{48,0},{1,17},{17,33},{33,49},{49,1},{2,18}... | collective-permute-start | bytes 98312 | tf_op jit(solution)/shard_map/ppermute | solution.py:47
  174.3 5.5 %collective-permute-start.5 = (f32[8192]{0:T(1024)S(1)}, f32[8192]{0:T(1024)S(1)}, u32[]{:S(2)}, u32[]{:S(2)}) collective-permute-start(f32[8192]{0:T(1024)S(1)} %add.284), channel_id=1, source_target_pairs={{0,32},{16,48},{32,0},{48,16},{1,33},{17,49},{33,1},{49,17},{2,34}... | collective-permute-start | bytes 98312 | tf_op jit(solution)/shard_map/ppermute | solution.py:47
  177.0 3.9 %collective-permute-start.6 = (f32[8192]{0:T(1024)S(1)}, f32[8192]{0:T(1024)S(1)}, u32[]{:S(2)}, u32[]{:S(2)}) collective-permute-start(f32[8192]{0:T(1024)S(1)} %add.284), channel_id=1, source_target_pairs={{0,48},{16,0},{32,16},{48,32},{1,49},{17,1},{33,17},{49,33},{2,50}... | collective-permute-start | bytes 98312 | tf_op jit(solution)/shard_map/ppermute | solution.py:47
  181.9 4.0 %collective-permute-start.7 = (f32[8192]{0:T(1024)S(1)}, f32[8192]{0:T(1024)S(1)}, u32[]{:S(2)}, u32[]{:S(2)}) collective-permute-start(f32[8192]{0:T(1024)S(1)} %bitcast.69), channel_id=1, source_target_pairs={{0,2},{2,0},{4,6},{6,4},{8,10},{10,8},{12,14},{14,12},{1,3},{3,1},... | collective-permute-start | bytes 98312 | tf_op jit(solution)/shard_map/ppermute | solution.py:56
  183.2 4.0 %collective-permute-start.10 = (f32[512]{0:T(512)S(1)}, f32[512]{0:T(512)S(1)}, u32[]{:S(2)}, u32[]{:S(2)}) collective-permute-start(f32[512]{0:T(512)S(1)} %get-tuple-element.6), channel_id=1, source_target_pairs={{0,128},{128,0},{1,129},{129,1},{2,130},{130,2},{3,131},{131,3},{4... | collective-permute-start | bytes 6152 | tf_op jit(solution)/shard_map/ppermute | solution.py:56
  185.9 4.8 %collective-permute-start.8 = (f32[8192]{0:T(1024)S(1)}, f32[8192]{0:T(1024)S(1)}, u32[]{:S(2)}, u32[]{:S(2)}) collective-permute-start(f32[8192]{0:T(1024)S(1)} %add.291), channel_id=1, source_target_pairs={{0,4},{2,6},{4,0},{6,2},{8,12},{10,14},{12,8},{14,10},{1,5},{3,7},... | collective-permute-start | bytes 98312 | tf_op jit(solution)/shard_map/ppermute | solution.py:56
  187.2 6.3 %collective-permute-start.11 = (f32[512]{0:T(512)S(1)}, f32[512]{0:T(512)S(1)}, u32[]{:S(2)}, u32[]{:S(2)}) collective-permute-start(f32[512]{0:T(512)S(1)} %add.295), channel_id=1, source_target_pairs={{0,1},{1,0},{2,3},{3,2},{4,5},{5,4},{6,7},{7,6},{8,9},{9,8},{10,11... | collective-permute-start | bytes 6152 | tf_op jit(solution)/shard_map/ppermute | solution.py:56
  190.7 7.8 %collective-permute-start.9 = (f32[8192]{0:T(1024)S(1)}, f32[8192]{0:T(1024)S(1)}, u32[]{:S(2)}, u32[]{:S(2)}) collective-permute-start(f32[8192]{0:T(1024)S(1)} %add.292), channel_id=1, source_target_pairs={{0,8},{2,10},{4,12},{6,14},{8,0},{10,2},{12,4},{14,6},{1,9},{3,11}... | collective-permute-start | bytes 98312 | tf_op jit(solution)/shard_map/ppermute | solution.py:56
  212.6 6.3 %collective-permute-start.12 = (bf16[128,512]{0,1:T(8,128)(2,1)S(1)}, bf16[128,512]{0,1:T(8,128)(2,1)S(1)}, u32[]{:S(2)}, u32[]{:S(2)}) collective-permute-start(bf16[128,512]{0,1:T(8,128)(2,1)S(1)} %get-tuple-element.11), channel_id=1, source_target_pairs={{0,1},{1,128},{128,129},{129,0},{2,3},{3,130},{130,131},{131,2},{4... | collective-permute-start | bytes 393224 | tf_op jit(solution)/shard_map/ppermute | solution.py:133
  215.7 5.0 %collective-permute-start.13 = (bf16[128,512]{0,1:T(8,128)(2,1)S(1)}, bf16[128,512]{0,1:T(8,128)(2,1)S(1)}, u32[]{:S(2)}, u32[]{:S(2)}) collective-permute-start(bf16[128,512]{0,1:T(8,128)(2,1)S(1)} %get-tuple-element.13), channel_id=1, source_target_pairs={{0,128},{1,129},{128,0},{129,1},{2,130},{3,131},{130,2},{131,3},{4... | collective-permute-start | bytes 393224 | tf_op jit(solution)/shard_map/ppermute | solution.py:133
  216.2 6.5 %collective-permute-start.14 = (bf16[128,512]{0,1:T(8,128)(2,1)S(1)}, bf16[128,512]{0,1:T(8,128)(2,1)S(1)}, u32[]{:S(2)}, u32[]{:S(2)}) collective-permute-start(bf16[128,512]{0,1:T(8,128)(2,1)S(1)} %get-tuple-element.12), channel_id=1, source_target_pairs={{0,129},{1,0},{128,1},{129,128},{2,131},{3,2},{130,3},{131,130},{4... | collective-permute-start | bytes 393224 | tf_op jit(solution)/shard_map/ppermute | solution.py:133
Sparse Core Ops, SparseCore 0:
  83.6 76.5 all-gather.1

commit v8 on v6

--- a/solution.py
+++ b/solution.py
@@ -98,11 +98,9 @@
     asking = asking.reshape(outer_count, cap_group)
     asked = lax.all_to_all(asking, OUTER, split_axis=0, concat_axis=0, tiled=True)
     looked = jnp.take(queue, jnp.maximum(asked, 0), axis=0)
-    looked = jnp.where((asked >= 0)[..., None], looked, jnp.zeros((), jnp.bfloat16))
     answered = lax.all_to_all(looked, OUTER, split_axis=0, concat_axis=0, tiled=True)
     answered = answered.reshape(outer_count * cap_group, feature_width)
     relayed = jnp.take(answered, jnp.minimum(group_place, outer_count * cap_group - 1), axis=0)
-    relayed = jnp.where((relay_slot >= 0)[:, None], relayed, jnp.zeros((), jnp.bfloat16))
     relayed = relayed.reshape(inner_count, cap_member, feature_width)
     returned = lax.all_to_all(relayed, INNER, split_axis=0, concat_axis=0, tiled=True)
     return jnp.take(

time: 233 us -> 233 us (level)
  no operation moved by 1% of the time
where the time goes in v8:
time: 233 us
  waiting for transfers between devices  112 us (48%)
  starting transfers between devices  34.2 us (15%)
  matrix products  25.6 us (11%)
  blocking collectives  25.4 us (11%)
  local copies, waits for them, and re-layouts  15.1 us (6%)
  between operations  13.7 us (6%)
  other arithmetic  6.06 us (3%)
    all_gather x1, waiting for transfers between devices, shards(): row_block = lax.all_gather(neighbour, ROWS, axis=0, tiled=True)  65.4 us
    all_to_all x1, blocking collectives, fetch_rows(): lax.all_to_all(request, INNER, split_axis=0, concat_axis=0, tiled=True)  25.4 us
    dot_general x1, matrix products, column_terms(): lax.dot_general(weights, row_block, (((0,), (0,)), ((), ())), preferred_e...  13.9 us
    all_to_all x1, waiting for transfers between devices, fetch_rows(): lax.all_to_all(relayed, INNER, split_axis=0, concat_axis=0, tiled=True)  12.9 us
    dot_general x1, matrix products, block_exp(): jnp.einsum('rd,cd->rc', row_block, column_block, preferred_element_type=j...  11.7 us
    ppermute x6, starting transfers between devices, tree_sum(): value = value + lax.ppermute(value, axis, pairs)  10.3 us
    ppermute x3, waiting for transfers between devices, scatter_columns(): total = total + lax.ppermute(piece, axes, ring_pairs(size, k))  8.13 us
    ppermute x6, waiting for transfers between devices, tree_sum(): value = value + lax.ppermute(value, axis, pairs)  7.49 us
  transfers between devices with their start and end apart: 19, of which 15 were waited for; matrix products, arithmetic and copies ran while one was open for 1% of the time, Pallas kernels for 0%

profile of v8, /device:TPU:8, one launch (start us, length us, event | category | flops | bytes accessed | tf_op | source)
XLA Modules:
  0.0 232.5 jit_solution(3000429454801674834)
XLA Ops:
  6.5 0.7 and_select_fusion.4
  7.2 0.7 fusion.35
  8.0 0.7 and_bitcast_fusion
  8.7 1.0 scatter_custom_fusion.1
  9.8 1.1 scatter_custom_fusion
  11.1 25.4 %all_to_all.24 = s32[64,4,2]{1,2,0:T(2,128)S(1)} all-to-all(s32[64,4,2]{1,2,0:T(2,128)S(1)} %copy.29), channel_id=1, replica_groups=mesh['xl'=2,'c'=2,'y'=4,'z'=8,'xh'=2] {'y','z','xh'}, dimensions={0} | all-to-all | bytes 4096 | tf_op jit(solution)/shard_map/all_to_all | solution.py:85
  37.4 1.4 scatter_custom_fusion.2
  38.8 0.7 all_to_all.16
  39.5 3.2 %all-to-all-start.1 = ((s32[4,1,64]{2,1,0:T(1,128)}), s32[4,1,64]{2,1,0:T(1,128)S(1)}, u32[]{:S(2)}, u32[]{:S(2)}) async-start(s32[4,1,64]{2,1,0:T(1,128)} %all_to_all.16), calls=%async_computation.1 | async-start | bytes 4096 | tf_op jit(solution)/shard_map/all_to_all | solution.py:99
  42.9 3.5 %all-to-all-done.1 = s32[4,1,64]{2,1,0:T(1,128)S(1)} async-done(((s32[4,1,64]{2,1,0:T(1,128)}), s32[4,1,64]{2,1,0:T(1,128)S(1)}, u32[]{:S(2)}, u32[]{:S(2)}) %all-to-all-start.1) | async-done | bytes 1056 | tf_op jit(solution)/shard_map/all_to_all | solution.py:99
  46.5 3.9 %gather_fusion = bf16[256,512]{1,0:T(8,128)(2,1)S(1)} fusion(bf16[4096,512]{1,0:T(8,128)(2,1)} %param.4, s32[1024]{0:T(1024)S(1)} %pad_clamp_fusion.4), kind=kCustom, calls=%fused_computation | custom fusion | bytes 525312 | tf_op jit(solution)/shard_map/jit(_take)/gather | solution.py:100
  50.5 0.8 broadcast_select_fusion
  51.3 3.4 %all-to-all-start.2 = ((bf16[4,64,512]{2,1,0:T(8,128)(2,1)}), bf16[4,64,512]{2,1,0:T(8,128)(2,1)S(1)}, u32[]{:S(2)}, u32[]{:S(2)}) async-start(bf16[4,64,512]{2,1,0:T(8,128)(2,1)} %broadcast_select_fusion), calls=%async_computation.2 | async-start | bytes 524288 | tf_op jit(solution)/shard_map/all_to_all | solution.py:101
  54.8 5.8 %all-to-all-done.2 = bf16[4,64,512]{2,1,0:T(8,128)(2,1)S(1)} async-done(((bf16[4,64,512]{2,1,0:T(8,128)(2,1)}), bf16[4,64,512]{2,1,0:T(8,128)(2,1)S(1)}, u32[]{:S(2)}, u32[]{:S(2)}) %all-to-all-start.2) | async-done | bytes 262176 | tf_op jit(solution)/shard_map/all_to_all | solution.py:101
  60.7 1.2 gather_fusion.1
  61.9 0.9 broadcast_select_fusion.1
  62.8 5.5 %all-to-all-start.3 = ((bf16[64,4,512]{2,1,0:T(4,128)(2,1)}), bf16[64,4,512]{2,1,0:T(4,128)(2,1)S(1)}, u32[]{:S(2)}, u32[]{:S(2)}) async-start(bf16[64,4,512]{2,1,0:T(4,128)(2,1)} %broadcast_select_fusion.1), calls=%async_computation.3 | async-start | bytes 524288 | tf_op jit(solution)/shard_map/all_to_all | solution.py:105
  68.4 12.9 %all-to-all-done.3 = bf16[64,4,512]{2,1,0:T(4,128)(2,1)S(1)} async-done(((bf16[64,4,512]{2,1,0:T(4,128)(2,1)}), bf16[64,4,512]{2,1,0:T(4,128)(2,1)S(1)}, u32[]{:S(2)}, u32[]{:S(2)}) %all-to-all-start.3) | async-done | bytes 262176 | tf_op jit(solution)/shard_map/all_to_all | solution.py:105
  81.4 0.8 gather_fusion.2
  82.4 0.8 fusion.9
  83.2 1.0 copy.35
  84.4 1.0 collective-permute-start
  85.4 0.7 collective-permute-start.1
  86.2 1.6 collective-permute-start.2
  88.0 3.4 %collective-permute-done = bf16[128,512]{0,1:T(8,128)(2,1)S(1)} collective-permute-done((bf16[128,512]{0,1:T(8,128)(2,1)S(1)}, bf16[128,512]{0,1:T(8,128)(2,1)S(1)}, u32[]{:S(2)}, u32[]{:S(2)}) %collective-permute-start) | collective-permute-done | bytes 131104 | tf_op jit(solution)/shard_map/ppermute | solution.py:118
  91.4 2.1 collective-permute-done.2
  93.6 0.6 gather_fusion.3
  94.6 65.4 %all-gather.2.cloned.1.call-done = bf16[8192,512]{1,0:T(8,128)(2,1)} async-done(((bf16[128,512]{1,0:T(8,128)(2,1)}), bf16[8192,512]{1,0:T(8,128)(2,1)}) %all-gather.2.cloned.1.call-update) | async-done | bytes 8388624 | tf_op jit(solution)/shard_map/all_gather | solution.py:146
  160.0 11.7 %fusion.1 = (f32[8192]{0:T(1024)S(1)}, f32[512]{0:T(512)S(1)}, f32[8192,512]{1,0:T(8,128)}) fusion(bf16[8192,512]{1,0:T(8,128)(2,1)} %all-gather.2.cloned.1.call-done, bf16[512,512]{1,0:T(8,128)(2,1)S(1)} %bitcast_select_fusion), kind=kOutput, calls=%fused_computation.11 | convolution fusion | flops 4307541504 | bytes 25724928 | tf_op jit(solution)/shard_map/rd,cd->rc/dot_general | solution.py:20
  171.9 0.9 collective-permute-done.3
  172.9 1.2 collective-permute-start.4
  174.1 2.7 %collective-permute-start.5 = (f32[8192]{0:T(1024)S(1)}, f32[8192]{0:T(1024)S(1)}, u32[]{:S(2)}, u32[]{:S(2)}) collective-permute-start(f32[8192]{0:T(1024)S(1)} %add.284), channel_id=1, source_target_pairs={{0,32},{16,48},{32,0},{48,16},{1,33},{17,49},{33,1},{49,17},{2,34}... | collective-permute-start | bytes 98312 | tf_op jit(solution)/shard_map/ppermute | solution.py:47
  177.0 2.6 %collective-permute-done.5 = f32[8192]{0:T(1024)S(1)} collective-permute-done((f32[8192]{0:T(1024)S(1)}, f32[8192]{0:T(1024)S(1)}, u32[]{:S(2)}, u32[]{:S(2)}) %collective-permute-start.5) | collective-permute-done | bytes 32800 | tf_op jit(solution)/shard_map/ppermute | solution.py:47
  179.6 1.1 collective-permute-done.6
  180.8 0.6 gather_fusion.4
  181.6 1.3 collective-permute-start.7
  183.0 1.6 collective-permute-start.10
  184.5 1.1 collective-permute-done.7
  185.6 1.3 collective-permute-start.8
  187.0 3.1 %collective-permute-start.11 = (f32[512]{0:T(512)S(1)}, f32[512]{0:T(512)S(1)}, u32[]{:S(2)}, u32[]{:S(2)}) collective-permute-start(f32[512]{0:T(512)S(1)} %add.295), channel_id=1, source_target_pairs={{0,1},{1,0},{2,3},{3,2},{4,5},{5,4},{6,7},{7,6},{8,9},{9,8},{10,11... | collective-permute-start | bytes 6152 | tf_op jit(solution)/shard_map/ppermute | solution.py:56
  190.4 2.8 %collective-permute-start.9 = (f32[8192]{0:T(1024)S(1)}, f32[8192]{0:T(1024)S(1)}, u32[]{:S(2)}, u32[]{:S(2)}) collective-permute-start(f32[8192]{0:T(1024)S(1)} %add.292), channel_id=1, source_target_pairs={{0,8},{2,10},{4,12},{6,14},{8,0},{10,2},{12,4},{14,6},{1,9},{3,11}... | collective-permute-start | bytes 98312 | tf_op jit(solution)/shard_map/ppermute | solution.py:56
  193.2 5.0 %collective-permute-done.9 = f32[8192]{0:T(1024)S(1)} collective-permute-done((f32[8192]{0:T(1024)S(1)}, f32[8192]{0:T(1024)S(1)}, u32[]{:S(2)}, u32[]{:S(2)}) %collective-permute-start.9) | collective-permute-done | bytes 32800 | tf_op jit(solution)/shard_map/ppermute | solution.py:56
  198.3 13.9 %fusion.2 = f32[512,512]{0,1:T(8,128)S(1)} fusion(bf16[8192,512]{1,0:T(8,128)(2,1)} %all-gather.2.cloned.1.call-done, f32[8192,512]{1,0:T(8,128)} %get-tuple-element.23, s32[512]{0:T(512)S(1)} %iota_subtract_fusion.1, f32[512]{0:T(512)S(1)} %add_divide_fusion.1, f32[8192]{0:T(1024)S(1)} %add_divide_fusion, s32[8192]{0:T(1024)S(1)} %iota_subtract_fusion, ...), kind=kOutput, calls=%fused_computation.12 | convolution fusion | flops 4332716032 | bytes 26300416 | tf_op jit(solution)/shard_map/dot_general | solution.py:37
  212.4 3.1 %collective-permute-start.12 = (f32[128,512]{0,1:T(8,128)S(1)}, f32[128,512]{0,1:T(8,128)S(1)}, u32[]{:S(2)}, u32[]{:S(2)}) collective-permute-start(f32[128,512]{0,1:T(8,128)S(1)} %get-tuple-element.13), channel_id=1, source_target_pairs={{0,1},{1,128},{128,129},{129,0},{2,3},{3,130},{130,131},{131,2},{4... | collective-permute-start | bytes 786440 | tf_op jit(solution)/shard_map/ppermute | solution.py:131
  216.5 5.3 %collective-permute-done.12 = f32[128,512]{0,1:T(8,128)S(1)} collective-permute-done((f32[128,512]{0,1:T(8,128)S(1)}, f32[128,512]{0,1:T(8,128)S(1)}, u32[]{:S(2)}, u32[]{:S(2)}) %collective-permute-start.12) | collective-permute-done | bytes 262176 | tf_op jit(solution)/shard_map/ppermute | solution.py:131
  221.9 1.5 collective-permute-done.13
  223.3 1.3 collective-permute-done.14
  224.8 0.8 copy.37
  (68 shorter events, 5.5 us)
Async XLA Ops:
  39.5 6.9 %all-to-all-start.1 = ((s32[4,1,64]{2,1,0:T(1,128)}), s32[4,1,64]{2,1,0:T(1,128)S(1)}, u32[]{:S(2)}, u32[]{:S(2)}) async-start(s32[4,1,64]{2,1,0:T(1,128)} %all_to_all.16), calls=%async_computation.1 | async-start | bytes 4096 | tf_op jit(solution)/shard_map/all_to_all | solution.py:99
  51.3 9.4 %all-to-all-start.2 = ((bf16[4,64,512]{2,1,0:T(8,128)(2,1)}), bf16[4,64,512]{2,1,0:T(8,128)(2,1)S(1)}, u32[]{:S(2)}, u32[]{:S(2)}) async-start(bf16[4,64,512]{2,1,0:T(8,128)(2,1)} %broadcast_select_fusion), calls=%async_computation.2 | async-start | bytes 524288 | tf_op jit(solution)/shard_map/all_to_all | solution.py:101
  62.8 18.5 %all-to-all-start.3 = ((bf16[64,4,512]{2,1,0:T(4,128)(2,1)}), bf16[64,4,512]{2,1,0:T(4,128)(2,1)S(1)}, u32[]{:S(2)}, u32[]{:S(2)}) async-start(bf16[64,4,512]{2,1,0:T(4,128)(2,1)} %broadcast_select_fusion.1), calls=%async_computation.3 | async-start | bytes 524288 | tf_op jit(solution)/shard_map/all_to_all | solution.py:105
  68.3 91.7 %all-gather.2.cloned.1.call-start = ((), (), s32[]{:S(2)}) async-start(), calls=%async_computation.4 | async-start | bytes 8519680 | tf_op jit(solution)/shard_map/all_gather | solution.py:146
  84.4 7.0 %collective-permute-start = (bf16[128,512]{0,1:T(8,128)(2,1)S(1)}, bf16[128,512]{0,1:T(8,128)(2,1)S(1)}, u32[]{:S(2)}, u32[]{:S(2)}) collective-permute-start(bf16[128,512]{0,1:T(8,128)(2,1)S(1)} %fusion.4), channel_id=1, source_target_pairs={{0,1},{1,128},{128,129},{129,0},{2,3},{3,130},{130,131},{131,2},{4... | collective-permute-start | bytes 393224 | tf_op jit(solution)/shard_map/ppermute | solution.py:118
  85.4 6.0 %collective-permute-start.1 = (bf16[128,512]{0,1:T(8,128)(2,1)S(1)}, bf16[128,512]{0,1:T(8,128)(2,1)S(1)}, u32[]{:S(2)}, u32[]{:S(2)}) collective-permute-start(bf16[128,512]{0,1:T(8,128)(2,1)S(1)} %fusion.4), channel_id=1, source_target_pairs={{0,128},{1,129},{128,0},{129,1},{2,130},{3,131},{130,2},{131,3},{4... | collective-permute-start | bytes 393224 | tf_op jit(solution)/shard_map/ppermute | solution.py:118
  86.2 7.3 %collective-permute-start.2 = (bf16[128,512]{0,1:T(8,128)(2,1)S(1)}, bf16[128,512]{0,1:T(8,128)(2,1)S(1)}, u32[]{:S(2)}, u32[]{:S(2)}) collective-permute-start(bf16[128,512]{0,1:T(8,128)(2,1)S(1)} %fusion.4), channel_id=1, source_target_pairs={{0,129},{1,0},{128,1},{129,128},{2,131},{3,2},{130,3},{131,130},{4... | collective-permute-start | bytes 393224 | tf_op jit(solution)/shard_map/ppermute | solution.py:118
  171.7 1.2 collective-permute-start.3
  172.9 4.1 %collective-permute-start.4 = (f32[8192]{0:T(1024)S(1)}, f32[8192]{0:T(1024)S(1)}, u32[]{:S(2)}, u32[]{:S(2)}) collective-permute-start(f32[8192]{0:T(1024)S(1)} %add.284), channel_id=1, source_target_pairs={{0,16},{16,32},{32,48},{48,0},{1,17},{17,33},{33,49},{49,1},{2,18}... | collective-permute-start | bytes 98312 | tf_op jit(solution)/shard_map/ppermute | solution.py:47
  174.1 5.5 %collective-permute-start.5 = (f32[8192]{0:T(1024)S(1)}, f32[8192]{0:T(1024)S(1)}, u32[]{:S(2)}, u32[]{:S(2)}) collective-permute-start(f32[8192]{0:T(1024)S(1)} %add.284), channel_id=1, source_target_pairs={{0,32},{16,48},{32,0},{48,16},{1,33},{17,49},{33,1},{49,17},{2,34}... | collective-permute-start | bytes 98312 | tf_op jit(solution)/shard_map/ppermute | solution.py:47
  176.8 3.9 %collective-permute-start.6 = (f32[8192]{0:T(1024)S(1)}, f32[8192]{0:T(1024)S(1)}, u32[]{:S(2)}, u32[]{:S(2)}) collective-permute-start(f32[8192]{0:T(1024)S(1)} %add.284), channel_id=1, source_target_pairs={{0,48},{16,0},{32,16},{48,32},{1,49},{17,1},{33,17},{49,33},{2,50}... | collective-permute-start | bytes 98312 | tf_op jit(solution)/shard_map/ppermute | solution.py:47
  181.6 4.0 %collective-permute-start.7 = (f32[8192]{0:T(1024)S(1)}, f32[8192]{0:T(1024)S(1)}, u32[]{:S(2)}, u32[]{:S(2)}) collective-permute-start(f32[8192]{0:T(1024)S(1)} %bitcast.66), channel_id=1, source_target_pairs={{0,2},{2,0},{4,6},{6,4},{8,10},{10,8},{12,14},{14,12},{1,3},{3,1},... | collective-permute-start | bytes 98312 | tf_op jit(solution)/shard_map/ppermute | solution.py:56
  183.0 4.0 %collective-permute-start.10 = (f32[512]{0:T(512)S(1)}, f32[512]{0:T(512)S(1)}, u32[]{:S(2)}, u32[]{:S(2)}) collective-permute-start(f32[512]{0:T(512)S(1)} %get-tuple-element.6), channel_id=1, source_target_pairs={{0,128},{128,0},{1,129},{129,1},{2,130},{130,2},{3,131},{131,3},{4... | collective-permute-start | bytes 6152 | tf_op jit(solution)/shard_map/ppermute | solution.py:56
  185.6 4.8 %collective-permute-start.8 = (f32[8192]{0:T(1024)S(1)}, f32[8192]{0:T(1024)S(1)}, u32[]{:S(2)}, u32[]{:S(2)}) collective-permute-start(f32[8192]{0:T(1024)S(1)} %add.291), channel_id=1, source_target_pairs={{0,4},{2,6},{4,0},{6,2},{8,12},{10,14},{12,8},{14,10},{1,5},{3,7},... | collective-permute-start | bytes 98312 | tf_op jit(solution)/shard_map/ppermute | solution.py:56
  187.0 6.3 %collective-permute-start.11 = (f32[512]{0:T(512)S(1)}, f32[512]{0:T(512)S(1)}, u32[]{:S(2)}, u32[]{:S(2)}) collective-permute-start(f32[512]{0:T(512)S(1)} %add.295), channel_id=1, source_target_pairs={{0,1},{1,0},{2,3},{3,2},{4,5},{5,4},{6,7},{7,6},{8,9},{9,8},{10,11... | collective-permute-start | bytes 6152 | tf_op jit(solution)/shard_map/ppermute | solution.py:56
  190.4 7.8 %collective-permute-start.9 = (f32[8192]{0:T(1024)S(1)}, f32[8192]{0:T(1024)S(1)}, u32[]{:S(2)}, u32[]{:S(2)}) collective-permute-start(f32[8192]{0:T(1024)S(1)} %add.292), channel_id=1, source_target_pairs={{0,8},{2,10},{4,12},{6,14},{8,0},{10,2},{12,4},{14,6},{1,9},{3,11}... | collective-permute-start | bytes 98312 | tf_op jit(solution)/shard_map/ppermute | solution.py:56
  212.4 9.5 %collective-permute-start.12 = (f32[128,512]{0,1:T(8,128)S(1)}, f32[128,512]{0,1:T(8,128)S(1)}, u32[]{:S(2)}, u32[]{:S(2)}) collective-permute-start(f32[128,512]{0,1:T(8,128)S(1)} %get-tuple-element.13), channel_id=1, source_target_pairs={{0,1},{1,128},{128,129},{129,0},{2,3},{3,130},{130,131},{131,2},{4... | collective-permute-start | bytes 786440 | tf_op jit(solution)/shard_map/ppermute | solution.py:131
  215.4 7.9 %collective-permute-start.13 = (f32[128,512]{0,1:T(8,128)S(1)}, f32[128,512]{0,1:T(8,128)S(1)}, u32[]{:S(2)}, u32[]{:S(2)}) collective-permute-start(f32[128,512]{0,1:T(8,128)S(1)} %get-tuple-element.15), channel_id=1, source_target_pairs={{0,128},{1,129},{128,0},{129,1},{2,130},{3,131},{130,2},{131,3},{4... | collective-permute-start | bytes 786440 | tf_op jit(solution)/shard_map/ppermute | solution.py:131
  216.0 8.7 %collective-permute-start.14 = (f32[128,512]{0,1:T(8,128)S(1)}, f32[128,512]{0,1:T(8,128)S(1)}, u32[]{:S(2)}, u32[]{:S(2)}) collective-permute-start(f32[128,512]{0,1:T(8,128)S(1)} %get-tuple-element.14), channel_id=1, source_target_pairs={{0,129},{1,0},{128,1},{129,128},{2,131},{3,2},{130,3},{131,130},{4... | collective-permute-start | bytes 786440 | tf_op jit(solution)/shard_map/ppermute | solution.py:131
Sparse Core Ops, SparseCore 0:
  83.3 76.5 all-gather.1
